TPU v7x, 1024 devices: a whole 8x8x8 slice. The times are simulated.
1024 devices in a mesh: morton: 16 (over z, core), slab: 64 (over x, y).
Axes of the slice: x: 8, y: 8, z: 8, core: 2. Of those that a mesh axis runs over, the one named last changes fastest.
Arguments:
- velocity: float32 [1024, 256, 256], P('slab', 'morton'), may hold values from -6 to 6
Outputs:
- approx: float32 [256, 64, 64], P('slab', 'morton')
- detail_two: float32 [7, 256, 64, 64], P(None, 'slab', 'morton')
- detail_one: float32 [7, 512, 128, 128], P(None, 'slab', 'morton')
All inputs are finite; a program needn't handle non-finite values.
Results may differ from a plain program's by a relative error of at most 0.00002.
Values sent between devices are 32-bit elements; how exact they have to be, the bound alone decides.
No kernel may reach another device: no remote copies, remote signals or barrier semaphores. Data moves between devices by JAX's collectives and lax.ppermute only.
A program may use at most 32 MiB of HBM per device.

v0:
```python
import jax
import jax.numpy as jnp
from jax import lax
from jax.sharding import PartitionSpec as P

LIFT_ALPHA = -1.586134342059924
LIFT_BETA = -0.052980118572961
LIFT_GAMMA = 0.882911075530934
LIFT_DELTA = 0.443506852043971
LIFT_SCALE = 1.149604398860241


def extended_2(x, sides, width):
    for axis, dim in sides:
        devices, length = (lax.axis_size(axis), x.shape[dim])
        up = [(i, (i + 1) % devices) for i in range(devices - 1)]
        down = [(j, i) for i, j in up]
        last = lax.slice_in_dim(x, length - width, length, axis=dim)
        initial = lax.slice_in_dim(x, 0, width, axis=dim)
        before = lax.ppermute(last, axis, up)
        after = lax.ppermute(initial, axis, down)
        x = jnp.concatenate([before, x, after], axis=dim)
    return x


def cut_range(values, start, stop, dimension):
    return lax.slice_in_dim(values, start, stop, axis=dimension)


def lifting(extended, dimension):
    halfway = extended.shape[dimension] // 2
    new_shape = extended.shape[:dimension] + (halfway, 2) + extended.shape[dimension + 1 :]
    paired = extended.reshape(new_shape)
    even_part = lax.index_in_dim(paired, 0, dimension + 1, keepdims=False)
    odd_part = lax.index_in_dim(paired, 1, dimension + 1, keepdims=False)
    first_detail = cut_range(odd_part, 0, halfway - 1, dimension) + LIFT_ALPHA * (
        cut_range(even_part, 0, halfway - 1, dimension)
        + cut_range(even_part, 1, halfway, dimension)
    )
    first_smooth = cut_range(even_part, 1, halfway - 1, dimension) + LIFT_BETA * (
        cut_range(first_detail, 0, halfway - 2, dimension)
        + cut_range(first_detail, 1, halfway - 1, dimension)
    )
    second_detail = cut_range(first_detail, 1, halfway - 2, dimension) + LIFT_GAMMA * (
        cut_range(first_smooth, 0, halfway - 3, dimension)
        + cut_range(first_smooth, 1, halfway - 2, dimension)
    )
    second_smooth = cut_range(first_smooth, 1, halfway - 3, dimension) + LIFT_DELTA * (
        cut_range(second_detail, 0, halfway - 4, dimension)
        + cut_range(second_detail, 1, halfway - 3, dimension)
    )
    lowpass = second_smooth * LIFT_SCALE
    highpass = cut_range(second_detail, 1, halfway - 3, dimension) / LIFT_SCALE
    return (lowpass, highpass)


def reflect_edges(extended, dimension, margin, at_low, at_high):
    length = extended.shape[dimension]
    low_mirror = jnp.flip(cut_range(extended, margin + 1, 2 * margin + 1, dimension), dimension)
    high_mirror = jnp.flip(
        cut_range(extended, length - 2 * margin - 1, length - margin - 1, dimension), dimension
    )
    leading = jnp.where(at_low, low_mirror, cut_range(extended, 0, margin, dimension))
    trailing = jnp.where(
        at_high, high_mirror, cut_range(extended, length - margin, length, dimension)
    )
    middle = cut_range(extended, margin, length - margin, dimension)
    return jnp.concatenate([leading, middle, trailing], axis=dimension)


def split_depth(planar):
    subbands = []
    for x_band in planar:
        padded = jnp.pad(x_band, ((0, 0), (0, 0), (4, 4)), mode="reflect")
        lowpass, highpass = lifting(padded, 2)
        subbands = subbands + [lowpass, highpass]
    return subbands


def split_plane(extended):
    planar = []
    for x_band in lifting(extended, 0):
        lowpass, highpass = lifting(x_band, 1)
        planar = planar + [lowpass, highpass]
    return planar


def per_device(velocity):
    slab_low = lax.axis_index("slab") == 0
    slab_high = lax.axis_index("slab") == lax.axis_size("slab") - 1
    morton_low = lax.axis_index("morton") == 0
    morton_high = lax.axis_index("morton") == lax.axis_size("morton") - 1
    margin = 4
    extended = extended_2(velocity, (("slab", 0),), margin)
    extended = reflect_edges(extended, 0, margin, slab_low, slab_high)
    lowpass, highpass = lifting(extended, 0)
    stacked = jnp.stack([lowpass, highpass])
    widened = extended_2(stacked, (("morton", 2),), margin)
    widened = reflect_edges(widened, 2, margin, morton_low, morton_high)
    low_rows, high_rows = lifting(widened, 2)
    planar = [low_rows[0], high_rows[0], low_rows[1], high_rows[1]]
    level_one = split_depth(planar)
    detail_one = jnp.stack([subband for subband in level_one[1:]])
    coarse = extended_2(level_one[0], (("morton", 1), ("slab", 0)), 4)
    coarse = reflect_edges(coarse, 0, 4, slab_low, slab_high)
    coarse = reflect_edges(coarse, 1, 4, morton_low, morton_high)
    level_two = split_depth(split_plane(coarse))
    return (level_two[0], jnp.stack(level_two[1:]), detail_one)


def solution(mesh):
    placed = (P("slab", "morton", None),)
    return jax.shard_map(
        per_device,
        mesh=mesh,
        in_specs=placed,
        out_specs=(
            P("slab", "morton", None),
            P(None, "slab", "morton", None),
            P(None, "slab", "morton", None),
        ),
        check_vma=False,
    )
```

profile of v0, /device:TPU:265, one launch (start us, length us, event | category | flops | bytes accessed | tf_op | source)
XLA Modules:
  0.0 69.9 jit_solution(8589205155266584237)
XLA Ops:
  0.6 1.0 %fusion.132 = (f32[4,16,256]{2,1,0:T(8,128)S(1)}, f32[4,16,256]{2,1,0:T(8,128)S(1)}, f32[4,16,256]{2,1,0:T(8,128)S(1)}, f32[4,16,256]{2,1,0:T(8,128)S(1)}) fusion(f32[16,16,256]{2,1,0:T(8,128)} %param.1), kind=kLoop, calls=%fused_computation.249 | loop fusion | bytes 524288 | tf_op jit(solution)/shard_map/slice | solution.py:27
  1.6 3.3 %collective-permute-start = (f32[4,16,256]{2,1,0:T(8,128)S(1)}, f32[4,16,256]{2,1,0:T(8,128)S(1)}, u32[]{:S(2)}, u32[]{:S(2)}) collective-permute-start(f32[4,16,256]{2,1,0:T(8,128)S(1)} %get-tuple-element.46), channel_id=1, source_target_pairs={{0,1},{1,2},{2,3},{3,4},{4,5},{5,6},{6,7},{7,8},{8,9},{9,10},{10,1... | collective-permute-start | bytes 196616 | tf_op jit(solution)/shard_map/ppermute | solution.py:20
  5.0 5.3 %collective-permute-start.1 = (f32[4,16,256]{2,1,0:T(8,128)S(1)}, f32[4,16,256]{2,1,0:T(8,128)S(1)}, u32[]{:S(2)}, u32[]{:S(2)}) collective-permute-start(f32[4,16,256]{2,1,0:T(8,128)S(1)} %get-tuple-element.47), channel_id=1, source_target_pairs={{1,0},{2,1},{3,2},{4,3},{5,4},{6,5},{7,6},{8,7},{9,8},{10,9},{11,1... | collective-permute-start | bytes 196616 | tf_op jit(solution)/shard_map/ppermute | solution.py:21
  10.3 1.3 %collective-permute-done.1 = f32[4,16,256]{2,1,0:T(8,128)S(1)} collective-permute-done((f32[4,16,256]{2,1,0:T(8,128)S(1)}, f32[4,16,256]{2,1,0:T(8,128)S(1)}, u32[]{:S(2)}, u32[]{:S(2)}) %collective-permute-start.1) | collective-permute-done | bytes 65568 | tf_op jit(solution)/shard_map/ppermute | solution.py:21
  11.9 6.6 %collective-permute-start.2 = (f32[2,8,4,256]{3,2,1,0:T(4,128)S(1)}, f32[2,8,4,256]{3,2,1,0:T(4,128)S(1)}, u32[]{:S(2)}, u32[]{:S(2)}) collective-permute-start(f32[2,8,4,256]{3,2,1,0:T(4,128)S(1)} %get-tuple-element.40), channel_id=1, source_target_pairs={{0,64},{64,128},{128,192},{192,256},{256,320},{320,384},{384,448},... | collective-permute-start | bytes 196616 | tf_op jit(solution)/shard_map/ppermute | solution.py:20
  18.5 0.2 rev.84
  18.6 0.2 rev.85
  18.8 1.9 %collective-permute-start.3 = (f32[2,8,4,256]{3,2,1,0:T(4,128)S(1)}, f32[2,8,4,256]{3,2,1,0:T(4,128)S(1)}, u32[]{:S(2)}, u32[]{:S(2)}) collective-permute-start(f32[2,8,4,256]{3,2,1,0:T(4,128)S(1)} %get-tuple-element.42), channel_id=1, source_target_pairs={{64,0},{128,64},{192,128},{256,192},{320,256},{384,320},{448,384},... | collective-permute-start | bytes 196616 | tf_op jit(solution)/shard_map/ppermute | solution.py:21
  20.8 3.6 %collective-permute-done.3 = f32[2,8,4,256]{3,2,1,0:T(4,128)S(1)} collective-permute-done((f32[2,8,4,256]{3,2,1,0:T(4,128)S(1)}, f32[2,8,4,256]{3,2,1,0:T(4,128)S(1)}, u32[]{:S(2)}, u32[]{:S(2)}) %collective-permute-start.3) | collective-permute-done | bytes 65568 | tf_op jit(solution)/shard_map/ppermute | solution.py:21
  24.5 0.1 copy.141
  25.9 0.4 copy.165
  26.8 0.2 copy.175
  26.9 0.2 copy.174
  27.3 0.4 copy.142
  28.1 0.2 copy.171
  28.3 0.6 constant_dynamic-update-slice_fusion.13
  29.0 1.0 %fusion.127 = (f32[8,4,128]{1,0,2:T(8,128)}, f32[8,4,128]{1,0,2:T(8,128)S(1)}) fusion(f32[8,8,128]{1,0,2:T(8,128)S(1)} %get-tuple-element.27), kind=kLoop, calls=%fused_computation.244 | loop fusion | bytes 65536 | tf_op jit(solution)/shard_map/slice | solution.py:18
  29.9 3.6 %collective-permute-start.4 = (f32[8,4,128]{1,0,2:T(8,128)}, f32[8,4,128]{1,0,2:T(8,128)S(1)}, u32[]{:S(2)}, u32[]{:S(2)}) collective-permute-start(f32[8,4,128]{1,0,2:T(8,128)} %get-tuple-element.28), channel_id=1, source_target_pairs={{0,64},{64,128},{128,192},{192,256},{256,320},{320,384},{384,448},... | collective-permute-start | bytes 49160 | tf_op jit(solution)/shard_map/ppermute | solution.py:20
  33.5 1.9 %collective-permute-start.5 = (f32[8,4,128]{1,0,2:T(8,128)S(1)}, f32[8,4,128]{1,0,2:T(8,128)S(1)}, u32[]{:S(2)}, u32[]{:S(2)}) collective-permute-start(f32[8,4,128]{1,0,2:T(8,128)S(1)} %get-tuple-element.29), channel_id=1, source_target_pairs={{64,0},{128,64},{192,128},{256,192},{320,256},{384,320},{448,384},... | collective-permute-start | bytes 49160 | tf_op jit(solution)/shard_map/ppermute | solution.py:21
  35.6 0.4 copy.162
  36.4 0.2 copy.173
  36.6 0.2 copy.172
  36.9 0.4 copy.168
  37.8 0.2 copy.176
  38.0 0.6 constant_dynamic-update-slice_fusion.12
  38.6 0.6 constant_dynamic-update-slice_fusion.11
  39.2 0.6 constant_dynamic-update-slice_fusion.10
  39.9 0.6 constant_dynamic-update-slice_fusion.9
  40.5 0.6 constant_dynamic-update-slice_fusion.8
  41.1 0.2 copy.145
  41.3 0.2 copy.177
  41.5 0.2 copy.144
  41.7 4.9 %collective-permute-done.5 = f32[8,4,128]{1,0,2:T(8,128)S(1)} collective-permute-done((f32[8,4,128]{1,0,2:T(8,128)S(1)}, f32[8,4,128]{1,0,2:T(8,128)S(1)}, u32[]{:S(2)}, u32[]{:S(2)}) %collective-permute-start.5) | collective-permute-done | bytes 16416 | tf_op jit(solution)/shard_map/ppermute | solution.py:21
  46.7 0.2 copy.146
  46.9 7.1 %collective-permute-start.7 = (f32[4,16,128]{2,1,0:T(8,128)S(1)}, f32[4,16,128]{2,1,0:T(8,128)S(1)}, u32[]{:S(2)}, u32[]{:S(2)}) collective-permute-start(f32[4,16,128]{2,1,0:T(8,128)S(1)} %get-tuple-element.65), channel_id=1, source_target_pairs={{1,0},{2,1},{3,2},{4,3},{5,4},{6,5},{7,6},{8,7},{9,8},{10,9},{11,1... | collective-permute-start | bytes 98312 | tf_op jit(solution)/shard_map/ppermute | solution.py:21
  54.0 0.6 constant_dynamic-update-slice_fusion.7
  54.6 1.9 %collective-permute-start.6 = (f32[4,16,128]{2,1,0:T(8,128)S(1)}, f32[4,16,128]{2,1,0:T(8,128)S(1)}, u32[]{:S(2)}, u32[]{:S(2)}) collective-permute-start(f32[4,16,128]{2,1,0:T(8,128)S(1)} %get-tuple-element.67), channel_id=1, source_target_pairs={{0,1},{1,2},{2,3},{3,4},{4,5},{5,6},{6,7},{7,8},{8,9},{9,10},{10,1... | collective-permute-start | bytes 98312 | tf_op jit(solution)/shard_map/ppermute | solution.py:20
  56.6 6.0 %collective-permute-done.6 = f32[4,16,128]{2,1,0:T(8,128)S(1)} collective-permute-done((f32[4,16,128]{2,1,0:T(8,128)S(1)}, f32[4,16,128]{2,1,0:T(8,128)S(1)}, u32[]{:S(2)}, u32[]{:S(2)}) %collective-permute-start.6) | collective-permute-done | bytes 32800 | tf_op jit(solution)/shard_map/ppermute | solution.py:20
  63.4 0.2 copy.148
  63.6 0.2 fusion.131
  64.2 0.7 fusion.117
  66.0 0.2 copy.151
  66.2 0.2 fusion.130
  67.1 0.2 copy.156
  67.3 0.2 fusion.129
  68.3 0.2 copy.159
  68.4 0.2 fusion.128
  69.3 0.6 copy-done.1
  (129 shorter events, 7.8 us)
Async XLA Ops:
  0.6 11.0 %copy-start = (f32[16,16,256]{2,1,0:T(8,128)S(1)}, f32[16,16,256]{2,1,0:T(8,128)}, u32[]{:S(2)}) copy-start(f32[16,16,256]{2,1,0:T(8,128)} %param.1) | copy-start | bytes 786436
  1.6 8.6 %collective-permute-start = (f32[4,16,256]{2,1,0:T(8,128)S(1)}, f32[4,16,256]{2,1,0:T(8,128)S(1)}, u32[]{:S(2)}, u32[]{:S(2)}) collective-permute-start(f32[4,16,256]{2,1,0:T(8,128)S(1)} %get-tuple-element.46), channel_id=1, source_target_pairs={{0,1},{1,2},{2,3},{3,4},{4,5},{5,6},{6,7},{7,8},{8,9},{9,10},{10,1... | collective-permute-start | bytes 196616 | tf_op jit(solution)/shard_map/ppermute | solution.py:20
  5.0 6.6 %collective-permute-start.1 = (f32[4,16,256]{2,1,0:T(8,128)S(1)}, f32[4,16,256]{2,1,0:T(8,128)S(1)}, u32[]{:S(2)}, u32[]{:S(2)}) collective-permute-start(f32[4,16,256]{2,1,0:T(8,128)S(1)} %get-tuple-element.47), channel_id=1, source_target_pairs={{1,0},{2,1},{3,2},{4,3},{5,4},{6,5},{7,6},{8,7},{9,8},{10,9},{11,1... | collective-permute-start | bytes 196616 | tf_op jit(solution)/shard_map/ppermute | solution.py:21
  11.9 8.9 %collective-permute-start.2 = (f32[2,8,4,256]{3,2,1,0:T(4,128)S(1)}, f32[2,8,4,256]{3,2,1,0:T(4,128)S(1)}, u32[]{:S(2)}, u32[]{:S(2)}) collective-permute-start(f32[2,8,4,256]{3,2,1,0:T(4,128)S(1)} %get-tuple-element.40), channel_id=1, source_target_pairs={{0,64},{64,128},{128,192},{192,256},{256,320},{320,384},{384,448},... | collective-permute-start | bytes 196616 | tf_op jit(solution)/shard_map/ppermute | solution.py:20
  18.8 5.6 %collective-permute-start.3 = (f32[2,8,4,256]{3,2,1,0:T(4,128)S(1)}, f32[2,8,4,256]{3,2,1,0:T(4,128)S(1)}, u32[]{:S(2)}, u32[]{:S(2)}) collective-permute-start(f32[2,8,4,256]{3,2,1,0:T(4,128)S(1)} %get-tuple-element.42), channel_id=1, source_target_pairs={{64,0},{128,64},{192,128},{256,192},{320,256},{384,320},{448,384},... | collective-permute-start | bytes 196616 | tf_op jit(solution)/shard_map/ppermute | solution.py:21
  29.9 11.5 %collective-permute-start.4 = (f32[8,4,128]{1,0,2:T(8,128)}, f32[8,4,128]{1,0,2:T(8,128)S(1)}, u32[]{:S(2)}, u32[]{:S(2)}) collective-permute-start(f32[8,4,128]{1,0,2:T(8,128)} %get-tuple-element.28), channel_id=1, source_target_pairs={{0,64},{64,128},{128,192},{192,256},{256,320},{320,384},{384,448},... | collective-permute-start | bytes 49160 | tf_op jit(solution)/shard_map/ppermute | solution.py:20
  33.5 13.1 %collective-permute-start.5 = (f32[8,4,128]{1,0,2:T(8,128)S(1)}, f32[8,4,128]{1,0,2:T(8,128)S(1)}, u32[]{:S(2)}, u32[]{:S(2)}) collective-permute-start(f32[8,4,128]{1,0,2:T(8,128)S(1)} %get-tuple-element.29), channel_id=1, source_target_pairs={{64,0},{128,64},{192,128},{256,192},{320,256},{384,320},{448,384},... | collective-permute-start | bytes 49160 | tf_op jit(solution)/shard_map/ppermute | solution.py:21
  46.9 9.6 %collective-permute-start.7 = (f32[4,16,128]{2,1,0:T(8,128)S(1)}, f32[4,16,128]{2,1,0:T(8,128)S(1)}, u32[]{:S(2)}, u32[]{:S(2)}) collective-permute-start(f32[4,16,128]{2,1,0:T(8,128)S(1)} %get-tuple-element.65), channel_id=1, source_target_pairs={{1,0},{2,1},{3,2},{4,3},{5,4},{6,5},{7,6},{8,7},{9,8},{10,9},{11,1... | collective-permute-start | bytes 98312 | tf_op jit(solution)/shard_map/ppermute | solution.py:21
  54.6 8.0 %collective-permute-start.6 = (f32[4,16,128]{2,1,0:T(8,128)S(1)}, f32[4,16,128]{2,1,0:T(8,128)S(1)}, u32[]{:S(2)}, u32[]{:S(2)}) collective-permute-start(f32[4,16,128]{2,1,0:T(8,128)S(1)} %get-tuple-element.67), channel_id=1, source_target_pairs={{0,1},{1,2},{2,3},{3,4},{4,5},{5,6},{6,7},{7,8},{8,9},{9,10},{10,1... | collective-permute-start | bytes 98312 | tf_op jit(solution)/shard_map/ppermute | solution.py:20
  69.3 0.6 copy-start.1
where the time goes:
time: 70.2 us; the launch traced here: 69.9 us
  starting transfers between devices  31.6 us (45%)
  local copies, waits for them, and re-layouts  16 us (23%)
  waiting for transfers between devices  15.9 us (23%)
  other arithmetic  5.05 us (7%)
  between operations  1.35 us (2%)
    ppermute x4, starting transfers between devices, extended_2(): after = lax.ppermute(initial, axis, down)  16.2 us
    ppermute x4, starting transfers between devices, extended_2(): before = lax.ppermute(last, axis, up)  15.4 us
    ppermute x4, waiting for transfers between devices, extended_2(): after = lax.ppermute(initial, axis, down)  9.83 us
    ppermute x4, waiting for transfers between devices, extended_2(): before = lax.ppermute(last, axis, up)  6.03 us
    unnamed x16, local copies, waits for them, and re-layouts  5.02 us
    concatenate x8, local copies, waits for them, and re-layouts, split_depth(): padded = jnp.pad(x_band, ((0, 0), (0, 0), (4, 4)), mode='reflect')  2.39 us
    another operation x8, local copies, waits for them, and re-layouts, per_device(): detail_one = jnp.stack([subband for subband in level_one[1:]])  1.97 us
  transfers between devices with their start and end apart: 8, of which 4 were waited for; matrix products, arithmetic and copies ran while one was open for 10% of the time, Pallas kernels for 0%

commit v1 on v0

v1 whole, which is shorter than its diff:
```python
import jax
import jax.numpy as jnp
from jax import lax
from jax.sharding import PartitionSpec as P

LIFT_ALPHA = -1.586134342059924
LIFT_BETA = -0.052980118572961
LIFT_GAMMA = 0.882911075530934
LIFT_DELTA = 0.443506852043971
LIFT_SCALE = 1.149604398860241

WIDE = 12
NARROW = 4


def cut_range(values, start, stop, dimension):
    return lax.slice_in_dim(values, start, stop, axis=dimension)


def lifting(extended, dimension):
    halfway = extended.shape[dimension] // 2
    new_shape = extended.shape[:dimension] + (halfway, 2) + extended.shape[dimension + 1 :]
    paired = extended.reshape(new_shape)
    even_part = lax.index_in_dim(paired, 0, dimension + 1, keepdims=False)
    odd_part = lax.index_in_dim(paired, 1, dimension + 1, keepdims=False)
    first_detail = cut_range(odd_part, 0, halfway - 1, dimension) + LIFT_ALPHA * (
        cut_range(even_part, 0, halfway - 1, dimension)
        + cut_range(even_part, 1, halfway, dimension)
    )
    first_smooth = cut_range(even_part, 1, halfway - 1, dimension) + LIFT_BETA * (
        cut_range(first_detail, 0, halfway - 2, dimension)
        + cut_range(first_detail, 1, halfway - 1, dimension)
    )
    second_detail = cut_range(first_detail, 1, halfway - 2, dimension) + LIFT_GAMMA * (
        cut_range(first_smooth, 0, halfway - 3, dimension)
        + cut_range(first_smooth, 1, halfway - 2, dimension)
    )
    second_smooth = cut_range(first_smooth, 1, halfway - 3, dimension) + LIFT_DELTA * (
        cut_range(second_detail, 0, halfway - 4, dimension)
        + cut_range(second_detail, 1, halfway - 3, dimension)
    )
    lowpass = second_smooth * LIFT_SCALE
    highpass = cut_range(second_detail, 1, halfway - 3, dimension) / LIFT_SCALE
    return (lowpass, highpass)


def part_of(block, offset, width, dimension):
    length = block.shape[dimension]
    if offset < 0:
        return cut_range(block, length - width, length, dimension)
    if offset > 0:
        return cut_range(block, 0, width, dimension)
    return block


def halo_pieces(wide, narrow):
    slabs, bricks = lax.axis_size("slab"), lax.axis_size("morton")
    received = {}
    for ox in (-1, 0, 1):
        for oy in (-1, 0, 1):
            if ox == 0 and oy == 0:
                continue
            pieces = []
            shapes = []
            for block, width in ((wide, WIDE), (narrow, NARROW)):
                piece = part_of(part_of(block, ox, width, 0), oy, width, 1)
                shapes.append(piece.shape)
                pieces.append(piece.reshape(-1, piece.shape[-1]))
            message = jnp.concatenate(pieces, axis=0)
            pairs = []
            for s in range(slabs):
                for m in range(bricks):
                    s_from, m_from = s + ox, m + oy
                    if 0 <= s_from < slabs and 0 <= m_from < bricks:
                        pairs.append((m_from * slabs + s_from, m * slabs + s))
            arrived = lax.ppermute(message, ("morton", "slab"), pairs)
            rows = [shapes[0][0] * shapes[0][1], shapes[1][0] * shapes[1][1]]
            received[(ox, oy)] = (
                arrived[: rows[0]].reshape(shapes[0]),
                arrived[rows[0] :].reshape(shapes[1]),
            )
    return received


def assemble(block, received, which):
    rows = []
    for ox in (-1, 0, 1):
        row = []
        for oy in (-1, 0, 1):
            row.append(block if ox == 0 and oy == 0 else received[(ox, oy)][which])
        rows.append(jnp.concatenate(row, axis=1))
    return jnp.concatenate(rows, axis=0)


def mirror_edges(extended, dimension, width, at_low, at_high, whole):
    length = extended.shape[dimension]
    shift = 1 if whole else 0
    low_mirror = jnp.flip(cut_range(extended, width + shift, 2 * width + shift, dimension), dimension)
    high_mirror = jnp.flip(
        cut_range(extended, length - 2 * width - shift, length - width - shift, dimension), dimension
    )
    leading = jnp.where(at_low, low_mirror, cut_range(extended, 0, width, dimension))
    trailing = jnp.where(at_high, high_mirror, cut_range(extended, length - width, length, dimension))
    middle = cut_range(extended, width, length - width, dimension)
    return jnp.concatenate([leading, middle, trailing], axis=dimension)


def per_device(velocity):
    slab_low = lax.axis_index("slab") == 0
    slab_high = lax.axis_index("slab") == lax.axis_size("slab") - 1
    brick_low = lax.axis_index("morton") == 0
    brick_high = lax.axis_index("morton") == lax.axis_size("morton") - 1

    padded = jnp.pad(velocity, ((0, 0), (0, 0), (4, 4)), mode="reflect")
    z_low, z_high = lifting(padded, 2)
    received = halo_pieces(z_low, z_high)

    wide = assemble(z_low, received, 0)
    wide = mirror_edges(wide, 1, WIDE, brick_low, brick_high, True)
    wide = mirror_edges(wide, 0, WIDE, slab_low, slab_high, True)
    narrow = assemble(z_high, received, 1)
    narrow = mirror_edges(narrow, 1, NARROW, brick_low, brick_high, True)
    narrow = mirror_edges(narrow, 0, NARROW, slab_low, slab_high, True)

    x_low, x_high = lifting(wide, 0)
    n_rows = velocity.shape[0] // 2
    n_cols = velocity.shape[1] // 2
    inner = slice(4, 4 + n_rows)
    window = slice(WIDE - 4, WIDE + 2 * n_cols + 4)
    coarse, band_2 = lifting(x_low, 1)
    band_2 = band_2[inner, 4 : 4 + n_cols]
    band_4, band_6 = lifting(x_high[inner, window], 1)
    xn_low, xn_high = lifting(narrow, 0)
    band_1, band_3 = lifting(xn_low, 1)
    band_5, band_7 = lifting(xn_high, 1)
    detail_one = jnp.stack([band_1, band_2, band_3, band_4, band_5, band_6, band_7])

    coarse = mirror_edges(coarse, 0, 4, slab_low, slab_high, True)
    coarse = mirror_edges(coarse, 1, 4, brick_low, brick_high, True)
    level_two = []
    for x_band in lifting(coarse, 0):
        for y_band in lifting(x_band, 1):
            padded = jnp.pad(y_band, ((0, 0), (0, 0), (4, 4)), mode="reflect")
            level_two.extend(lifting(padded, 2))
    return (level_two[0], jnp.stack(level_two[1:]), detail_one)


def solution(mesh):
    placed = (P("slab", "morton", None),)
    return jax.shard_map(
        per_device,
        mesh=mesh,
        in_specs=placed,
        out_specs=(
            P("slab", "morton", None),
            P(None, "slab", "morton", None),
            P(None, "slab", "morton", None),
        ),
        check_vma=False,
    )
```

time: 70.2 us -> 118 us (1.68)
  the two profiles are of different devices: /device:TPU:265 before, /device:TPU:393 now
where the time goes in v1:
time: 118 us; the launch traced here: 116 us
  local copies, waits for them, and re-layouts  53.3 us (45%)
  starting transfers between devices  36.9 us (31%)
  other arithmetic  16.1 us (14%)
  waiting for transfers between devices  8.53 us (7%)
  between operations  1.71 us (1%)
    ppermute x8, starting transfers between devices, halo_pieces(): arrived = lax.ppermute(message, ('morton', 'slab'), pairs)  36.9 us
    slice x31, local copies, waits for them, and re-layouts, cut_range(): return lax.slice_in_dim(values, start, stop, axis=dimension)  25.7 us
    ppermute x8, waiting for transfers between devices, halo_pieces(): arrived = lax.ppermute(message, ('morton', 'slab'), pairs)  8.53 us
    reshape x8, local copies, waits for them, and re-layouts, halo_pieces(): pieces.append(piece.reshape(-1, piece.shape[-1]))  7.18 us
    concatenate x8, other arithmetic, halo_pieces(): message = jnp.concatenate(pieces, axis=0)  5.94 us
    unnamed x39, local copies, waits for them, and re-layouts  4.49 us
    slice x9, local copies, waits for them, and re-layouts, halo_pieces(): arrived[:rows[0]].reshape(shapes[0])  3.61 us
    slice x8, local copies, waits for them, and re-layouts, halo_pieces(): arrived[rows[0]:].reshape(shapes[1])  2.93 us
  transfers between devices with their start and end apart: 8, of which 2 were waited for; matrix products, arithmetic and copies ran while one was open for 32% of the time, Pallas kernels for 0%

profile of v1, /device:TPU:393, one launch (start us, length us, event | category | flops | bytes accessed | tf_op | source)
XLA Modules:
  0.0 116.5 jit_solution(10807076958310211824)
XLA Ops:
  0.6 1.1 fusion.148
  2.2 1.3 %copy.237 = f32[16,16,264]{1,0,2:T(8,128)S(1)} copy(f32[16,16,264]{2,1,0:T(8,128)S(1)} %pad_maximum_fusion.2) | data formatting | bytes 540672 | tf_op jit(solution)/shard_map/jit(_pad)/concatenate | solution.py:114
  4.4 1.4 %fusion.140 = (f32[16,4,128]{1,0,2:T(8,128)S(1)}, f32[16,4,128]{1,0,2:T(8,128)}) fusion(f32[16,16,128]{1,0,2:T(8,128)S(1)} %get-tuple-element.15), kind=kLoop, calls=%fused_computation.265 | loop fusion | bytes 131072 | tf_op jit(solution)/shard_map/slice | solution.py:17
  5.8 1.6 %copy.248 = f32[16,4,128]{2,1,0:T(4,128)S(1)} copy(f32[16,4,128]{1,0,2:T(8,128)} %get-tuple-element.37) | data formatting | bytes 65536 | tf_op jit(solution)/shard_map/slice | solution.py:17
  7.5 1.7 %fusion.139 = (f32[16,12,128]{1,0,2:T(8,128)}, f32[16,12,128]{1,0,2:T(8,128)}) fusion(f32[16,16,128]{1,0,2:T(8,128)S(1)} %get-tuple-element.14), kind=kLoop, calls=%fused_computation.264 | loop fusion | bytes 393216 | tf_op jit(solution)/shard_map/slice | solution.py:17
  9.2 1.6 %reshape.292 = f32[192,128]{0,1:T(8,128)S(1)} reshape(f32[16,12,128]{1,0,2:T(8,128)} %get-tuple-element.35) | data formatting | bytes 196608 | tf_op jit(solution)/shard_map/reshape | solution.py:68
  11.6 2.6 %collective-permute-start.4 = (f32[256,128]{1,0:T(8,128)}, f32[256,128]{1,0:T(8,128)}, u32[]{:S(2)}, u32[]{:S(2)}) collective-permute-start(f32[256,128]{1,0:T(8,128)} %pad_maximum_fusion.7), channel_id=1, source_target_pairs={{64,0},{128,64},{192,128},{256,192},{320,256},{384,320},{448,384},... | collective-permute-start | bytes 393224 | tf_op jit(solution)/shard_map/ppermute | solution.py:76
  14.6 1.6 %reshape.291 = f32[192,128]{0,1:T(8,128)S(1)} reshape(f32[16,12,128]{1,0,2:T(8,128)} %get-tuple-element.34) | data formatting | bytes 196608 | tf_op jit(solution)/shard_map/reshape | solution.py:68
  17.0 6.0 %collective-permute-start.3 = (f32[256,128]{1,0:T(8,128)}, f32[256,128]{1,0:T(8,128)}, u32[]{:S(2)}, u32[]{:S(2)}) collective-permute-start(f32[256,128]{1,0:T(8,128)} %pad_maximum_fusion.6), channel_id=1, source_target_pairs={{0,64},{64,128},{128,192},{192,256},{256,320},{320,384},{384,448},... | collective-permute-start | bytes 393224 | tf_op jit(solution)/shard_map/ppermute | solution.py:76
  23.1 0.8 fusion.138
  23.8 1.2 %fusion.137 = (f32[12,16,128]{1,0,2:T(8,128)S(1)}, f32[12,16,128]{1,0,2:T(8,128)}) fusion(f32[16,16,128]{1,0,2:T(8,128)S(1)} %get-tuple-element.14), kind=kLoop, calls=%fused_computation.262 | loop fusion | bytes 393216 | tf_op jit(solution)/shard_map/slice | solution.py:17
  25.0 1.0 copy.253
  26.1 1.5 %copy.252 = f32[12,16,128]{2,1,0:T(8,128)S(1)} copy(f32[12,16,128]{1,0,2:T(8,128)} %get-tuple-element.31) | data formatting | bytes 196608 | tf_op jit(solution)/shard_map/slice | solution.py:17
  28.3 5.9 %collective-permute-start.6 = (f32[256,128]{1,0:T(8,128)}, f32[256,128]{1,0:T(8,128)S(1)}, u32[]{:S(2)}, u32[]{:S(2)}) collective-permute-start(f32[256,128]{1,0:T(8,128)} %pad_maximum_fusion.8), channel_id=1, source_target_pairs={{1,0},{65,64},{129,128},{193,192},{257,256},{321,320},{385,384},{4... | collective-permute-start | bytes 393224 | tf_op jit(solution)/shard_map/ppermute | solution.py:76
  34.1 1.3 %fusion.136 = (f32[4,4,128]{1,0,2:T(4,128)}, f32[4,4,128]{1,0,2:T(4,128)}, f32[4,4,128]{1,0,2:T(4,128)}, f32[4,4,128]{1,0,2:T(4,128)}) fusion(f32[16,16,128]{1,0,2:T(8,128)S(1)} %get-tuple-element.15), kind=kLoop, calls=%fused_computation.261 | loop fusion | bytes 65536 | tf_op jit(solution)/shard_map/slice | solution.py:17
  35.4 2.7 %fusion.135 = (f32[12,12,128]{1,0,2:T(8,128)}, f32[12,12,128]{1,0,2:T(8,128)}, f32[12,12,128]{1,0,2:T(8,128)}, f32[12,12,128]{1,0,2:T(8,128)}) fusion(f32[16,16,128]{1,0,2:T(8,128)S(1)} %get-tuple-element.14), kind=kLoop, calls=%fused_computation.260 | loop fusion | bytes 589824 | tf_op jit(solution)/shard_map/slice | solution.py:17
  38.1 1.0 copy.240
  39.1 2.2 %copy.239 = f32[12,12,128]{2,1,0:T(8,128)} copy(f32[12,12,128]{1,0,2:T(8,128)} %get-tuple-element.22) | data formatting | bytes 147456 | tf_op jit(solution)/shard_map/slice | solution.py:17
  41.4 1.5 %reshape.181 = f32[144,128]{1,0:T(8,128)} reshape(f32[12,12,128]{2,1,0:T(8,128)} %copy.239) | data formatting | bytes 147456 | tf_op jit(solution)/shard_map/reshape | solution.py:68
  42.9 1.5 %pad_maximum_fusion.11 = f32[160,128]{1,0:T(8,128)} fusion(f32[16,128]{1,0:T(8,128)S(1)} %bitcast.190, f32[144,128]{1,0:T(8,128)} %reshape.181), kind=kLoop, calls=%fused_computation.78 | loop fusion | flops 20480 | bytes 163840 | tf_op jit(solution)/shard_map/concatenate | solution.py:69
  44.4 1.9 %collective-permute-start = (f32[160,128]{1,0:T(8,128)}, f32[160,128]{1,0:T(8,128)}, u32[]{:S(2)}, u32[]{:S(2)}) collective-permute-start(f32[160,128]{1,0:T(8,128)} %pad_maximum_fusion.11), channel_id=1, source_target_pairs={{0,65},{64,129},{128,193},{192,257},{256,321},{320,385},{384,449},... | collective-permute-start | bytes 245768 | tf_op jit(solution)/shard_map/ppermute | solution.py:76
  46.3 1.0 copy.255
  47.4 2.2 %copy.254 = f32[12,12,128]{2,1,0:T(8,128)} copy(f32[12,12,128]{1,0,2:T(8,128)} %get-tuple-element.23) | data formatting | bytes 147456 | tf_op jit(solution)/shard_map/slice | solution.py:17
  49.6 1.5 %reshape.202 = f32[144,128]{1,0:T(8,128)} reshape(f32[12,12,128]{2,1,0:T(8,128)} %copy.254) | data formatting | bytes 147456 | tf_op jit(solution)/shard_map/reshape | solution.py:68
  51.1 1.5 %pad_maximum_fusion.14 = f32[160,128]{1,0:T(8,128)} fusion(f32[16,128]{1,0:T(8,128)S(1)} %bitcast.191, f32[144,128]{1,0:T(8,128)} %reshape.202), kind=kLoop, calls=%fused_computation.81 | loop fusion | flops 20480 | bytes 163840 | tf_op jit(solution)/shard_map/concatenate | solution.py:69
  52.6 7.0 %collective-permute-start.7 = (f32[160,128]{1,0:T(8,128)}, f32[160,128]{1,0:T(8,128)}, u32[]{:S(2)}, u32[]{:S(2)}) collective-permute-start(f32[160,128]{1,0:T(8,128)} %pad_maximum_fusion.14), channel_id=1, source_target_pairs={{65,0},{129,64},{193,128},{257,192},{321,256},{385,320},{449,384},... | collective-permute-start | bytes 245768 | tf_op jit(solution)/shard_map/ppermute | solution.py:76
  59.6 0.7 copy.242
  60.3 1.0 copy.251
  61.4 1.1 copy.244
  62.8 1.6 %copy.250 = f32[12,12,128]{2,1,0:T(8,128)S(1)} copy(f32[12,12,128]{1,0,2:T(8,128)} %get-tuple-element.24) | data formatting | bytes 147456 | tf_op jit(solution)/shard_map/slice | solution.py:17
  65.5 0.9 pad_maximum_fusion.13
  66.4 1.9 %collective-permute-start.1 = (f32[256,128]{1,0:T(8,128)S(1)}, f32[256,128]{1,0:T(8,128)S(1)}, u32[]{:S(2)}, u32[]{:S(2)}) collective-permute-start(f32[256,128]{1,0:T(8,128)S(1)} %pad_maximum_fusion.5), channel_id=1, source_target_pairs={{0,1},{64,65},{128,129},{192,193},{256,257},{320,321},{384,385},{4... | collective-permute-start | bytes 393224 | tf_op jit(solution)/shard_map/ppermute | solution.py:76
  68.3 9.6 %collective-permute-start.5 = (f32[160,128]{1,0:T(8,128)S(1)}, f32[160,128]{1,0:T(8,128)S(1)}, u32[]{:S(2)}, u32[]{:S(2)}) collective-permute-start(f32[160,128]{1,0:T(8,128)S(1)} %pad_maximum_fusion.13), channel_id=1, source_target_pairs={{1,64},{65,128},{129,192},{193,256},{257,320},{321,384},{385,448},... | collective-permute-start | bytes 245768 | tf_op jit(solution)/shard_map/ppermute | solution.py:76
  77.9 1.4 %collective-permute-done.5 = f32[160,128]{1,0:T(8,128)S(1)} collective-permute-done((f32[160,128]{1,0:T(8,128)S(1)}, f32[160,128]{1,0:T(8,128)S(1)}, u32[]{:S(2)}, u32[]{:S(2)}) %collective-permute-start.5) | collective-permute-done | bytes 81952 | tf_op jit(solution)/shard_map/ppermute | solution.py:76
  79.3 2.1 %collective-permute-start.2 = (f32[160,128]{1,0:T(8,128)S(1)}, f32[160,128]{1,0:T(8,128)S(1)}, u32[]{:S(2)}, u32[]{:S(2)}) collective-permute-start(f32[160,128]{1,0:T(8,128)S(1)} %pad_maximum_fusion.12), channel_id=1, source_target_pairs={{64,1},{128,65},{192,129},{256,193},{320,257},{384,321},{448,385},... | collective-permute-start | bytes 245768 | tf_op jit(solution)/shard_map/ppermute | solution.py:76
  82.3 0.9 slice.1178
  83.2 0.9 slice.1199
  84.1 7.1 %collective-permute-done.2 = f32[160,128]{1,0:T(8,128)S(1)} collective-permute-done((f32[160,128]{1,0:T(8,128)S(1)}, f32[160,128]{1,0:T(8,128)S(1)}, u32[]{:S(2)}, u32[]{:S(2)}) %collective-permute-start.2) | collective-permute-done | bytes 81952 | tf_op jit(solution)/shard_map/ppermute | solution.py:76
  91.2 0.7 slice.1350
  92.6 0.8 slice.1354
  93.3 0.8 slice.1353
  95.8 0.8 pad_maximum_fusion.3
  96.6 0.9 slice.1190
  97.5 0.9 slice.1187
  99.5 0.8 multiply_bitcast_fusion
  103.9 0.8 copy.304
  105.7 0.9 pad_maximum_fusion.9
  109.8 0.9 slice.1387
  (209 shorter events, 22.4 us)
Async XLA Ops:
  0.6 1.4 %copy-start.1 = (f32[16,16,256]{2,1,0:T(8,128)S(1)}, f32[16,16,256]{2,1,0:T(8,128)}, u32[]{:S(2)}) copy-start(f32[16,16,256]{2,1,0:T(8,128)} %param.1) | copy-start | bytes 786436
  11.6 81.0 %collective-permute-start.4 = (f32[256,128]{1,0:T(8,128)}, f32[256,128]{1,0:T(8,128)}, u32[]{:S(2)}, u32[]{:S(2)}) collective-permute-start(f32[256,128]{1,0:T(8,128)} %pad_maximum_fusion.7), channel_id=1, source_target_pairs={{64,0},{128,64},{192,128},{256,192},{320,256},{384,320},{448,384},... | collective-permute-start | bytes 393224 | tf_op jit(solution)/shard_map/ppermute | solution.py:76
  17.0 76.3 %collective-permute-start.3 = (f32[256,128]{1,0:T(8,128)}, f32[256,128]{1,0:T(8,128)}, u32[]{:S(2)}, u32[]{:S(2)}) collective-permute-start(f32[256,128]{1,0:T(8,128)} %pad_maximum_fusion.6), channel_id=1, source_target_pairs={{0,64},{64,128},{128,192},{192,256},{256,320},{320,384},{384,448},... | collective-permute-start | bytes 393224 | tf_op jit(solution)/shard_map/ppermute | solution.py:76
  28.3 65.8 %collective-permute-start.6 = (f32[256,128]{1,0:T(8,128)}, f32[256,128]{1,0:T(8,128)S(1)}, u32[]{:S(2)}, u32[]{:S(2)}) collective-permute-start(f32[256,128]{1,0:T(8,128)} %pad_maximum_fusion.8), channel_id=1, source_target_pairs={{1,0},{65,64},{129,128},{193,192},{257,256},{321,320},{385,384},{4... | collective-permute-start | bytes 393224 | tf_op jit(solution)/shard_map/ppermute | solution.py:76
  44.4 21.9 %collective-permute-start = (f32[160,128]{1,0:T(8,128)}, f32[160,128]{1,0:T(8,128)}, u32[]{:S(2)}, u32[]{:S(2)}) collective-permute-start(f32[160,128]{1,0:T(8,128)} %pad_maximum_fusion.11), channel_id=1, source_target_pairs={{0,65},{64,129},{128,193},{192,257},{256,321},{320,385},{384,449},... | collective-permute-start | bytes 245768 | tf_op jit(solution)/shard_map/ppermute | solution.py:76
  52.6 15.7 %collective-permute-start.7 = (f32[160,128]{1,0:T(8,128)}, f32[160,128]{1,0:T(8,128)}, u32[]{:S(2)}, u32[]{:S(2)}) collective-permute-start(f32[160,128]{1,0:T(8,128)} %pad_maximum_fusion.14), channel_id=1, source_target_pairs={{65,0},{129,64},{193,128},{257,192},{321,256},{385,320},{449,384},... | collective-permute-start | bytes 245768 | tf_op jit(solution)/shard_map/ppermute | solution.py:76
  62.8 2.3 %copy-start = (f32[12,12,128]{1,0,2:T(8,128)S(1)}, f32[12,12,128]{1,0,2:T(8,128)}, u32[]{:S(2)}) copy-start(f32[12,12,128]{1,0,2:T(8,128)} %get-tuple-element.25) | copy-start | bytes 221188
  62.8 2.6 %copy-start.9 = (f32[4,16,128]{2,1,0:T(8,128)S(1)}, f32[4,16,128]{2,1,0:T(8,128)}, u32[]{:S(2)}) copy-start(f32[4,16,128]{2,1,0:T(8,128)} %copy.242) | copy-start | bytes 98308
  66.4 27.8 %collective-permute-start.1 = (f32[256,128]{1,0:T(8,128)S(1)}, f32[256,128]{1,0:T(8,128)S(1)}, u32[]{:S(2)}, u32[]{:S(2)}) collective-permute-start(f32[256,128]{1,0:T(8,128)S(1)} %pad_maximum_fusion.5), channel_id=1, source_target_pairs={{0,1},{64,65},{128,129},{192,193},{256,257},{320,321},{384,385},{4... | collective-permute-start | bytes 393224 | tf_op jit(solution)/shard_map/ppermute | solution.py:76
  68.3 11.0 %collective-permute-start.5 = (f32[160,128]{1,0:T(8,128)S(1)}, f32[160,128]{1,0:T(8,128)S(1)}, u32[]{:S(2)}, u32[]{:S(2)}) collective-permute-start(f32[160,128]{1,0:T(8,128)S(1)} %pad_maximum_fusion.13), channel_id=1, source_target_pairs={{1,64},{65,128},{129,192},{193,256},{257,320},{321,384},{385,448},... | collective-permute-start | bytes 245768 | tf_op jit(solution)/shard_map/ppermute | solution.py:76
  79.3 11.8 %collective-permute-start.2 = (f32[160,128]{1,0:T(8,128)S(1)}, f32[160,128]{1,0:T(8,128)S(1)}, u32[]{:S(2)}, u32[]{:S(2)}) collective-permute-start(f32[160,128]{1,0:T(8,128)S(1)} %pad_maximum_fusion.12), channel_id=1, source_target_pairs={{64,1},{128,65},{192,129},{256,193},{320,257},{384,321},{448,385},... | collective-permute-start | bytes 245768 | tf_op jit(solution)/shard_map/ppermute | solution.py:76
  94.1 0.9 copy-start.4
  94.1 0.7 copy-start.7
  95.1 3.3 %copy-start.2 = (f32[24,4,128]{2,1,0:T(4,128)}, f32[24,4,128]{2,1,0:T(4,128)S(1)}, u32[]{:S(2)}) copy-start(f32[24,4,128]{2,1,0:T(4,128)S(1)} %maximum_select_fusion.2) | copy-start | bytes 147460
  95.2 3.3 %copy-start.8 = (f32[256,128]{1,0:T(8,128)S(1)}, f32[256,128]{1,0:T(8,128)}, u32[]{:S(2)}) copy-start(f32[256,128]{1,0:T(8,128)} %copy-done.7) | copy-start | bytes 393220
  95.2 3.3 %slice-start.1 = ((f32[256,128]{1,0:T(8,128)}), f32[192,128]{1,0:T(8,128)S(1)}, s32[]{:S(2)}) async-start(f32[256,128]{1,0:T(8,128)} %copy-done.4), calls=%async_computation.1 | async-start | bytes 196608 | tf_op jit(solution)/shard_map/slice | solution.py:79
  106.9 2.4 %copy-start.3 = (f32[24,4,128]{2,1,0:T(4,128)S(1)}, f32[24,4,128]{2,1,0:T(4,128)}, u32[]{:S(2)}) copy-start(f32[24,4,128]{2,1,0:T(4,128)} %copy-done.2) | copy-start | bytes 147460
  106.9 2.4 %copy-start.5 = (f32[4,24,128]{2,1,0:T(8,128)S(1)}, f32[4,24,128]{2,1,0:T(8,128)}, u32[]{:S(2)}) copy-start(f32[4,24,128]{2,1,0:T(8,128)} %get-tuple-element.52) | copy-start | bytes 147460
  107.0 2.4 %copy-start.6 = (f32[4,24,128]{2,1,0:T(8,128)S(1)}, f32[4,24,128]{2,1,0:T(8,128)}, u32[]{:S(2)}) copy-start(f32[4,24,128]{2,1,0:T(8,128)} %get-tuple-element.53) | copy-start | bytes 147460
  107.7 1.7 %slice-start = ((f32[24,24,128]{2,1,0:T(8,128)}), f32[16,24,128]{2,1,0:T(8,128)S(1)}, s32[]{:S(2)}) async-start(f32[24,24,128]{2,1,0:T(8,128)} %pad_maximum_fusion.3), calls=%async_computation | async-start | bytes 393216 | tf_op jit(solution)/shard_map/slice | solution.py:17
  115.1 0.6 copy-start.11
  115.8 0.7 copy-start.10

commit v2 on v0

v2 whole, which is shorter than its diff:
```python
import numpy as np
import jax
import jax.numpy as jnp
from jax import lax
from jax.sharding import PartitionSpec as P

LIFT_ALPHA = -1.586134342059924
LIFT_BETA = -0.052980118572961
LIFT_GAMMA = 0.882911075530934
LIFT_DELTA = 0.443506852043971
LIFT_SCALE = 1.149604398860241

EXACT = lax.Precision.HIGHEST


def lift_rows(signal):
    extended = np.pad(signal, ((4, 4), (0, 0)), mode="reflect")
    even, odd = extended[0::2], extended[1::2]
    first_detail = odd[:-1] + LIFT_ALPHA * (even[:-1] + even[1:])
    first_smooth = even[1:-1] + LIFT_BETA * (first_detail[:-1] + first_detail[1:])
    second_detail = first_detail[1:-1] + LIFT_GAMMA * (first_smooth[:-1] + first_smooth[1:])
    second_smooth = first_smooth[1:-1] + LIFT_DELTA * (second_detail[:-1] + second_detail[1:])
    return second_smooth * LIFT_SCALE, second_detail[1:] / LIFT_SCALE


def level_maps(length):
    low, high = lift_rows(np.eye(length))
    low_two, high_two = lift_rows(low)
    return (low, high), (low_two, high_two)


def window_maps(block, halo, level, blocks=8):
    length = block * blocks
    bands = level_maps(length)[level]
    share = block // (2 * (level + 1))
    width = halo[0] + block + halo[1]
    maps = []
    for place in (0, blocks // 2, blocks - 1):
        rows = np.concatenate([band[place * share : (place + 1) * share] for band in bands])
        matrix = np.zeros((rows.shape[0], width))
        for i in range(width):
            cell = place * block - halo[0] + i
            if 0 <= cell < length:
                matrix[:, i] = rows[:, cell]
        maps.append(matrix.astype(np.float32))
    return maps


def chosen(maps, at_low, at_high):
    low, inside, high = (jnp.asarray(m) for m in maps)
    return jnp.where(at_low, low, jnp.where(at_high, high, inside))


def exchange(lower_half, upper_half, axis):
    devices = lax.axis_size(axis)
    up = [(i, i + 1) for i in range(devices - 1)]
    down = [(i + 1, i) for i in range(devices - 1)]
    from_below = lax.ppermute(upper_half, axis, up)
    from_above = lax.ppermute(lower_half, axis, down)
    return from_below, from_above


def per_device(velocity):
    nx, ny, nz = velocity.shape
    slab_low = lax.axis_index("slab") == 0
    slab_high = lax.axis_index("slab") == lax.axis_size("slab") - 1
    brick_low = lax.axis_index("morton") == 0
    brick_high = lax.axis_index("morton") == lax.axis_size("morton") - 1

    (z_low, z_high), (z2_low, z2_high) = level_maps(nz)
    z_maps = np.stack([z_low.T, z_high.T, np.concatenate([z2_low, z2_high]).T]).astype(np.float32)
    lanes = z_maps.shape[2]
    u = jnp.einsum("xyz,bzk->xbyk", velocity, jnp.asarray(z_maps), precision=EXACT)

    wide = 12
    one_rows = u[:, 0:2]
    two_rows = u[:, 2]
    flat = lambda a: a.reshape(-1, lanes)
    top = jnp.concatenate([flat(one_rows[nx - 4 :]), flat(two_rows[nx - wide :])])
    bottom = jnp.concatenate([flat(one_rows[:4]), flat(two_rows[:wide])])
    below, above = exchange(bottom, top, "slab")
    split = 4 * 2 * ny
    one_ext = jnp.concatenate(
        [below[:split].reshape(4, 2, ny, lanes), one_rows, above[:split].reshape(4, 2, ny, lanes)]
    )
    two_ext = jnp.concatenate(
        [below[split:].reshape(wide, ny, lanes), two_rows, above[split:].reshape(wide, ny, lanes)]
    )
    a1x = chosen(window_maps(nx, (4, 4), 0), slab_low, slab_high)
    a2x = chosen(window_maps(nx, (wide, wide), 1), slab_low, slab_high)
    x_one = jnp.einsum("kx,xbyz->kbyz", a1x, one_ext, precision=EXACT)
    x_two = jnp.einsum("kx,xyz->kyz", a2x, two_ext, precision=EXACT)

    narrow = 8
    kx1, kx2 = x_one.shape[0], x_two.shape[0]
    top = jnp.concatenate([flat(x_one[:, :, ny - narrow :]), flat(x_two)])
    bottom = jnp.concatenate([flat(x_one[:, :, :narrow]), flat(x_two)])
    below, above = exchange(bottom, top, "morton")
    split = kx1 * 2 * narrow
    one_ext = jnp.concatenate(
        [
            below[:split].reshape(kx1, 2, narrow, lanes),
            x_one,
            above[:split].reshape(kx1, 2, narrow, lanes),
        ],
        axis=2,
    )
    two_ext = jnp.concatenate(
        [below[split:].reshape(kx2, ny, lanes), x_two, above[split:].reshape(kx2, ny, lanes)],
        axis=1,
    )
    a1y = chosen(window_maps(ny, (narrow, narrow), 0), brick_low, brick_high)
    a2y = chosen(window_maps(ny, (ny, ny), 1), brick_low, brick_high)
    y_one = jnp.einsum("ky,abyz->abkz", a1y, one_ext, precision=EXACT)
    y_two = jnp.einsum("ky,ayz->akz", a2y, two_ext, precision=EXACT)

    hx, hy = nx // 2, ny // 2
    level_one = y_one.reshape(2, hx, 2, 2, hy, lanes).transpose(0, 3, 2, 1, 4, 5)
    level_one = level_one.reshape(8, hx, hy, lanes)
    qx, qy, qz = nx // 4, ny // 4, nz // 4
    level_two = y_two.reshape(2, qx, 2, qy, 2, qz).transpose(0, 2, 4, 1, 3, 5)
    level_two = level_two.reshape(8, qx, qy, qz)
    return (level_two[0], level_two[1:], level_one[1:])


def solution(mesh):
    placed = (P("slab", "morton", None),)
    return jax.shard_map(
        per_device,
        mesh=mesh,
        in_specs=placed,
        out_specs=(
            P("slab", "morton", None),
            P(None, "slab", "morton", None),
            P(None, "slab", "morton", None),
        ),
        check_vma=False,
    )
```

time: 70.2 us -> 43.7 us (0.62)
  the two profiles are of different devices: /device:TPU:265 before, /device:TPU:393 now
where the time goes in v2:
time: 43.7 us; the launch traced here: 43.2 us
  starting transfers between devices  17.6 us (40%)
  waiting for transfers between devices  14.2 us (32%)
  local copies, waits for them, and re-layouts  6.98 us (16%)
  matrix products  3.22 us (7%)
  between operations  1.03 us (2%)
    ppermute x2, starting transfers between devices, exchange(): from_below = lax.ppermute(upper_half, axis, up)  9.78 us
    ppermute x2, waiting for transfers between devices, exchange(): from_below = lax.ppermute(upper_half, axis, up)  7.8 us
    ppermute x2, starting transfers between devices, exchange(): from_above = lax.ppermute(lower_half, axis, down)  7.78 us
    ppermute x2, waiting for transfers between devices, exchange(): from_above = lax.ppermute(lower_half, axis, down)  6.42 us
    unnamed x30, local copies, waits for them, and re-layouts  3.65 us
    dot_general x1, matrix products, per_device(): jnp.einsum('xyz,bzk->xbyk', velocity, jnp.asarray(z_maps), precision=EXACT)  1.62 us
    slice x2, local copies, waits for them, and re-layouts, per_device(): return (level_two[0], level_two[1:], level_one[1:])  1.33 us
    slice x2, local copies, waits for them, and re-layouts, per_device(): one_rows = u[:, 0:2]  0.89 us
  transfers between devices with their start and end apart: 4, of which 4 were waited for; matrix products, arithmetic and copies ran while one was open for 0% of the time, Pallas kernels for 0%

profile of v2, /device:TPU:393, one launch (start us, length us, event | category | flops | bytes accessed | tf_op | source)
XLA Modules:
  0.0 43.2 jit_solution(9045862620178365223)
XLA Ops:
  0.6 0.0 copy-start
  0.6 0.9 %copy-done = f32[16,16,256]{2,1,0:T(8,128)S(1)} copy-done((f32[16,16,256]{2,1,0:T(8,128)S(1)}, f32[16,16,256]{2,1,0:T(8,128)}, u32[]{:S(2)}) %copy-start) | copy-done | bytes 262168
  1.6 1.6 %convolution_bitcast_fusion = f32[16,3,16,128]{3,2,0,1:T(8,128)S(1)} fusion(f32[3,256,128,1]{2,1,3,0:T(8,128)} %constant.55, f32[16,16,256]{2,1,0:T(8,128)S(1)} %copy-done), kind=kOutput, calls=%fused_computation | convolution fusion | flops 301989888 | bytes 1048576 | tf_op jit(solution)/shard_map/xyz,bzk->xbyk/dot_general | solution.py:73
  3.2 0.0 copy-start.1
  3.3 5.9 %collective-permute-start.1 = (f32[320,128]{1,0:T(8,128)S(1)}, f32[320,128]{1,0:T(8,128)S(1)}, u32[]{:S(2)}, u32[]{:S(2)}) collective-permute-start(f32[320,128]{1,0:T(8,128)S(1)} %pad_maximum_fusion.7), channel_id=1, source_target_pairs={{1,0},{2,1},{3,2},{4,3},{5,4},{6,5},{7,6},{8,7},{9,8},{10,9},{11,1... | collective-permute-start | bytes 491528 | tf_op jit(solution)/shard_map/ppermute | solution.py:59
  9.2 1.9 %collective-permute-start = (f32[320,128]{1,0:T(8,128)S(1)}, f32[320,128]{1,0:T(8,128)S(1)}, u32[]{:S(2)}, u32[]{:S(2)}) collective-permute-start(f32[320,128]{1,0:T(8,128)S(1)} %pad_maximum_fusion.6), channel_id=1, source_target_pairs={{0,1},{1,2},{2,3},{3,4},{4,5},{5,6},{6,7},{7,8},{8,9},{9,10},{10,1... | collective-permute-start | bytes 491528 | tf_op jit(solution)/shard_map/ppermute | solution.py:58
  11.1 0.0 copy-done.1
  11.2 0.8 %collective-permute-done.1 = f32[320,128]{1,0:T(8,128)S(1)} collective-permute-done((f32[320,128]{1,0:T(8,128)S(1)}, f32[320,128]{1,0:T(8,128)S(1)}, u32[]{:S(2)}, u32[]{:S(2)}) %collective-permute-start.1) | collective-permute-done | bytes 163872 | tf_op jit(solution)/shard_map/ppermute | solution.py:59
  12.0 0.0 copy-start.2
  12.0 7.1 %collective-permute-done = f32[320,128]{1,0:T(8,128)S(1)} collective-permute-done((f32[320,128]{1,0:T(8,128)S(1)}, f32[320,128]{1,0:T(8,128)S(1)}, u32[]{:S(2)}, u32[]{:S(2)}) %collective-permute-start) | collective-permute-done | bytes 163872 | tf_op jit(solution)/shard_map/ppermute | solution.py:58
  19.2 0.0 copy-start.12
  19.2 0.0 copy-start.13
  19.2 0.0 copy-start.14
  19.3 0.6 %copy-done.12 = f32[8,40]{1,0:T(8,128)S(1)} copy-done((f32[8,40]{1,0:T(8,128)S(1)}, f32[8,40]{1,0:T(8,128)}, u32[]{:S(2)}) %copy-start.12) | copy-done | bytes 1304
  19.9 0.0 copy-done.13
  19.9 0.0 copy-done.14
  19.9 0.4 fusion.4
  20.3 0.0 slice-start
  20.3 0.0 copy-done.2
  20.3 0.0 slice-start.1
  20.3 0.9 %slice-done = f32[16,2,16,128]{3,2,0,1:T(8,128)S(1)} async-done(((f32[16,3,16,128]{3,2,0,1:T(8,128)}), f32[16,2,16,128]{3,2,0,1:T(8,128)S(1)}, s32[]{:S(2)}) %slice-start) | async-done | bytes 262168 | tf_op jit(solution)/shard_map/slice | solution.py:76
  21.2 0.0 slice-done.1
  21.3 0.7 %copy-done.6 = f32[16,24]{1,0:T(8,128)S(1)} copy-done((f32[16,24]{1,0:T(8,128)S(1)}, f32[16,24]{1,0:T(8,128)}, u32[]{:S(2)}) %copy-start.6) | copy-done | bytes 1560
  21.9 0.0 copy-done.7
  21.9 0.0 copy-done.8
  22.0 0.5 %fusion.2 = f32[16,2,16,128]{3,0,2,1:T(8,128)S(1)} fusion(f32[24,2,16,128]{3,2,0,1:T(8,128)S(1)} %pad_maximum_fusion.1, f32[16,24]{1,0:T(8,128)S(1)} %copy-done.8, f32[16,24]{1,0:T(8,128)S(1)} %copy-done.6, f32[16,24]{1,0:T(8,128)S(1)} %copy-done.7, pred[]{:T(512)S(6)} %eq.13, pred[]{:T(512)S(6)} %eq.12), kind=kOutput, calls=%fused_computation.6 | convolution fusion | flops 18875136 | bytes 659970 | tf_op jit(solution)/shard_map/kx,xbyz->kbyz/dot_general | solution.py:91
  22.6 7.9 %collective-permute-start.2 = (f32[384,128]{1,0:T(8,128)S(1)}, f32[384,128]{1,0:T(8,128)S(1)}, u32[]{:S(2)}, u32[]{:S(2)}) collective-permute-start(f32[384,128]{1,0:T(8,128)S(1)} %get-tuple-element.9), channel_id=1, source_target_pairs={{0,64},{64,128},{128,192},{192,256},{256,320},{320,384},{384,448},... | collective-permute-start | bytes 589832 | tf_op jit(solution)/shard_map/ppermute | solution.py:58
  30.5 1.9 %collective-permute-start.3 = (f32[384,128]{1,0:T(8,128)S(1)}, f32[384,128]{1,0:T(8,128)S(1)}, u32[]{:S(2)}, u32[]{:S(2)}) collective-permute-start(f32[384,128]{1,0:T(8,128)S(1)} %get-tuple-element.10), channel_id=1, source_target_pairs={{64,0},{128,64},{192,128},{256,192},{320,256},{384,320},{448,384},... | collective-permute-start | bytes 589832 | tf_op jit(solution)/shard_map/ppermute | solution.py:59
  32.4 0.7 %collective-permute-done.2 = f32[384,128]{1,0:T(8,128)S(1)} collective-permute-done((f32[384,128]{1,0:T(8,128)S(1)}, f32[384,128]{1,0:T(8,128)S(1)}, u32[]{:S(2)}, u32[]{:S(2)}) %collective-permute-start.2) | collective-permute-done | bytes 196640 | tf_op jit(solution)/shard_map/ppermute | solution.py:58
  33.1 5.6 %collective-permute-done.3 = f32[384,128]{1,0:T(8,128)S(1)} collective-permute-done((f32[384,128]{1,0:T(8,128)S(1)}, f32[384,128]{1,0:T(8,128)S(1)}, u32[]{:S(2)}, u32[]{:S(2)}) %collective-permute-start.3) | collective-permute-done | bytes 196640 | tf_op jit(solution)/shard_map/ppermute | solution.py:59
  38.7 0.0 copy-start.9
  38.7 0.0 copy-start.10
  38.7 0.0 copy-start.11
  38.8 0.6 %copy-done.9 = f32[8,48]{1,0:T(8,128)S(1)} copy-done((f32[8,48]{1,0:T(8,128)S(1)}, f32[8,48]{1,0:T(8,128)}, u32[]{:S(2)}) %copy-start.9) | copy-done | bytes 1560
  39.4 0.0 copy-done.10
  39.4 0.0 copy-done.11
  39.4 0.2 convolution_bitcast_fusion.1
  39.7 0.1 reshape.81
  39.8 0.6 %slice_bitcast_fusion.1 = f32[4,4,64]{2,1,0:T(4,128)} fusion(f32[8,4,4,64]{3,2,1,0:T(4,128)S(1)} %bitcast.68), kind=kLoop, calls=%fused_computation.19 | loop fusion | bytes 8192 | tf_op jit(solution)/shard_map/squeeze | solution.py:123
  40.4 0.6 %slice.97 = f32[7,4,4,64]{3,2,1,0:T(4,128)} slice(f32[8,4,4,64]{3,2,1,0:T(4,128)S(1)} %bitcast.69), slice={[1:8], [0:4], [0:4], [0:64]} | slice | bytes 57344 | tf_op jit(solution)/shard_map/slice | solution.py:123
  41.2 0.0 copy-start.3
  41.2 0.0 copy-start.4
  41.2 0.0 copy-start.5
  41.2 0.6 %copy-done.3 = f32[16,32]{1,0:T(8,128)S(1)} copy-done((f32[16,32]{1,0:T(8,128)S(1)}, f32[16,32]{1,0:T(8,128)}, u32[]{:S(2)}) %copy-start.3) | copy-done | bytes 2072
  41.9 0.0 copy-done.4
  41.9 0.0 copy-done.5
  41.9 0.5 %fusion = f32[16,2,128,16]{2,3,1,0:T(8,128)S(1)} fusion(f32[16,2,32,128]{3,0,2,1:T(8,128)S(1)} %pad_maximum_fusion, f32[16,32]{1,0:T(8,128)S(1)} %copy-done.5, f32[16,32]{1,0:T(8,128)S(1)} %copy-done.3, f32[16,32]{1,0:T(8,128)S(1)} %copy-done.4, pred[]{:T(512)S(6)} %eq.15, pred[]{:T(512)S(6)} %eq.14), kind=kOutput, calls=%fused_computation.3 | convolution fusion | flops 25166848 | bytes 792578 | tf_op jit(solution)/shard_map/ky,abyz->abkz/dot_general | solution.py:114
  42.5 0.7 %slice.100 = f32[7,8,8,128]{3,2,1,0:T(8,128)} slice(f32[8,8,8,128]{3,2,1,0:T(8,128)S(1)} %bitcast.55), slice={[1:8], [0:8], [0:8], [0:128]} | slice | bytes 458752 | tf_op jit(solution)/shard_map/slice | solution.py:123
  (32 shorter events, 0.6 us)
Async XLA Ops:
  0.6 1.0 %copy-start = (f32[16,16,256]{2,1,0:T(8,128)S(1)}, f32[16,16,256]{2,1,0:T(8,128)}, u32[]{:S(2)}) copy-start(f32[16,16,256]{2,1,0:T(8,128)} %param.14) | copy-start | bytes 786436
  3.2 7.9 %copy-start.1 = (f32[16,3,16,128]{3,2,0,1:T(8,128)}, f32[16,3,16,128]{3,2,0,1:T(8,128)S(1)}, u32[]{:S(2)}) copy-start(f32[16,3,16,128]{3,2,0,1:T(8,128)S(1)} %convolution_bitcast_fusion) | copy-start | bytes 1179652
  3.3 8.7 %collective-permute-start.1 = (f32[320,128]{1,0:T(8,128)S(1)}, f32[320,128]{1,0:T(8,128)S(1)}, u32[]{:S(2)}, u32[]{:S(2)}) collective-permute-start(f32[320,128]{1,0:T(8,128)S(1)} %pad_maximum_fusion.7), channel_id=1, source_target_pairs={{1,0},{2,1},{3,2},{4,3},{5,4},{6,5},{7,6},{8,7},{9,8},{10,9},{11,1... | collective-permute-start | bytes 491528 | tf_op jit(solution)/shard_map/ppermute | solution.py:59
  9.2 10.0 %collective-permute-start = (f32[320,128]{1,0:T(8,128)S(1)}, f32[320,128]{1,0:T(8,128)S(1)}, u32[]{:S(2)}, u32[]{:S(2)}) collective-permute-start(f32[320,128]{1,0:T(8,128)S(1)} %pad_maximum_fusion.6), channel_id=1, source_target_pairs={{0,1},{1,2},{2,3},{3,4},{4,5},{5,6},{6,7},{7,8},{8,9},{9,10},{10,1... | collective-permute-start | bytes 491528 | tf_op jit(solution)/shard_map/ppermute | solution.py:58
  12.0 8.3 %copy-start.2 = (f32[320,128]{1,0:T(8,128)}, f32[320,128]{1,0:T(8,128)S(1)}, u32[]{:S(2)}) copy-start(f32[320,128]{1,0:T(8,128)S(1)} %collective-permute-done.1) | copy-start | bytes 491524
  19.2 0.7 %copy-start.12 = (f32[8,40]{1,0:T(8,128)S(1)}, f32[8,40]{1,0:T(8,128)}, u32[]{:S(2)}) copy-start(f32[8,40]{1,0:T(8,128)} %constant.47.clone) | copy-start | bytes 3844
  19.2 0.7 %copy-start.13 = (f32[8,40]{1,0:T(8,128)S(1)}, f32[8,40]{1,0:T(8,128)}, u32[]{:S(2)}) copy-start(f32[8,40]{1,0:T(8,128)} %constant.46.clone) | copy-start | bytes 3844
  19.2 0.7 %copy-start.14 = (f32[8,40]{1,0:T(8,128)S(1)}, f32[8,40]{1,0:T(8,128)}, u32[]{:S(2)}) copy-start(f32[8,40]{1,0:T(8,128)} %constant.45.clone) | copy-start | bytes 3844
  20.3 1.0 %slice-start = ((f32[16,3,16,128]{3,2,0,1:T(8,128)}), f32[16,2,16,128]{3,2,0,1:T(8,128)S(1)}, s32[]{:S(2)}) async-start(f32[16,3,16,128]{3,2,0,1:T(8,128)} %copy-done.1), calls=%async_computation | async-start | bytes 524288 | tf_op jit(solution)/shard_map/slice | solution.py:76
  20.3 0.9 %slice-start.1 = ((f32[320,128]{1,0:T(8,128)}), f32[128,128]{1,0:T(8,128)S(1)}, s32[]{:S(2)}) async-start(f32[320,128]{1,0:T(8,128)} %copy-done.2), calls=%async_computation.1 | async-start | bytes 131072 | tf_op jit(solution)/shard_map/slice | solution.py:84
  21.2 0.7 %copy-start.6 = (f32[16,24]{1,0:T(8,128)S(1)}, f32[16,24]{1,0:T(8,128)}, u32[]{:S(2)}) copy-start(f32[16,24]{1,0:T(8,128)} %constant.44.clone) | copy-start | bytes 4612
  21.2 0.7 %copy-start.7 = (f32[16,24]{1,0:T(8,128)S(1)}, f32[16,24]{1,0:T(8,128)}, u32[]{:S(2)}) copy-start(f32[16,24]{1,0:T(8,128)} %constant.43.clone) | copy-start | bytes 4612
  21.2 0.7 %copy-start.8 = (f32[16,24]{1,0:T(8,128)S(1)}, f32[16,24]{1,0:T(8,128)}, u32[]{:S(2)}) copy-start(f32[16,24]{1,0:T(8,128)} %constant.42.clone) | copy-start | bytes 4612
  22.6 10.5 %collective-permute-start.2 = (f32[384,128]{1,0:T(8,128)S(1)}, f32[384,128]{1,0:T(8,128)S(1)}, u32[]{:S(2)}, u32[]{:S(2)}) collective-permute-start(f32[384,128]{1,0:T(8,128)S(1)} %get-tuple-element.9), channel_id=1, source_target_pairs={{0,64},{64,128},{128,192},{192,256},{256,320},{320,384},{384,448},... | collective-permute-start | bytes 589832 | tf_op jit(solution)/shard_map/ppermute | solution.py:58
  30.5 8.2 %collective-permute-start.3 = (f32[384,128]{1,0:T(8,128)S(1)}, f32[384,128]{1,0:T(8,128)S(1)}, u32[]{:S(2)}, u32[]{:S(2)}) collective-permute-start(f32[384,128]{1,0:T(8,128)S(1)} %get-tuple-element.10), channel_id=1, source_target_pairs={{64,0},{128,64},{192,128},{256,192},{320,256},{384,320},{448,384},... | collective-permute-start | bytes 589832 | tf_op jit(solution)/shard_map/ppermute | solution.py:59
  38.7 0.7 %copy-start.9 = (f32[8,48]{1,0:T(8,128)S(1)}, f32[8,48]{1,0:T(8,128)}, u32[]{:S(2)}) copy-start(f32[8,48]{1,0:T(8,128)} %constant.53.clone) | copy-start | bytes 4612
  38.7 0.7 %copy-start.10 = (f32[8,48]{1,0:T(8,128)S(1)}, f32[8,48]{1,0:T(8,128)}, u32[]{:S(2)}) copy-start(f32[8,48]{1,0:T(8,128)} %constant.52.clone) | copy-start | bytes 4612
  38.7 0.7 %copy-start.11 = (f32[8,48]{1,0:T(8,128)S(1)}, f32[8,48]{1,0:T(8,128)}, u32[]{:S(2)}) copy-start(f32[8,48]{1,0:T(8,128)} %constant.51.clone) | copy-start | bytes 4612
  41.2 0.7 %copy-start.3 = (f32[16,32]{1,0:T(8,128)S(1)}, f32[16,32]{1,0:T(8,128)}, u32[]{:S(2)}) copy-start(f32[16,32]{1,0:T(8,128)} %constant.50.clone) | copy-start | bytes 6148
  41.2 0.7 %copy-start.4 = (f32[16,32]{1,0:T(8,128)S(1)}, f32[16,32]{1,0:T(8,128)}, u32[]{:S(2)}) copy-start(f32[16,32]{1,0:T(8,128)} %constant.49.clone) | copy-start | bytes 6148
  41.2 0.7 %copy-start.5 = (f32[16,32]{1,0:T(8,128)S(1)}, f32[16,32]{1,0:T(8,128)}, u32[]{:S(2)}) copy-start(f32[16,32]{1,0:T(8,128)} %constant.48.clone) | copy-start | bytes 6148

commit v3 on v2

--- a/solution.py
+++ b/solution.py
@@ -51,13 +51,46 @@
     return jnp.where(at_low, low, jnp.where(at_high, high, inside))
 
 
-def exchange(lower_half, upper_half, axis):
-    devices = lax.axis_size(axis)
-    up = [(i, i + 1) for i in range(devices - 1)]
-    down = [(i + 1, i) for i in range(devices - 1)]
-    from_below = lax.ppermute(upper_half, axis, up)
-    from_above = lax.ppermute(lower_half, axis, down)
-    return from_below, from_above
+def neighbours(pieces_of):
+    slabs, bricks = lax.axis_size("slab"), lax.axis_size("morton")
+    received = {}
+    for ox in (-1, 0, 1):
+        for oy in (-1, 0, 1):
+            if ox == 0 and oy == 0:
+                continue
+            pieces = pieces_of(ox, oy)
+            message = jnp.concatenate([p.reshape(-1, p.shape[-1]) for p in pieces])
+            pairs = []
+            for s in range(slabs):
+                for m in range(bricks):
+                    s_from, m_from = s + ox, m + oy
+                    if 0 <= s_from < slabs and 0 <= m_from < bricks:
+                        pairs.append((m_from * slabs + s_from, m * slabs + s))
+            arrived = lax.ppermute(message, ("morton", "slab"), pairs)
+            unpacked, at = [], 0
+            for p in pieces:
+                rows = p.size // p.shape[-1]
+                unpacked.append(arrived[at : at + rows].reshape(p.shape))
+                at += rows
+            received[(ox, oy)] = unpacked
+    return received
+
+
+def edge(block, offset, width, dimension):
+    length = block.shape[dimension]
+    if offset < 0:
+        return lax.slice_in_dim(block, length - width, length, axis=dimension)
+    if offset > 0:
+        return lax.slice_in_dim(block, 0, width, axis=dimension)
+    return block
+
+
+def assemble(own, received, which, x_dim, y_dim):
+    rows = []
+    for ox in (-1, 0, 1):
+        row = [own if ox == 0 and oy == 0 else received[(ox, oy)][which] for oy in (-1, 0, 1)]
+        rows.append(jnp.concatenate(row, axis=y_dim))
+    return jnp.concatenate(rows, axis=x_dim)
 
 
 def per_device(velocity):
@@ -71,48 +104,29 @@
     z_maps = np.stack([z_low.T, z_high.T, np.concatenate([z2_low, z2_high]).T]).astype(np.float32)
     lanes = z_maps.shape[2]
     u = jnp.einsum("xyz,bzk->xbyk", velocity, jnp.asarray(z_maps), precision=EXACT)
+    one = u[:, 0:2]
+    two = u[:, 2]
 
-    wide = 12
-    one_rows = u[:, 0:2]
-    two_rows = u[:, 2]
-    flat = lambda a: a.reshape(-1, lanes)
-    top = jnp.concatenate([flat(one_rows[nx - 4 :]), flat(two_rows[nx - wide :])])
-    bottom = jnp.concatenate([flat(one_rows[:4]), flat(two_rows[:wide])])
-    below, above = exchange(bottom, top, "slab")
-    split = 4 * 2 * ny
-    one_ext = jnp.concatenate(
-        [below[:split].reshape(4, 2, ny, lanes), one_rows, above[:split].reshape(4, 2, ny, lanes)]
-    )
-    two_ext = jnp.concatenate(
-        [below[split:].reshape(wide, ny, lanes), two_rows, above[split:].reshape(wide, ny, lanes)]
-    )
-    a1x = chosen(window_maps(nx, (4, 4), 0), slab_low, slab_high)
-    a2x = chosen(window_maps(nx, (wide, wide), 1), slab_low, slab_high)
+    rows_one, rows_two, cols_one, cols_two = 4, 12, 8, ny
+
+    def pieces_of(ox, oy):
+        return [
+            edge(edge(one, ox, rows_one, 0), oy, cols_one, 2),
+            edge(edge(two, ox, rows_two, 0), oy, cols_two, 1),
+        ]
+
+    received = neighbours(pieces_of)
+    one_ext = assemble(one, received, 0, 0, 2)
+    two_ext = assemble(two, received, 1, 0, 1)
+
+    a1x = chosen(window_maps(nx, (rows_one, rows_one), 0), slab_low, slab_high)
+    a2x = chosen(window_maps(nx, (rows_two, rows_two), 1), slab_low, slab_high)
+    a1y = chosen(window_maps(ny, (cols_one, cols_one), 0), brick_low, brick_high)
+    a2y = chosen(window_maps(ny, (cols_two, cols_two), 1), brick_low, brick_high)
     x_one = jnp.einsum("kx,xbyz->kbyz", a1x, one_ext, precision=EXACT)
     x_two = jnp.einsum("kx,xyz->kyz", a2x, two_ext, precision=EXACT)
-
-    narrow = 8
-    kx1, kx2 = x_one.shape[0], x_two.shape[0]
-    top = jnp.concatenate([flat(x_one[:, :, ny - narrow :]), flat(x_two)])
-    bottom = jnp.concatenate([flat(x_one[:, :, :narrow]), flat(x_two)])
-    below, above = exchange(bottom, top, "morton")
-    split = kx1 * 2 * narrow
-    one_ext = jnp.concatenate(
-        [
-            below[:split].reshape(kx1, 2, narrow, lanes),
-            x_one,
-            above[:split].reshape(kx1, 2, narrow, lanes),
-        ],
-        axis=2,
-    )
-    two_ext = jnp.concatenate(
-        [below[split:].reshape(kx2, ny, lanes), x_two, above[split:].reshape(kx2, ny, lanes)],
-        axis=1,
-    )
-    a1y = chosen(window_maps(ny, (narrow, narrow), 0), brick_low, brick_high)
-    a2y = chosen(window_maps(ny, (ny, ny), 1), brick_low, brick_high)
-    y_one = jnp.einsum("ky,abyz->abkz", a1y, one_ext, precision=EXACT)
-    y_two = jnp.einsum("ky,ayz->akz", a2y, two_ext, precision=EXACT)
+    y_one = jnp.einsum("ky,abyz->abkz", a1y, x_one, precision=EXACT)
+    y_two = jnp.einsum("ky,ayz->akz", a2y, x_two, precision=EXACT)
 
     hx, hy = nx // 2, ny // 2
     level_one = y_one.reshape(2, hx, 2, 2, hy, lanes).transpose(0, 3, 2, 1, 4, 5)

time: 43.7 us -> 54 us (1.24)
  the two profiles are of different devices: /device:TPU:393 before, /device:TPU:503 now
where the time goes in v3:
time: 54 us; the launch traced here: 53.4 us
  starting transfers between devices  36.1 us (67%)
  local copies, waits for them, and re-layouts  6.76 us (13%)
  waiting for transfers between devices  4.76 us (9%)
  matrix products  4.22 us (8%)
  between operations  1.26 us (2%)
    ppermute x8, starting transfers between devices, neighbours(): arrived = lax.ppermute(message, ('morton', 'slab'), pairs)  36.1 us
    ppermute x8, waiting for transfers between devices, neighbours(): arrived = lax.ppermute(message, ('morton', 'slab'), pairs)  4.76 us
    unnamed x40, local copies, waits for them, and re-layouts  3.55 us
    dot_general x1, matrix products, per_device(): jnp.einsum('xyz,bzk->xbyk', velocity, jnp.asarray(z_maps), precision=EXACT)  1.62 us
    slice x2, local copies, waits for them, and re-layouts, per_device(): return (level_two[0], level_two[1:], level_one[1:])  1.33 us
  transfers between devices with their start and end apart: 8, of which 1 were waited for; matrix products, arithmetic and copies ran while one was open for 0% of the time, Pallas kernels for 0%

profile of v3, /device:TPU:503, one launch (start us, length us, event | category | flops | bytes accessed | tf_op | source)
XLA Modules:
  0.0 53.4 jit_solution(8018456322279050070)
XLA Ops:
  0.6 0.0 copy-start
  0.6 0.9 %copy-done = f32[16,16,256]{2,1,0:T(8,128)S(1)} copy-done((f32[16,16,256]{2,1,0:T(8,128)S(1)}, f32[16,16,256]{2,1,0:T(8,128)}, u32[]{:S(2)}) %copy-start) | copy-done | bytes 262168
  1.6 1.6 %convolution_bitcast_fusion = f32[16,3,16,128]{3,2,0,1:T(8,128)S(1)} fusion(f32[3,256,128,1]{2,1,3,0:T(8,128)} %constant.55, f32[16,16,256]{2,1,0:T(8,128)S(1)} %copy-done), kind=kOutput, calls=%fused_computation | convolution fusion | flops 301989888 | bytes 1048576 | tf_op jit(solution)/shard_map/xyz,bzk->xbyk/dot_general | solution.py:106
  3.3 7.4 %collective-permute-start.5 = (f32[256,128]{1,0:T(8,128)S(1)}, f32[256,128]{1,0:T(8,128)S(1)}, u32[]{:S(2)}, u32[]{:S(2)}) collective-permute-start(f32[256,128]{1,0:T(8,128)S(1)} %get-tuple-element.23), channel_id=1, source_target_pairs={{1,64},{65,128},{129,192},{193,256},{257,320},{321,384},{385,448},... | collective-permute-start | bytes 393224 | tf_op jit(solution)/shard_map/ppermute | solution.py:69
  10.7 1.9 %collective-permute-start.7 = (f32[256,128]{1,0:T(8,128)S(1)}, f32[256,128]{1,0:T(8,128)S(1)}, u32[]{:S(2)}, u32[]{:S(2)}) collective-permute-start(f32[256,128]{1,0:T(8,128)S(1)} %get-tuple-element.24), channel_id=1, source_target_pairs={{65,0},{129,64},{193,128},{257,192},{321,256},{385,320},{449,384},... | collective-permute-start | bytes 393224 | tf_op jit(solution)/shard_map/ppermute | solution.py:69
  12.7 9.1 %collective-permute-start = (f32[256,128]{1,0:T(8,128)S(1)}, f32[256,128]{1,0:T(8,128)S(1)}, u32[]{:S(2)}, u32[]{:S(2)}) collective-permute-start(f32[256,128]{1,0:T(8,128)S(1)} %get-tuple-element.21), channel_id=1, source_target_pairs={{0,65},{64,129},{128,193},{192,257},{256,321},{320,385},{384,449},... | collective-permute-start | bytes 393224 | tf_op jit(solution)/shard_map/ppermute | solution.py:69
  21.7 1.9 %collective-permute-start.2 = (f32[256,128]{1,0:T(8,128)S(1)}, f32[256,128]{1,0:T(8,128)S(1)}, u32[]{:S(2)}, u32[]{:S(2)}) collective-permute-start(f32[256,128]{1,0:T(8,128)S(1)} %get-tuple-element.22), channel_id=1, source_target_pairs={{64,1},{128,65},{192,129},{256,193},{320,257},{384,321},{448,385},... | collective-permute-start | bytes 393224 | tf_op jit(solution)/shard_map/ppermute | solution.py:69
  23.7 1.9 %collective-permute-start.6 = (f32[320,128]{1,0:T(8,128)S(1)}, f32[320,128]{1,0:T(8,128)S(1)}, u32[]{:S(2)}, u32[]{:S(2)}) collective-permute-start(f32[320,128]{1,0:T(8,128)S(1)} %pad_maximum_fusion.4), channel_id=1, source_target_pairs={{1,0},{65,64},{129,128},{193,192},{257,256},{321,320},{385,384},{4... | collective-permute-start | bytes 491528 | tf_op jit(solution)/shard_map/ppermute | solution.py:69
  25.8 0.0 collective-permute-done.5
  25.8 6.3 %collective-permute-start.3 = (f32[512,128]{1,0:T(8,128)S(1)}, f32[512,128]{1,0:T(8,128)S(1)}, u32[]{:S(2)}, u32[]{:S(2)}) collective-permute-start(f32[512,128]{1,0:T(8,128)S(1)} %get-tuple-element.19), channel_id=1, source_target_pairs={{0,64},{64,128},{128,192},{192,256},{256,320},{320,384},{384,448},... | collective-permute-start | bytes 786440 | tf_op jit(solution)/shard_map/ppermute | solution.py:69
  32.2 0.0 collective-permute-done.7
  32.2 5.7 %collective-permute-start.1 = (f32[320,128]{1,0:T(8,128)S(1)}, f32[320,128]{1,0:T(8,128)S(1)}, u32[]{:S(2)}, u32[]{:S(2)}) collective-permute-start(f32[320,128]{1,0:T(8,128)S(1)} %pad_maximum_fusion.3), channel_id=1, source_target_pairs={{0,1},{64,65},{128,129},{192,193},{256,257},{320,321},{384,385},{4... | collective-permute-start | bytes 491528 | tf_op jit(solution)/shard_map/ppermute | solution.py:69
  38.0 0.0 collective-permute-done
  38.0 1.9 %collective-permute-start.4 = (f32[512,128]{1,0:T(8,128)S(1)}, f32[512,128]{1,0:T(8,128)S(1)}, u32[]{:S(2)}, u32[]{:S(2)}) collective-permute-start(f32[512,128]{1,0:T(8,128)S(1)} %get-tuple-element.20), channel_id=1, source_target_pairs={{64,0},{128,64},{192,128},{256,192},{320,256},{384,320},{448,384},... | collective-permute-start | bytes 786440 | tf_op jit(solution)/shard_map/ppermute | solution.py:69
  39.9 0.0 collective-permute-done.2
  39.9 0.6 %copy-done.5 = f32[256,128]{1,0:T(8,128)} copy-done((f32[256,128]{1,0:T(8,128)}, f32[256,128]{1,0:T(8,128)S(1)}, u32[]{:S(2)}) %copy-start.5) | copy-done | bytes 131096
  40.6 0.0 collective-permute-done.6
  40.6 0.7 %slice-done.1 = f32[64,128]{1,0:T(8,128)S(1)} async-done(((f32[256,128]{1,0:T(8,128)}), f32[64,128]{1,0:T(8,128)S(1)}, s32[]{:S(2)}) %slice-start.1) | async-done | bytes 32792 | tf_op jit(solution)/shard_map/slice | solution.py:73
  41.3 0.0 slice-done.3
  41.4 0.0 collective-permute-done.1
  41.4 0.6 %copy-done.6 = f32[320,128]{1,0:T(8,128)} copy-done((f32[320,128]{1,0:T(8,128)}, f32[320,128]{1,0:T(8,128)S(1)}, u32[]{:S(2)}) %copy-start.6) | copy-done | bytes 163864
  42.1 0.0 collective-permute-done.3
  42.1 0.0 slice-start.2
  42.1 0.0 slice-start.6
  42.1 0.0 slice-start.8
  42.1 4.7 %collective-permute-done.4 = f32[512,128]{1,0:T(8,128)S(1)} collective-permute-done((f32[512,128]{1,0:T(8,128)S(1)}, f32[512,128]{1,0:T(8,128)S(1)}, u32[]{:S(2)}, u32[]{:S(2)}) %collective-permute-start.4) | collective-permute-done | bytes 262176 | tf_op jit(solution)/shard_map/ppermute | solution.py:69
  47.0 0.0 copy-start.17
  47.0 0.0 copy-start.18
  47.0 0.0 copy-start.19
  47.0 0.1 maximum_maximum_fusion
  47.1 0.6 %copy-done.17 = f32[8,40]{1,0:T(8,128)S(1)} copy-done((f32[8,40]{1,0:T(8,128)S(1)}, f32[8,40]{1,0:T(8,128)}, u32[]{:S(2)}) %copy-start.17) | copy-done | bytes 1304
  47.6 0.0 copy-done.18
  47.7 0.0 copy-done.19
  47.7 0.8 %fusion = f32[8,48,128]{2,0,1:T(8,128)S(1)} fusion(f32[40,48,128]{2,1,0:T(8,128)S(1)} %maximum_maximum_fusion, f32[8,40]{1,0:T(8,128)S(1)} %copy-done.19, f32[8,40]{1,0:T(8,128)S(1)} %copy-done.17, f32[8,40]{1,0:T(8,128)S(1)} %copy-done.18, pred[]{:T(512)S(6)} %eq.13, pred[]{:T(512)S(6)} %eq.12), kind=kOutput, calls=%fused_computation.3 | convolution fusion | flops 23593600 | bytes 1183490 | tf_op jit(solution)/shard_map/kx,xyz->kyz/dot_general | solution.py:127
  48.5 0.0 slice-start
  48.5 0.2 convolution_bitcast_fusion.1
  48.8 0.1 reshape.122
  48.9 0.6 %slice_bitcast_fusion = f32[4,4,64]{2,1,0:T(4,128)} fusion(f32[8,4,4,64]{3,2,1,0:T(4,128)S(1)} %bitcast.92), kind=kLoop, calls=%fused_computation.22 | loop fusion | bytes 8192 | tf_op jit(solution)/shard_map/squeeze | solution.py:137
  49.5 0.6 %slice.164 = f32[7,4,4,64]{3,2,1,0:T(4,128)} slice(f32[8,4,4,64]{3,2,1,0:T(4,128)S(1)} %bitcast.93), slice={[1:8], [0:4], [0:4], [0:64]} | slice | bytes 57344 | tf_op jit(solution)/shard_map/slice | solution.py:137
  50.2 0.1 slice-done.5
  50.3 0.0 slice-done.7
  50.3 0.1 pad_maximum_fusion
  50.4 0.6 %copy-done.11 = f32[16,24]{1,0:T(8,128)S(1)} copy-done((f32[16,24]{1,0:T(8,128)S(1)}, f32[16,24]{1,0:T(8,128)}, u32[]{:S(2)}) %copy-start.11) | copy-done | bytes 1560
  51.0 0.0 copy-done.12
  51.0 0.0 copy-done.13
  51.1 1.0 %fusion.2 = f32[16,2,32,128]{3,0,2,1:T(8,128)S(1)} fusion(f32[24,2,32,128]{3,2,0,1:T(8,128)S(1)} %pad_maximum_fusion, f32[16,24]{1,0:T(8,128)S(1)} %copy-done.13, f32[16,24]{1,0:T(8,128)S(1)} %copy-done.11, f32[16,24]{1,0:T(8,128)S(1)} %copy-done.12, pred[]{:T(512)S(6)} %eq.13, pred[]{:T(512)S(6)} %eq.12), kind=kOutput, calls=%fused_computation.6 | convolution fusion | flops 37749504 | bytes 1315330 | tf_op jit(solution)/shard_map/kx,xbyz->kbyz/dot_general | solution.py:126
  52.1 0.5 %fusion.4 = f32[16,2,128,16]{2,3,1,0:T(8,128)S(1)} fusion(f32[16,2,32,128]{3,0,2,1:T(8,128)S(1)} %fusion.2, f32[16,32]{1,0:T(8,128)S(1)} %copy-done.10, f32[16,32]{1,0:T(8,128)S(1)} %copy-done.8, f32[16,32]{1,0:T(8,128)S(1)} %copy-done.9, pred[]{:T(512)S(6)} %eq.15, pred[]{:T(512)S(6)} %eq.14), kind=kOutput, calls=%fused_computation.8 | convolution fusion | flops 25166848 | bytes 792578 | tf_op jit(solution)/shard_map/ky,abyz->abkz/dot_general | solution.py:128
  52.7 0.7 %slice.174 = f32[7,8,8,128]{3,2,1,0:T(8,128)} slice(f32[8,8,8,128]{3,2,1,0:T(8,128)S(1)} %bitcast.67), slice={[1:8], [0:8], [0:8], [0:128]} | slice | bytes 458752 | tf_op jit(solution)/shard_map/slice | solution.py:137
  (67 shorter events, 0.4 us)
Async XLA Ops:
  0.6 1.0 %copy-start = (f32[16,16,256]{2,1,0:T(8,128)S(1)}, f32[16,16,256]{2,1,0:T(8,128)}, u32[]{:S(2)}) copy-start(f32[16,16,256]{2,1,0:T(8,128)} %param.14) | copy-start | bytes 786436
  3.2 34.7 %copy-start.1 = (f32[16,3,16,128]{3,2,0,1:T(8,128)}, f32[16,3,16,128]{3,2,0,1:T(8,128)S(1)}, u32[]{:S(2)}) copy-start(f32[16,3,16,128]{3,2,0,1:T(8,128)S(1)} %convolution_bitcast_fusion) | copy-start | bytes 1179652
  3.3 22.5 %collective-permute-start.5 = (f32[256,128]{1,0:T(8,128)S(1)}, f32[256,128]{1,0:T(8,128)S(1)}, u32[]{:S(2)}, u32[]{:S(2)}) collective-permute-start(f32[256,128]{1,0:T(8,128)S(1)} %get-tuple-element.23), channel_id=1, source_target_pairs={{1,64},{65,128},{129,192},{193,256},{257,320},{321,384},{385,448},... | collective-permute-start | bytes 393224 | tf_op jit(solution)/shard_map/ppermute | solution.py:69
  10.7 21.5 %collective-permute-start.7 = (f32[256,128]{1,0:T(8,128)S(1)}, f32[256,128]{1,0:T(8,128)S(1)}, u32[]{:S(2)}, u32[]{:S(2)}) collective-permute-start(f32[256,128]{1,0:T(8,128)S(1)} %get-tuple-element.24), channel_id=1, source_target_pairs={{65,0},{129,64},{193,128},{257,192},{321,256},{385,320},{449,384},... | collective-permute-start | bytes 393224 | tf_op jit(solution)/shard_map/ppermute | solution.py:69
  12.7 25.3 %collective-permute-start = (f32[256,128]{1,0:T(8,128)S(1)}, f32[256,128]{1,0:T(8,128)S(1)}, u32[]{:S(2)}, u32[]{:S(2)}) collective-permute-start(f32[256,128]{1,0:T(8,128)S(1)} %get-tuple-element.21), channel_id=1, source_target_pairs={{0,65},{64,129},{128,193},{192,257},{256,321},{320,385},{384,449},... | collective-permute-start | bytes 393224 | tf_op jit(solution)/shard_map/ppermute | solution.py:69
  21.7 18.2 %collective-permute-start.2 = (f32[256,128]{1,0:T(8,128)S(1)}, f32[256,128]{1,0:T(8,128)S(1)}, u32[]{:S(2)}, u32[]{:S(2)}) collective-permute-start(f32[256,128]{1,0:T(8,128)S(1)} %get-tuple-element.22), channel_id=1, source_target_pairs={{64,1},{128,65},{192,129},{256,193},{320,257},{384,321},{448,385},... | collective-permute-start | bytes 393224 | tf_op jit(solution)/shard_map/ppermute | solution.py:69
  23.7 16.9 %collective-permute-start.6 = (f32[320,128]{1,0:T(8,128)S(1)}, f32[320,128]{1,0:T(8,128)S(1)}, u32[]{:S(2)}, u32[]{:S(2)}) collective-permute-start(f32[320,128]{1,0:T(8,128)S(1)} %pad_maximum_fusion.4), channel_id=1, source_target_pairs={{1,0},{65,64},{129,128},{193,192},{257,256},{321,320},{385,384},{4... | collective-permute-start | bytes 491528 | tf_op jit(solution)/shard_map/ppermute | solution.py:69
  25.8 12.1 %copy-start.2 = (f32[256,128]{1,0:T(8,128)}, f32[256,128]{1,0:T(8,128)S(1)}, u32[]{:S(2)}) copy-start(f32[256,128]{1,0:T(8,128)S(1)} %collective-permute-done.5) | copy-start | bytes 393220
  25.8 16.2 %collective-permute-start.3 = (f32[512,128]{1,0:T(8,128)S(1)}, f32[512,128]{1,0:T(8,128)S(1)}, u32[]{:S(2)}, u32[]{:S(2)}) collective-permute-start(f32[512,128]{1,0:T(8,128)S(1)} %get-tuple-element.19), channel_id=1, source_target_pairs={{0,64},{64,128},{128,192},{192,256},{256,320},{320,384},{384,448},... | collective-permute-start | bytes 786440 | tf_op jit(solution)/shard_map/ppermute | solution.py:69
  32.2 5.8 %copy-start.3 = (f32[256,128]{1,0:T(8,128)}, f32[256,128]{1,0:T(8,128)S(1)}, u32[]{:S(2)}) copy-start(f32[256,128]{1,0:T(8,128)S(1)} %collective-permute-done.7) | copy-start | bytes 393220
  32.2 9.2 %collective-permute-start.1 = (f32[320,128]{1,0:T(8,128)S(1)}, f32[320,128]{1,0:T(8,128)S(1)}, u32[]{:S(2)}, u32[]{:S(2)}) collective-permute-start(f32[320,128]{1,0:T(8,128)S(1)} %pad_maximum_fusion.3), channel_id=1, source_target_pairs={{0,1},{64,65},{128,129},{192,193},{256,257},{320,321},{384,385},{4... | collective-permute-start | bytes 491528 | tf_op jit(solution)/shard_map/ppermute | solution.py:69
  38.0 1.9 %copy-start.4 = (f32[256,128]{1,0:T(8,128)}, f32[256,128]{1,0:T(8,128)S(1)}, u32[]{:S(2)}) copy-start(f32[256,128]{1,0:T(8,128)S(1)} %collective-permute-done) | copy-start | bytes 393220
  38.0 8.9 %collective-permute-start.4 = (f32[512,128]{1,0:T(8,128)S(1)}, f32[512,128]{1,0:T(8,128)S(1)}, u32[]{:S(2)}, u32[]{:S(2)}) collective-permute-start(f32[512,128]{1,0:T(8,128)S(1)} %get-tuple-element.20), channel_id=1, source_target_pairs={{64,0},{128,64},{192,128},{256,192},{320,256},{384,320},{448,384},... | collective-permute-start | bytes 786440 | tf_op jit(solution)/shard_map/ppermute | solution.py:69
  39.9 0.6 %copy-start.5 = (f32[256,128]{1,0:T(8,128)}, f32[256,128]{1,0:T(8,128)S(1)}, u32[]{:S(2)}) copy-start(f32[256,128]{1,0:T(8,128)S(1)} %collective-permute-done.2) | copy-start | bytes 393220
  40.6 0.8 %slice-start.1 = ((f32[256,128]{1,0:T(8,128)}), f32[64,128]{1,0:T(8,128)S(1)}, s32[]{:S(2)}) async-start(f32[256,128]{1,0:T(8,128)} %copy-done.2), calls=%async_computation.1 | async-start | bytes 65536 | tf_op jit(solution)/shard_map/slice | solution.py:73
  40.6 0.8 %slice-start.3 = ((f32[256,128]{1,0:T(8,128)}), f32[64,128]{1,0:T(8,128)S(1)}, s32[]{:S(2)}) async-start(f32[256,128]{1,0:T(8,128)} %copy-done.3), calls=%async_computation.3 | async-start | bytes 65536 | tf_op jit(solution)/shard_map/slice | solution.py:73
  40.6 0.8 %copy-start.7 = (f32[320,128]{1,0:T(8,128)}, f32[320,128]{1,0:T(8,128)S(1)}, u32[]{:S(2)}) copy-start(f32[320,128]{1,0:T(8,128)S(1)} %collective-permute-done.6) | copy-start | bytes 491524
  41.4 0.7 %copy-start.6 = (f32[320,128]{1,0:T(8,128)}, f32[320,128]{1,0:T(8,128)S(1)}, u32[]{:S(2)}) copy-start(f32[320,128]{1,0:T(8,128)S(1)} %collective-permute-done.1) | copy-start | bytes 491524
  42.1 4.8 %slice-start.11 = ((f32[320,128]{1,0:T(8,128)}), f32[192,128]{1,0:T(8,128)S(1)}, s32[]{:S(2)}) async-start(f32[320,128]{1,0:T(8,128)} %copy-done.7), calls=%async_computation.11 | async-start | bytes 196608 | tf_op jit(solution)/shard_map/slice | solution.py:73
  42.1 4.8 %slice-start.2 = ((f32[256,128]{1,0:T(8,128)}), f32[192,128]{1,0:T(8,128)S(1)}, s32[]{:S(2)}) async-start(f32[256,128]{1,0:T(8,128)} %copy-done.2), calls=%async_computation.2 | async-start | bytes 196608 | tf_op jit(solution)/shard_map/slice | solution.py:73
  42.1 4.8 %slice-start.4 = ((f32[256,128]{1,0:T(8,128)}), f32[192,128]{1,0:T(8,128)S(1)}, s32[]{:S(2)}) async-start(f32[256,128]{1,0:T(8,128)} %copy-done.3), calls=%async_computation.4 | async-start | bytes 196608 | tf_op jit(solution)/shard_map/slice | solution.py:73
  42.1 4.8 %slice-start.6 = ((f32[256,128]{1,0:T(8,128)}), f32[192,128]{1,0:T(8,128)S(1)}, s32[]{:S(2)}) async-start(f32[256,128]{1,0:T(8,128)} %copy-done.4), calls=%async_computation.6 | async-start | bytes 196608 | tf_op jit(solution)/shard_map/slice | solution.py:73
  42.1 4.8 %slice-start.8 = ((f32[256,128]{1,0:T(8,128)}), f32[192,128]{1,0:T(8,128)S(1)}, s32[]{:S(2)}) async-start(f32[256,128]{1,0:T(8,128)} %copy-done.5), calls=%async_computation.8 | async-start | bytes 196608 | tf_op jit(solution)/shard_map/slice | solution.py:73
  42.1 4.8 %slice-start.10 = ((f32[320,128]{1,0:T(8,128)}), f32[192,128]{1,0:T(8,128)S(1)}, s32[]{:S(2)}) async-start(f32[320,128]{1,0:T(8,128)} %copy-done.6), calls=%async_computation.10 | async-start | bytes 196608 | tf_op jit(solution)/shard_map/slice | solution.py:73
  47.0 0.7 %copy-start.17 = (f32[8,40]{1,0:T(8,128)S(1)}, f32[8,40]{1,0:T(8,128)}, u32[]{:S(2)}) copy-start(f32[8,40]{1,0:T(8,128)} %constant.47.clone) | copy-start | bytes 3844
  47.0 0.7 %copy-start.18 = (f32[8,40]{1,0:T(8,128)S(1)}, f32[8,40]{1,0:T(8,128)}, u32[]{:S(2)}) copy-start(f32[8,40]{1,0:T(8,128)} %constant.46.clone) | copy-start | bytes 3844
  47.0 0.7 %copy-start.19 = (f32[8,40]{1,0:T(8,128)S(1)}, f32[8,40]{1,0:T(8,128)}, u32[]{:S(2)}) copy-start(f32[8,40]{1,0:T(8,128)} %constant.45.clone) | copy-start | bytes 3844
  47.7 0.8 %copy-start.14 = (f32[8,48]{1,0:T(8,128)S(1)}, f32[8,48]{1,0:T(8,128)}, u32[]{:S(2)}) copy-start(f32[8,48]{1,0:T(8,128)} %constant.53.clone) | copy-start | bytes 4612
  47.7 0.8 %copy-start.15 = (f32[8,48]{1,0:T(8,128)S(1)}, f32[8,48]{1,0:T(8,128)}, u32[]{:S(2)}) copy-start(f32[8,48]{1,0:T(8,128)} %constant.52.clone) | copy-start | bytes 4612
  47.7 0.8 %copy-start.16 = (f32[8,48]{1,0:T(8,128)S(1)}, f32[8,48]{1,0:T(8,128)}, u32[]{:S(2)}) copy-start(f32[8,48]{1,0:T(8,128)} %constant.51.clone) | copy-start | bytes 4612
  48.5 1.6 %slice-start = ((f32[16,3,16,128]{3,2,0,1:T(8,128)}), f32[16,2,16,128]{3,2,0,1:T(8,128)S(1)}, s32[]{:S(2)}) async-start(f32[16,3,16,128]{3,2,0,1:T(8,128)} %copy-done.1), calls=%async_computation | async-start | bytes 524288 | tf_op jit(solution)/shard_map/slice | solution.py:107
  48.9 1.3 %slice-start.9 = ((f32[320,128]{1,0:T(8,128)}), f32[128,128]{1,0:T(8,128)S(1)}, s32[]{:S(2)}) async-start(f32[320,128]{1,0:T(8,128)} %copy-done.6), calls=%async_computation.9 | async-start | bytes 131072 | tf_op jit(solution)/shard_map/slice | solution.py:73
  49.5 0.8 %slice-start.5 = ((f32[256,128]{1,0:T(8,128)}), f32[64,128]{1,0:T(8,128)S(1)}, s32[]{:S(2)}) async-start(f32[256,128]{1,0:T(8,128)} %copy-done.4), calls=%async_computation.5 | async-start | bytes 65536 | tf_op jit(solution)/shard_map/slice | solution.py:73
  49.5 0.8 %slice-start.7 = ((f32[256,128]{1,0:T(8,128)}), f32[64,128]{1,0:T(8,128)S(1)}, s32[]{:S(2)}) async-start(f32[256,128]{1,0:T(8,128)} %copy-done.5), calls=%async_computation.7 | async-start | bytes 65536 | tf_op jit(solution)/shard_map/slice | solution.py:73
  50.3 0.7 %copy-start.11 = (f32[16,24]{1,0:T(8,128)S(1)}, f32[16,24]{1,0:T(8,128)}, u32[]{:S(2)}) copy-start(f32[16,24]{1,0:T(8,128)} %constant.44.clone) | copy-start | bytes 4612
  50.3 0.7 %copy-start.12 = (f32[16,24]{1,0:T(8,128)S(1)}, f32[16,24]{1,0:T(8,128)}, u32[]{:S(2)}) copy-start(f32[16,24]{1,0:T(8,128)} %constant.43.clone) | copy-start | bytes 4612
  50.3 0.7 %copy-start.13 = (f32[16,24]{1,0:T(8,128)S(1)}, f32[16,24]{1,0:T(8,128)}, u32[]{:S(2)}) copy-start(f32[16,24]{1,0:T(8,128)} %constant.42.clone) | copy-start | bytes 4612
  51.1 1.0 %copy-start.8 = (f32[16,32]{1,0:T(8,128)S(1)}, f32[16,32]{1,0:T(8,128)}, u32[]{:S(2)}) copy-start(f32[16,32]{1,0:T(8,128)} %constant.50.clone) | copy-start | bytes 6148
  51.1 1.0 %copy-start.9 = (f32[16,32]{1,0:T(8,128)S(1)}, f32[16,32]{1,0:T(8,128)}, u32[]{:S(2)}) copy-start(f32[16,32]{1,0:T(8,128)} %constant.49.clone) | copy-start | bytes 6148
  51.1 1.0 %copy-start.10 = (f32[16,32]{1,0:T(8,128)S(1)}, f32[16,32]{1,0:T(8,128)}, u32[]{:S(2)}) copy-start(f32[16,32]{1,0:T(8,128)} %constant.48.clone) | copy-start | bytes 6148

commit v4 on v2

--- a/solution.py
+++ b/solution.py
@@ -46,9 +46,30 @@
     return maps
 
 
-def chosen(maps, at_low, at_high):
-    low, inside, high = (jnp.asarray(m) for m in maps)
-    return jnp.where(at_low, low, jnp.where(at_high, high, inside))
+def packed_maps(block):
+    parts = [
+        window_maps(block, (4, 4), 0),
+        window_maps(block, (12, 12), 1),
+        window_maps(block, (8, 8), 0),
+        window_maps(block, (block, block), 1),
+    ]
+    height = sum(p[0].shape[0] for p in parts)
+    width = -(-max(p[0].shape[1] for p in parts) // 128) * 128
+    table = np.zeros((3, height, width), np.float32)
+    places, row = [], 0
+    for p in parts:
+        rows, cols = p[0].shape
+        for case in range(3):
+            table[case, row : row + rows, :cols] = p[case]
+        places.append((row, rows, cols))
+        row += rows
+    return table, places
+
+
+def case_of(axis):
+    index = lax.axis_index(axis)
+    last = lax.axis_size(axis) - 1
+    return jnp.where(index == 0, 0, jnp.where(index == last, 2, 1))
 
 
 def exchange(lower_half, upper_half, axis):
@@ -62,10 +83,6 @@
 
 def per_device(velocity):
     nx, ny, nz = velocity.shape
-    slab_low = lax.axis_index("slab") == 0
-    slab_high = lax.axis_index("slab") == lax.axis_size("slab") - 1
-    brick_low = lax.axis_index("morton") == 0
-    brick_high = lax.axis_index("morton") == lax.axis_size("morton") - 1
 
     (z_low, z_high), (z2_low, z2_high) = level_maps(nz)
     z_maps = np.stack([z_low.T, z_high.T, np.concatenate([z2_low, z2_high]).T]).astype(np.float32)
@@ -86,8 +103,13 @@
     two_ext = jnp.concatenate(
         [below[split:].reshape(wide, ny, lanes), two_rows, above[split:].reshape(wide, ny, lanes)]
     )
-    a1x = chosen(window_maps(nx, (4, 4), 0), slab_low, slab_high)
-    a2x = chosen(window_maps(nx, (wide, wide), 1), slab_low, slab_high)
+    assert nx == ny and wide == 12
+    table, places = packed_maps(nx)
+    table = jnp.asarray(table)
+    x_maps = lax.dynamic_index_in_dim(table, case_of("slab"), keepdims=False)
+    y_maps = lax.dynamic_index_in_dim(table, case_of("morton"), keepdims=False)
+    pick = lambda maps, i: maps[places[i][0] : places[i][0] + places[i][1], : places[i][2]]
+    a1x, a2x = pick(x_maps, 0), pick(x_maps, 1)
     x_one = jnp.einsum("kx,xbyz->kbyz", a1x, one_ext, precision=EXACT)
     x_two = jnp.einsum("kx,xyz->kyz", a2x, two_ext, precision=EXACT)
 
@@ -109,8 +131,7 @@
         [below[split:].reshape(kx2, ny, lanes), x_two, above[split:].reshape(kx2, ny, lanes)],
         axis=1,
     )
-    a1y = chosen(window_maps(ny, (narrow, narrow), 0), brick_low, brick_high)
-    a2y = chosen(window_maps(ny, (ny, ny), 1), brick_low, brick_high)
+    a1y, a2y = pick(y_maps, 2), pick(y_maps, 3)
     y_one = jnp.einsum("ky,abyz->abkz", a1y, one_ext, precision=EXACT)
     y_two = jnp.einsum("ky,ayz->akz", a2y, two_ext, precision=EXACT)
 

time: 43.7 us -> 41.6 us (0.952)
  waiting for transfers between devices: 14.2 us -> 12.7 us
    unnamed x30 -> x8, local copies, waits for them, and re-layouts: 3.65 us -> 2.48 us
    slice x1 -> x2, local copies, waits for them, and re-layouts: 0.01 us -> 0.88 us  [per_device(): above[split:].reshape(wide, ny, lanes)]
    ppermute x2, waiting for transfers between devices: 6.42 us -> 5.58 us  [exchange(): from_above = lax.ppermute(lower_half, axis, down)]
    ppermute x2, waiting for transfers between devices: 7.8 us -> 7.11 us  [exchange(): from_below = lax.ppermute(upper_half, axis, up)]
  transfers between devices with their start and end apart: 4 -> 4, of which waited for: 4 -> 3; matrix products, arithmetic and copies ran while one was open for 0% -> 0% of each run, Pallas kernels for 0% -> 0%
where the time goes in v4:
time: 41.6 us; the launch traced here: 41.2 us
  starting transfers between devices  17.6 us (42%)
  waiting for transfers between devices  12.7 us (31%)
  local copies, waits for them, and re-layouts  6.63 us (16%)
  matrix products  3.22 us (8%)
  between operations  0.95 us (2%)
    ppermute x2, starting transfers between devices, exchange(): from_below = lax.ppermute(upper_half, axis, up)  9.78 us
    ppermute x2, starting transfers between devices, exchange(): from_above = lax.ppermute(lower_half, axis, down)  7.79 us
    ppermute x2, waiting for transfers between devices, exchange(): from_below = lax.ppermute(upper_half, axis, up)  7.11 us
    ppermute x2, waiting for transfers between devices, exchange(): from_above = lax.ppermute(lower_half, axis, down)  5.58 us
    unnamed x8, local copies, waits for them, and re-layouts  2.48 us
    dot_general x1, matrix products, per_device(): jnp.einsum('xyz,bzk->xbyk', velocity, jnp.asarray(z_maps), precision=EXACT)  1.62 us
    slice x2, local copies, waits for them, and re-layouts, per_device(): return (level_two[0], level_two[1:], level_one[1:])  1.33 us
    slice x2, local copies, waits for them, and re-layouts, per_device(): above[split:].reshape(wide, ny, lanes)  0.88 us
  transfers between devices with their start and end apart: 4, of which 3 were waited for; matrix products, arithmetic and copies ran while one was open for 0% of the time, Pallas kernels for 0%

profile of v4, /device:TPU:393, one launch (start us, length us, event | category | flops | bytes accessed | tf_op | source)
XLA Modules:
  0.0 41.2 jit_solution(5634665055192776128)
XLA Ops:
  0.6 0.0 copy-start
  0.6 0.9 %copy-done = f32[16,16,256]{2,1,0:T(8,128)S(1)} copy-done((f32[16,16,256]{2,1,0:T(8,128)S(1)}, f32[16,16,256]{2,1,0:T(8,128)}, u32[]{:S(2)}) %copy-start) | copy-done | bytes 262168
  1.6 1.6 %convolution_bitcast_fusion = f32[16,3,16,128]{3,2,0,1:T(8,128)S(1)} fusion(f32[3,256,128,1]{2,1,3,0:T(8,128)} %constant.34, f32[16,16,256]{2,1,0:T(8,128)S(1)} %copy-done), kind=kOutput, calls=%fused_computation | convolution fusion | flops 301989888 | bytes 1048576 | tf_op jit(solution)/shard_map/xyz,bzk->xbyk/dot_general | solution.py:90
  3.2 0.0 copy-start.1
  3.3 5.9 %collective-permute-start.1 = (f32[320,128]{1,0:T(8,128)S(1)}, f32[320,128]{1,0:T(8,128)S(1)}, u32[]{:S(2)}, u32[]{:S(2)}) collective-permute-start(f32[320,128]{1,0:T(8,128)S(1)} %pad_maximum_fusion.7), channel_id=1, source_target_pairs={{1,0},{2,1},{3,2},{4,3},{5,4},{6,5},{7,6},{8,7},{9,8},{10,9},{11,1... | collective-permute-start | bytes 491528 | tf_op jit(solution)/shard_map/ppermute | solution.py:80
  9.2 1.9 %collective-permute-start = (f32[320,128]{1,0:T(8,128)S(1)}, f32[320,128]{1,0:T(8,128)S(1)}, u32[]{:S(2)}, u32[]{:S(2)}) collective-permute-start(f32[320,128]{1,0:T(8,128)S(1)} %pad_maximum_fusion.6), channel_id=1, source_target_pairs={{0,1},{1,2},{2,3},{3,4},{4,5},{5,6},{6,7},{7,8},{8,9},{9,10},{10,1... | collective-permute-start | bytes 491528 | tf_op jit(solution)/shard_map/ppermute | solution.py:79
  11.2 0.0 copy-done.1
  11.2 0.0 copy-start.3
  11.2 0.9 %copy-done.3 = f32[3,48,128]{2,1,0:T(8,128)S(1)} copy-done((f32[3,48,128]{2,1,0:T(8,128)S(1)}, f32[3,48,128]{2,1,0:T(8,128)}, u32[]{:S(2)}) %copy-start.3) | copy-done | bytes 73752
  12.1 0.0 collective-permute-done.1
  12.1 0.0 copy-start.2
  12.1 0.7 %copy-done.2 = f32[320,128]{1,0:T(8,128)} copy-done((f32[320,128]{1,0:T(8,128)}, f32[320,128]{1,0:T(8,128)S(1)}, u32[]{:S(2)}) %copy-start.2) | copy-done | bytes 163864
  12.7 6.4 %collective-permute-done = f32[320,128]{1,0:T(8,128)S(1)} collective-permute-done((f32[320,128]{1,0:T(8,128)S(1)}, f32[320,128]{1,0:T(8,128)S(1)}, u32[]{:S(2)}, u32[]{:S(2)}) %collective-permute-start) | collective-permute-done | bytes 163872 | tf_op jit(solution)/shard_map/ppermute | solution.py:79
  19.2 0.0 slice-start.1
  19.2 0.9 %slice-done.1 = f32[192,128]{1,0:T(8,128)S(1)} async-done(((f32[320,128]{1,0:T(8,128)}), f32[192,128]{1,0:T(8,128)S(1)}, s32[]{:S(2)}) %slice-start.1) | async-done | bytes 98328 | tf_op jit(solution)/shard_map/slice | solution.py:104
  20.1 0.0 slice-start
  20.1 0.4 fusion.4
  20.5 0.0 slice-start.2
  20.5 0.6 %slice-done = f32[16,2,16,128]{3,2,0,1:T(8,128)S(1)} async-done(((f32[16,3,16,128]{3,2,0,1:T(8,128)}), f32[16,2,16,128]{3,2,0,1:T(8,128)S(1)}, s32[]{:S(2)}) %slice-start) | async-done | bytes 262168 | tf_op jit(solution)/shard_map/slice | solution.py:93
  21.0 0.3 slice-done.2
  21.4 0.5 %fusion.2 = f32[16,2,16,128]{3,0,2,1:T(8,128)S(1)} fusion(f32[24,2,16,128]{3,2,0,1:T(8,128)S(1)} %pad_maximum_fusion.1, f32[48,128]{1,0:T(8,128)S(1)} %get-tuple-element.10), kind=kOutput, calls=%fused_computation.6 | convolution fusion | flops 18874368 | bytes 663552 | tf_op jit(solution)/shard_map/kx,xbyz->kbyz/dot_general | solution.py:113
  22.0 7.9 %collective-permute-start.2 = (f32[384,128]{1,0:T(8,128)S(1)}, f32[384,128]{1,0:T(8,128)S(1)}, u32[]{:S(2)}, u32[]{:S(2)}) collective-permute-start(f32[384,128]{1,0:T(8,128)S(1)} %get-tuple-element.11), channel_id=1, source_target_pairs={{0,64},{64,128},{128,192},{192,256},{256,320},{320,384},{384,448},... | collective-permute-start | bytes 589832 | tf_op jit(solution)/shard_map/ppermute | solution.py:79
  29.9 1.9 %collective-permute-start.3 = (f32[384,128]{1,0:T(8,128)S(1)}, f32[384,128]{1,0:T(8,128)S(1)}, u32[]{:S(2)}, u32[]{:S(2)}) collective-permute-start(f32[384,128]{1,0:T(8,128)S(1)} %get-tuple-element.12), channel_id=1, source_target_pairs={{64,0},{128,64},{192,128},{256,192},{320,256},{384,320},{448,384},... | collective-permute-start | bytes 589832 | tf_op jit(solution)/shard_map/ppermute | solution.py:80
  31.8 0.7 %collective-permute-done.2 = f32[384,128]{1,0:T(8,128)S(1)} collective-permute-done((f32[384,128]{1,0:T(8,128)S(1)}, f32[384,128]{1,0:T(8,128)S(1)}, u32[]{:S(2)}, u32[]{:S(2)}) %collective-permute-start.2) | collective-permute-done | bytes 196640 | tf_op jit(solution)/shard_map/ppermute | solution.py:79
  32.5 5.6 %collective-permute-done.3 = f32[384,128]{1,0:T(8,128)S(1)} collective-permute-done((f32[384,128]{1,0:T(8,128)S(1)}, f32[384,128]{1,0:T(8,128)S(1)}, u32[]{:S(2)}, u32[]{:S(2)}) %collective-permute-start.3) | collective-permute-done | bytes 196640 | tf_op jit(solution)/shard_map/ppermute | solution.py:80
  38.2 0.2 convolution_bitcast_fusion.1
  38.4 0.1 reshape.81
  38.5 0.6 %slice_bitcast_fusion.3 = f32[4,4,64]{2,1,0:T(4,128)} fusion(f32[8,4,4,64]{3,2,1,0:T(4,128)S(1)} %bitcast.72), kind=kLoop, calls=%fused_computation.22 | loop fusion | bytes 8192 | tf_op jit(solution)/shard_map/squeeze | solution.py:144
  39.1 0.6 %slice.116 = f32[7,4,4,64]{3,2,1,0:T(4,128)} slice(f32[8,4,4,64]{3,2,1,0:T(4,128)S(1)} %bitcast.73), slice={[1:8], [0:4], [0:4], [0:64]} | slice | bytes 57344 | tf_op jit(solution)/shard_map/slice | solution.py:144
  39.9 0.5 %fusion = f32[16,2,128,16]{2,3,1,0:T(8,128)S(1)} fusion(f32[16,2,32,128]{3,0,2,1:T(8,128)S(1)} %pad_maximum_fusion, f32[48,128]{1,0:T(8,128)S(1)} %get-tuple-element.9), kind=kOutput, calls=%fused_computation.3 | convolution fusion | flops 25165824 | bytes 794624 | tf_op jit(solution)/shard_map/ky,abyz->abkz/dot_general | solution.py:135
  40.5 0.7 %slice.120 = f32[7,8,8,128]{3,2,1,0:T(8,128)} slice(f32[8,8,8,128]{3,2,1,0:T(8,128)S(1)} %bitcast.59), slice={[1:8], [0:8], [0:8], [0:128]} | slice | bytes 458752 | tf_op jit(solution)/shard_map/slice | solution.py:144
  (29 shorter events, 0.6 us)
Async XLA Ops:
  0.6 1.0 %copy-start = (f32[16,16,256]{2,1,0:T(8,128)S(1)}, f32[16,16,256]{2,1,0:T(8,128)}, u32[]{:S(2)}) copy-start(f32[16,16,256]{2,1,0:T(8,128)} %param.3) | copy-start | bytes 786436
  3.2 7.9 %copy-start.1 = (f32[16,3,16,128]{3,2,0,1:T(8,128)}, f32[16,3,16,128]{3,2,0,1:T(8,128)S(1)}, u32[]{:S(2)}) copy-start(f32[16,3,16,128]{3,2,0,1:T(8,128)S(1)} %convolution_bitcast_fusion) | copy-start | bytes 1179652
  3.3 8.8 %collective-permute-start.1 = (f32[320,128]{1,0:T(8,128)S(1)}, f32[320,128]{1,0:T(8,128)S(1)}, u32[]{:S(2)}, u32[]{:S(2)}) collective-permute-start(f32[320,128]{1,0:T(8,128)S(1)} %pad_maximum_fusion.7), channel_id=1, source_target_pairs={{1,0},{2,1},{3,2},{4,3},{5,4},{6,5},{7,6},{8,7},{9,8},{10,9},{11,1... | collective-permute-start | bytes 491528 | tf_op jit(solution)/shard_map/ppermute | solution.py:80
  9.2 10.0 %collective-permute-start = (f32[320,128]{1,0:T(8,128)S(1)}, f32[320,128]{1,0:T(8,128)S(1)}, u32[]{:S(2)}, u32[]{:S(2)}) collective-permute-start(f32[320,128]{1,0:T(8,128)S(1)} %pad_maximum_fusion.6), channel_id=1, source_target_pairs={{0,1},{1,2},{2,3},{3,4},{4,5},{5,6},{6,7},{7,8},{8,9},{9,10},{10,1... | collective-permute-start | bytes 491528 | tf_op jit(solution)/shard_map/ppermute | solution.py:79
  11.2 0.9 %copy-start.3 = (f32[3,48,128]{2,1,0:T(8,128)S(1)}, f32[3,48,128]{2,1,0:T(8,128)}, u32[]{:S(2)}) copy-start(f32[3,48,128]{2,1,0:T(8,128)} %constant.32.clone) | copy-start | bytes 221188
  12.1 0.7 %copy-start.2 = (f32[320,128]{1,0:T(8,128)}, f32[320,128]{1,0:T(8,128)S(1)}, u32[]{:S(2)}) copy-start(f32[320,128]{1,0:T(8,128)S(1)} %collective-permute-done.1) | copy-start | bytes 491524
  19.2 0.9 %slice-start.1 = ((f32[320,128]{1,0:T(8,128)}), f32[192,128]{1,0:T(8,128)S(1)}, s32[]{:S(2)}) async-start(f32[320,128]{1,0:T(8,128)} %copy-done.2), calls=%async_computation.1 | async-start | bytes 196608 | tf_op jit(solution)/shard_map/slice | solution.py:104
  20.1 1.0 %slice-start = ((f32[16,3,16,128]{3,2,0,1:T(8,128)}), f32[16,2,16,128]{3,2,0,1:T(8,128)S(1)}, s32[]{:S(2)}) async-start(f32[16,3,16,128]{3,2,0,1:T(8,128)} %copy-done.1), calls=%async_computation | async-start | bytes 524288 | tf_op jit(solution)/shard_map/slice | solution.py:93
  20.5 0.9 %slice-start.2 = ((f32[320,128]{1,0:T(8,128)}), f32[128,128]{1,0:T(8,128)S(1)}, s32[]{:S(2)}) async-start(f32[320,128]{1,0:T(8,128)} %copy-done.2), calls=%async_computation.2 | async-start | bytes 131072 | tf_op jit(solution)/shard_map/slice | solution.py:101
  22.0 10.5 %collective-permute-start.2 = (f32[384,128]{1,0:T(8,128)S(1)}, f32[384,128]{1,0:T(8,128)S(1)}, u32[]{:S(2)}, u32[]{:S(2)}) collective-permute-start(f32[384,128]{1,0:T(8,128)S(1)} %get-tuple-element.11), channel_id=1, source_target_pairs={{0,64},{64,128},{128,192},{192,256},{256,320},{320,384},{384,448},... | collective-permute-start | bytes 589832 | tf_op jit(solution)/shard_map/ppermute | solution.py:79
  29.9 8.2 %collective-permute-start.3 = (f32[384,128]{1,0:T(8,128)S(1)}, f32[384,128]{1,0:T(8,128)S(1)}, u32[]{:S(2)}, u32[]{:S(2)}) collective-permute-start(f32[384,128]{1,0:T(8,128)S(1)} %get-tuple-element.12), channel_id=1, source_target_pairs={{64,0},{128,64},{192,128},{256,192},{320,256},{384,320},{448,384},... | collective-permute-start | bytes 589832 | tf_op jit(solution)/shard_map/ppermute | solution.py:80

commit v5 on v4

--- a/solution.py
+++ b/solution.py
@@ -3,6 +3,8 @@
 import jax.numpy as jnp
 from jax import lax
 from jax.sharding import PartitionSpec as P
+from jax.experimental import pallas as pl
+from jax.experimental.pallas import tpu as pltpu
 
 LIFT_ALPHA = -1.586134342059924
 LIFT_BETA = -0.052980118572961
@@ -79,6 +81,78 @@
     from_below = lax.ppermute(upper_half, axis, up)
     from_above = lax.ppermute(lower_half, axis, down)
     return from_below, from_above
+
+
+def y_pass_kernel(one_ref, two_ref, below_ref, above_ref, a1_ref, a2_ref, approx_ref, two_out, one_out):
+    n_two, lanes = two_ref.shape
+    n_one = one_ref.shape[0]
+    ny = 2 * one_out.shape[2]
+    slabs_one = n_one // ny
+    slabs_two = n_two // ny
+    narrow = (below_ref.shape[0] - n_two) // slabs_one
+    blocks = []
+    for s in range(slabs_one):
+        blocks.append(
+            jnp.concatenate(
+                [
+                    below_ref[s * narrow : (s + 1) * narrow, :],
+                    one_ref[s * ny : (s + 1) * ny, :],
+                    above_ref[s * narrow : (s + 1) * narrow, :],
+                ]
+            )
+        )
+    result = jnp.dot(a1_ref[...], jnp.concatenate(blocks, axis=1), precision=EXACT,
+                     preferred_element_type=jnp.float32)
+    half_x, half_y = one_out.shape[1], one_out.shape[2]
+    for s in range(slabs_one):
+        kx, bz = divmod(s, 2)
+        bx, kx8 = divmod(kx, half_x)
+        block = result[:, s * lanes : (s + 1) * lanes]
+        for by in range(2):
+            band = 4 * bx + 2 * by + bz
+            if band:
+                one_out[band - 1, kx8] = block[by * half_y : (by + 1) * half_y]
+    base = n_one // ny * narrow
+    blocks = []
+    for s in range(slabs_two):
+        blocks.append(
+            jnp.concatenate(
+                [
+                    below_ref[base + s * ny : base + (s + 1) * ny, :],
+                    two_ref[s * ny : (s + 1) * ny, :],
+                    above_ref[base + s * ny : base + (s + 1) * ny, :],
+                ]
+            )
+        )
+    result = jnp.dot(a2_ref[...], jnp.concatenate(blocks, axis=1), precision=EXACT,
+                     preferred_element_type=jnp.float32)
+    quarter_x, quarter_y, quarter_z = approx_ref.shape
+    for s in range(slabs_two):
+        bx, kx4 = divmod(s, quarter_x)
+        block = result[:, s * lanes : (s + 1) * lanes]
+        for by in range(2):
+            for bz in range(2):
+                piece = block[by * quarter_y : (by + 1) * quarter_y, bz * quarter_z : (bz + 1) * quarter_z]
+                band = 4 * bx + 2 * by + bz
+                if band:
+                    two_out[band - 1, kx4] = piece
+                else:
+                    approx_ref[kx4] = piece
+
+
+def y_pass(x_one, x_two, below, above, a1y, a2y, nx, ny, nz):
+    vmem = pl.BlockSpec(memory_space=pltpu.VMEM)
+    lanes = x_one.shape[-1]
+    return pl.pallas_call(
+        y_pass_kernel,
+        out_shape=(
+            jax.ShapeDtypeStruct((nx // 4, ny // 4, nz // 4), jnp.float32),
+            jax.ShapeDtypeStruct((7, nx // 4, ny // 4, nz // 4), jnp.float32),
+            jax.ShapeDtypeStruct((7, nx // 2, ny // 2, lanes), jnp.float32),
+        ),
+        in_specs=[vmem] * 6,
+        out_specs=(vmem, vmem, vmem),
+    )(x_one.reshape(-1, lanes), x_two.reshape(-1, lanes), below, above, a1y, a2y)
 
 
 def per_device(velocity):
@@ -118,30 +192,8 @@
     top = jnp.concatenate([flat(x_one[:, :, ny - narrow :]), flat(x_two)])
     bottom = jnp.concatenate([flat(x_one[:, :, :narrow]), flat(x_two)])
     below, above = exchange(bottom, top, "morton")
-    split = kx1 * 2 * narrow
-    one_ext = jnp.concatenate(
-        [
-            below[:split].reshape(kx1, 2, narrow, lanes),
-            x_one,
-            above[:split].reshape(kx1, 2, narrow, lanes),
-        ],
-        axis=2,
-    )
-    two_ext = jnp.concatenate(
-        [below[split:].reshape(kx2, ny, lanes), x_two, above[split:].reshape(kx2, ny, lanes)],
-        axis=1,
-    )
     a1y, a2y = pick(y_maps, 2), pick(y_maps, 3)
-    y_one = jnp.einsum("ky,abyz->abkz", a1y, one_ext, precision=EXACT)
-    y_two = jnp.einsum("ky,ayz->akz", a2y, two_ext, precision=EXACT)
-
-    hx, hy = nx // 2, ny // 2
-    level_one = y_one.reshape(2, hx, 2, 2, hy, lanes).transpose(0, 3, 2, 1, 4, 5)
-    level_one = level_one.reshape(8, hx, hy, lanes)
-    qx, qy, qz = nx // 4, ny // 4, nz // 4
-    level_two = y_two.reshape(2, qx, 2, qy, 2, qz).transpose(0, 2, 4, 1, 3, 5)
-    level_two = level_two.reshape(8, qx, qy, qz)
-    return (level_two[0], level_two[1:], level_one[1:])
+    return y_pass(x_one, x_two, below, above, a1y, a2y, nx, ny, nz)
 
 
 def solution(mesh):

time: 41.6 us -> 39 us (0.938)
  the two profiles are of different devices: /device:TPU:393 before, /device:TPU:1 now
where the time goes in v5:
time: 39 us; the launch traced here: 38.6 us
  starting transfers between devices  24.4 us (63%)
  local copies, waits for them, and re-layouts  7.1 us (18%)
  matrix products  2.44 us (6%)
  Pallas kernels  2.42 us (6%)
  waiting for transfers between devices  1.32 us (3%)
  between operations  0.89 us (2%)
    ppermute x2, starting transfers between devices, exchange(): from_above = lax.ppermute(lower_half, axis, down)  17.7 us
    ppermute x2, starting transfers between devices, exchange(): from_below = lax.ppermute(upper_half, axis, up)  6.7 us
    unnamed x14, local copies, waits for them, and re-layouts  3.15 us
    pallas_call x1, Pallas kernels, y_pass(): pl.pallas_call(y_pass_kernel, out_shape=(jax.ShapeDtypeStruct((nx // 4, n...  2.42 us
    dot_general x1, matrix products, per_device(): jnp.einsum('xyz,bzk->xbyk', velocity, jnp.asarray(z_maps), precision=EXACT)  1.61 us
    ppermute x2, waiting for transfers between devices, exchange(): from_below = lax.ppermute(upper_half, axis, up)  1.31 us
    slice x2, local copies, waits for them, and re-layouts, per_device(): maps[places[i][0]:places[i][0] + places[i][1], :places[i][2]]  1.19 us
    slice x2, local copies, waits for them, and re-layouts, per_device(): one_rows = u[:, 0:2]  0.91 us
  transfers between devices with their start and end apart: 4, of which 2 were waited for; matrix products, arithmetic and copies ran while one was open for 5% of the time, Pallas kernels for 0%

profile of v5, /device:TPU:1, one launch (start us, length us, event | category | flops | bytes accessed | tf_op | source)
XLA Modules:
  0.0 38.6 jit_solution(3544521538402604920)
XLA Ops:
  0.6 0.0 copy-start
  0.6 0.9 %copy-done = f32[16,16,256]{2,1,0:T(8,128)S(1)} copy-done((f32[16,16,256]{2,1,0:T(8,128)S(1)}, f32[16,16,256]{2,1,0:T(8,128)}, u32[]{:S(2)}) %copy-start) | copy-done | bytes 262168
  1.6 1.6 %convolution_bitcast_fusion = f32[16,3,16,128]{3,2,0,1:T(8,128)S(1)} fusion(f32[3,256,128,1]{2,1,3,0:T(8,128)} %constant.34, f32[16,16,256]{2,1,0:T(8,128)S(1)} %copy-done), kind=kOutput, calls=%fused_computation | convolution fusion | flops 301989888 | bytes 1048576 | tf_op jit(solution)/shard_map/xyz,bzk->xbyk/dot_general | solution.py:164
  3.2 0.0 copy-start.1
  3.3 1.3 %collective-permute-start.1 = (f32[320,128]{1,0:T(8,128)S(1)}, f32[320,128]{1,0:T(8,128)S(1)}, u32[]{:S(2)}, u32[]{:S(2)}) collective-permute-start(f32[320,128]{1,0:T(8,128)S(1)} %pad_maximum_fusion.5), channel_id=1, source_target_pairs={{1,0},{2,1},{3,2},{4,3},{5,4},{6,5},{7,6},{8,7},{9,8},{10,9},{11,1... | collective-permute-start | bytes 491528 | tf_op jit(solution)/shard_map/ppermute | solution.py:82
  4.6 4.8 %collective-permute-start = (f32[320,128]{1,0:T(8,128)S(1)}, f32[320,128]{1,0:T(8,128)S(1)}, u32[]{:S(2)}, u32[]{:S(2)}) collective-permute-start(f32[320,128]{1,0:T(8,128)S(1)} %pad_maximum_fusion.4), channel_id=1, source_target_pairs={{0,1},{1,2},{2,3},{3,4},{4,5},{5,6},{6,7},{7,8},{8,9},{9,10},{10,1... | collective-permute-start | bytes 491528 | tf_op jit(solution)/shard_map/ppermute | solution.py:81
  9.4 0.0 copy-done.1
  9.4 0.0 copy-start.6
  9.5 0.9 %copy-done.6 = f32[3,48,128]{2,1,0:T(8,128)S(1)} copy-done((f32[3,48,128]{2,1,0:T(8,128)S(1)}, f32[3,48,128]{2,1,0:T(8,128)}, u32[]{:S(2)}) %copy-start.6) | copy-done | bytes 73752
  10.3 0.0 collective-permute-done.1
  10.3 0.0 copy-start.3
  10.3 0.7 %copy-done.3 = f32[320,128]{1,0:T(8,128)} copy-done((f32[320,128]{1,0:T(8,128)}, f32[320,128]{1,0:T(8,128)S(1)}, u32[]{:S(2)}) %copy-start.3) | copy-done | bytes 163864
  11.0 0.7 %collective-permute-done = f32[320,128]{1,0:T(8,128)S(1)} collective-permute-done((f32[320,128]{1,0:T(8,128)S(1)}, f32[320,128]{1,0:T(8,128)S(1)}, u32[]{:S(2)}, u32[]{:S(2)}) %collective-permute-start) | collective-permute-done | bytes 163872 | tf_op jit(solution)/shard_map/ppermute | solution.py:81
  11.7 0.0 slice-start.1
  11.7 0.9 %slice-done.1 = f32[192,128]{1,0:T(8,128)S(1)} async-done(((f32[320,128]{1,0:T(8,128)}), f32[192,128]{1,0:T(8,128)S(1)}, s32[]{:S(2)}) %slice-start.1) | async-done | bytes 98328 | tf_op jit(solution)/shard_map/slice | solution.py:178
  12.6 0.4 fusion.2
  13.0 0.0 slice-start
  13.0 0.0 copy-start.2
  13.0 0.0 slice-start.2
  13.0 0.9 %slice-done = f32[16,2,16,128]{3,2,0,1:T(8,128)S(1)} async-done(((f32[16,3,16,128]{3,2,0,1:T(8,128)}), f32[16,2,16,128]{3,2,0,1:T(8,128)S(1)}, s32[]{:S(2)}) %slice-start) | async-done | bytes 262168 | tf_op jit(solution)/shard_map/slice | solution.py:167
  14.0 0.0 slice-done.2
  14.0 0.5 %fusion = f32[16,2,16,128]{3,0,2,1:T(8,128)S(1)} fusion(f32[24,2,16,128]{3,2,0,1:T(8,128)S(1)} %pad_maximum_fusion, f32[48,128]{1,0:T(8,128)S(1)} %get-tuple-element.10), kind=kOutput, calls=%fused_computation.2 | convolution fusion | flops 18874368 | bytes 663552 | tf_op jit(solution)/shard_map/kx,xbyz->kbyz/dot_general | solution.py:187
  14.6 0.0 copy-done.2
  14.6 16.4 %collective-permute-start.3 = (f32[384,128]{1,0:T(8,128)S(1)}, f32[384,128]{1,0:T(8,128)S(1)}, u32[]{:S(2)}, u32[]{:S(2)}) collective-permute-start(f32[384,128]{1,0:T(8,128)S(1)} %get-tuple-element.11), channel_id=1, source_target_pairs={{64,0},{128,64},{192,128},{256,192},{320,256},{384,320},{448,384},... | collective-permute-start | bytes 589832 | tf_op jit(solution)/shard_map/ppermute | solution.py:82
  31.0 1.9 %collective-permute-start.2 = (f32[384,128]{1,0:T(8,128)S(1)}, f32[384,128]{1,0:T(8,128)S(1)}, u32[]{:S(2)}, u32[]{:S(2)}) collective-permute-start(f32[384,128]{1,0:T(8,128)S(1)} %get-tuple-element.12), channel_id=1, source_target_pairs={{0,64},{64,128},{128,192},{192,256},{256,320},{320,384},{384,448},... | collective-permute-start | bytes 589832 | tf_op jit(solution)/shard_map/ppermute | solution.py:81
  33.0 0.6 %slice.85.a2_ref = f32[8,48]{1,0:T(8,128)} slice(f32[48,128]{1,0:T(8,128)S(1)} %get-tuple-element.9), slice={[40:48], [0:48]} | slice | bytes 3072 | tf_op jit(solution)/shard_map/slice | solution.py:185
  33.5 0.6 %slice.84.a1_ref = f32[16,32]{1,0:T(8,128)} slice(f32[48,128]{1,0:T(8,128)S(1)} %get-tuple-element.9), slice={[24:40], [0:32]} | slice | bytes 4096 | tf_op jit(solution)/shard_map/slice | solution.py:185
  34.1 0.8 %copy.17 = f32[16,2,16,128]{3,2,1,0:T(8,128)} copy(f32[16,2,16,128]{3,0,2,1:T(8,128)S(1)} %fusion) | data formatting | bytes 524288 | tf_op jit(solution)/shard_map/kx,xbyz->kbyz/dot_general | solution.py:187
  34.9 0.0 collective-permute-done.3.above_ref
  34.9 0.0 copy-start.4
  34.9 0.6 %collective-permute-done.2.below_ref = f32[384,128]{1,0:T(8,128)S(1)} collective-permute-done((f32[384,128]{1,0:T(8,128)S(1)}, f32[384,128]{1,0:T(8,128)S(1)}, u32[]{:S(2)}, u32[]{:S(2)}) %collective-permute-start.2) | collective-permute-done | bytes 196640 | tf_op jit(solution)/shard_map/ppermute | solution.py:81
  35.5 0.0 copy-start.5
  35.5 0.1 copy-done.4
  35.6 0.6 %copy-done.5 = f32[384,128]{1,0:T(8,128)} copy-done((f32[384,128]{1,0:T(8,128)}, f32[384,128]{1,0:T(8,128)S(1)}, u32[]{:S(2)}) %copy-start.5) | copy-done | bytes 196632
  36.2 2.4 %shard_map.58 = (f32[4,4,64]{2,1,0:T(4,128)}, f32[7,4,4,64]{3,2,1,0:T(4,128)}, f32[7,8,8,128]{3,2,1,0:T(8,128)}) custom-call(f32[512,128]{1,0:T(8,128)} %bitcast.35, f32[128,128]{1,0:T(8,128)} %bitcast.37, f32[384,128]{1,0:T(8,128)} %copy-done.5, f32[384,128]{1,0:T(8,128)} %copy-done.4, f32[16,32]{1,0:T(8,128)} %slice.84.a1_ref, f32[8,48]{1,0:T(8,128)} %slice.85.a2_ref), custom_call_target="tpu_custom_call" | custom-call | tf_op jit(solution)/shard_map/pallas_call | solution.py:146
  (17 shorter events, 0.3 us)
Async XLA Ops:
  0.6 1.0 %copy-start = (f32[16,16,256]{2,1,0:T(8,128)S(1)}, f32[16,16,256]{2,1,0:T(8,128)}, u32[]{:S(2)}) copy-start(f32[16,16,256]{2,1,0:T(8,128)} %param.3) | copy-start | bytes 786436
  3.2 6.2 %copy-start.1 = (f32[16,3,16,128]{3,2,0,1:T(8,128)}, f32[16,3,16,128]{3,2,0,1:T(8,128)S(1)}, u32[]{:S(2)}) copy-start(f32[16,3,16,128]{3,2,0,1:T(8,128)S(1)} %convolution_bitcast_fusion) | copy-start | bytes 1179652
  3.3 7.0 %collective-permute-start.1 = (f32[320,128]{1,0:T(8,128)S(1)}, f32[320,128]{1,0:T(8,128)S(1)}, u32[]{:S(2)}, u32[]{:S(2)}) collective-permute-start(f32[320,128]{1,0:T(8,128)S(1)} %pad_maximum_fusion.5), channel_id=1, source_target_pairs={{1,0},{2,1},{3,2},{4,3},{5,4},{6,5},{7,6},{8,7},{9,8},{10,9},{11,1... | collective-permute-start | bytes 491528 | tf_op jit(solution)/shard_map/ppermute | solution.py:82
  4.6 7.1 %collective-permute-start = (f32[320,128]{1,0:T(8,128)S(1)}, f32[320,128]{1,0:T(8,128)S(1)}, u32[]{:S(2)}, u32[]{:S(2)}) collective-permute-start(f32[320,128]{1,0:T(8,128)S(1)} %pad_maximum_fusion.4), channel_id=1, source_target_pairs={{0,1},{1,2},{2,3},{3,4},{4,5},{5,6},{6,7},{7,8},{8,9},{9,10},{10,1... | collective-permute-start | bytes 491528 | tf_op jit(solution)/shard_map/ppermute | solution.py:81
  9.4 0.9 %copy-start.6 = (f32[3,48,128]{2,1,0:T(8,128)S(1)}, f32[3,48,128]{2,1,0:T(8,128)}, u32[]{:S(2)}) copy-start(f32[3,48,128]{2,1,0:T(8,128)} %constant.32.clone) | copy-start | bytes 221188
  10.3 0.7 %copy-start.3 = (f32[320,128]{1,0:T(8,128)}, f32[320,128]{1,0:T(8,128)S(1)}, u32[]{:S(2)}) copy-start(f32[320,128]{1,0:T(8,128)S(1)} %collective-permute-done.1) | copy-start | bytes 491524
  11.7 0.9 %slice-start.1 = ((f32[320,128]{1,0:T(8,128)}), f32[192,128]{1,0:T(8,128)S(1)}, s32[]{:S(2)}) async-start(f32[320,128]{1,0:T(8,128)} %copy-done.3), calls=%async_computation.1 | async-start | bytes 196608 | tf_op jit(solution)/shard_map/slice | solution.py:178
  13.0 1.0 %slice-start = ((f32[16,3,16,128]{3,2,0,1:T(8,128)}), f32[16,2,16,128]{3,2,0,1:T(8,128)S(1)}, s32[]{:S(2)}) async-start(f32[16,3,16,128]{3,2,0,1:T(8,128)} %copy-done.1), calls=%async_computation | async-start | bytes 524288 | tf_op jit(solution)/shard_map/slice | solution.py:167
  13.0 1.6 %copy-start.2 = (f32[8,16,128]{2,1,0:T(8,128)}, f32[8,16,128]{2,1,0:T(8,128)S(1)}, u32[]{:S(2)}) copy-start(f32[8,16,128]{2,1,0:T(8,128)S(1)} %copy.19) | copy-start | bytes 196612
  13.0 0.9 %slice-start.2 = ((f32[320,128]{1,0:T(8,128)}), f32[128,128]{1,0:T(8,128)S(1)}, s32[]{:S(2)}) async-start(f32[320,128]{1,0:T(8,128)} %copy-done.3), calls=%async_computation.2 | async-start | bytes 131072 | tf_op jit(solution)/shard_map/slice | solution.py:175
  14.6 20.3 %collective-permute-start.3 = (f32[384,128]{1,0:T(8,128)S(1)}, f32[384,128]{1,0:T(8,128)S(1)}, u32[]{:S(2)}, u32[]{:S(2)}) collective-permute-start(f32[384,128]{1,0:T(8,128)S(1)} %get-tuple-element.11), channel_id=1, source_target_pairs={{64,0},{128,64},{192,128},{256,192},{320,256},{384,320},{448,384},... | collective-permute-start | bytes 589832 | tf_op jit(solution)/shard_map/ppermute | solution.py:82
  31.0 4.5 %collective-permute-start.2 = (f32[384,128]{1,0:T(8,128)S(1)}, f32[384,128]{1,0:T(8,128)S(1)}, u32[]{:S(2)}, u32[]{:S(2)}) collective-permute-start(f32[384,128]{1,0:T(8,128)S(1)} %get-tuple-element.12), channel_id=1, source_target_pairs={{0,64},{64,128},{128,192},{192,256},{256,320},{320,384},{384,448},... | collective-permute-start | bytes 589832 | tf_op jit(solution)/shard_map/ppermute | solution.py:81
  34.9 0.7 %copy-start.4 = (f32[384,128]{1,0:T(8,128)}, f32[384,128]{1,0:T(8,128)S(1)}, u32[]{:S(2)}) copy-start(f32[384,128]{1,0:T(8,128)S(1)} %collective-permute-done.3.above_ref) | copy-start | bytes 589828
  35.5 0.7 %copy-start.5 = (f32[384,128]{1,0:T(8,128)}, f32[384,128]{1,0:T(8,128)S(1)}, u32[]{:S(2)}) copy-start(f32[384,128]{1,0:T(8,128)S(1)} %collective-permute-done.2.below_ref) | copy-start | bytes 589828

commit v6 on v5

--- a/solution.py
+++ b/solution.py
@@ -1,3 +1,5 @@
+import functools
+
 import numpy as np
 import jax
 import jax.numpy as jnp
@@ -83,7 +85,7 @@
     return from_below, from_above
 
 
-def y_pass_kernel(one_ref, two_ref, below_ref, above_ref, a1_ref, a2_ref, approx_ref, two_out, one_out):
+def y_pass_kernel(one_ref, two_ref, below_ref, above_ref, maps_ref, approx_ref, two_out, one_out, *, places):
     n_two, lanes = two_ref.shape
     n_one = one_ref.shape[0]
     ny = 2 * one_out.shape[2]
@@ -101,7 +103,9 @@
                 ]
             )
         )
-    result = jnp.dot(a1_ref[...], jnp.concatenate(blocks, axis=1), precision=EXACT,
+    row, rows, cols = places[2]
+    a1 = maps_ref[row : row + rows, :][:, :cols]
+    result = jnp.dot(a1, jnp.concatenate(blocks, axis=1), precision=EXACT,
                      preferred_element_type=jnp.float32)
     half_x, half_y = one_out.shape[1], one_out.shape[2]
     for s in range(slabs_one):
@@ -124,7 +128,9 @@
                 ]
             )
         )
-    result = jnp.dot(a2_ref[...], jnp.concatenate(blocks, axis=1), precision=EXACT,
+    row, rows, cols = places[3]
+    a2 = maps_ref[row : row + rows, :][:, :cols]
+    result = jnp.dot(a2, jnp.concatenate(blocks, axis=1), precision=EXACT,
                      preferred_element_type=jnp.float32)
     quarter_x, quarter_y, quarter_z = approx_ref.shape
     for s in range(slabs_two):
@@ -140,19 +146,19 @@
                     approx_ref[kx4] = piece
 
 
-def y_pass(x_one, x_two, below, above, a1y, a2y, nx, ny, nz):
+def y_pass(x_one, x_two, below, above, y_maps, places, nx, ny, nz):
     vmem = pl.BlockSpec(memory_space=pltpu.VMEM)
     lanes = x_one.shape[-1]
     return pl.pallas_call(
-        y_pass_kernel,
+        functools.partial(y_pass_kernel, places=tuple(places)),
         out_shape=(
             jax.ShapeDtypeStruct((nx // 4, ny // 4, nz // 4), jnp.float32),
             jax.ShapeDtypeStruct((7, nx // 4, ny // 4, nz // 4), jnp.float32),
             jax.ShapeDtypeStruct((7, nx // 2, ny // 2, lanes), jnp.float32),
         ),
-        in_specs=[vmem] * 6,
+        in_specs=[vmem] * 5,
         out_specs=(vmem, vmem, vmem),
-    )(x_one.reshape(-1, lanes), x_two.reshape(-1, lanes), below, above, a1y, a2y)
+    )(x_one.reshape(-1, lanes), x_two.reshape(-1, lanes), below, above, y_maps)
 
 
 def per_device(velocity):
@@ -192,8 +198,7 @@
     top = jnp.concatenate([flat(x_one[:, :, ny - narrow :]), flat(x_two)])
     bottom = jnp.concatenate([flat(x_one[:, :, :narrow]), flat(x_two)])
     below, above = exchange(bottom, top, "morton")
-    a1y, a2y = pick(y_maps, 2), pick(y_maps, 3)
-    return y_pass(x_one, x_two, below, above, a1y, a2y, nx, ny, nz)
+    return y_pass(x_one, x_two, below, above, y_maps, places, nx, ny, nz)
 
 
 def solution(mesh):

time: 39 us -> 39 us (level)
  waiting for transfers between devices: 1.32 us -> 1.89 us
  local copies, waits for them, and re-layouts: 7.1 us -> 6.53 us
    slice x2 -> x0, local copies, waits for them, and re-layouts: 1.19 us -> none  [per_device(): maps[places[i][0]:places[i][0] + places[i][1], :places[i][2]]]
    squeeze x1, local copies, waits for them, and re-layouts: 0.01 us -> 0.61 us  [per_device(): y_maps = lax.dynamic_index_in_dim(table, case_of('morton'), keepdims=False)]
    ppermute x2, waiting for transfers between devices: 1.31 us -> 1.89 us  [exchange(): from_below = lax.ppermute(upper_half, axis, up)]
  transfers between devices with their start and end apart: 4 -> 4, of which waited for: 2 -> 2; matrix products, arithmetic and copies ran while one was open for 5% -> 4% of each run, Pallas kernels for 0% -> 0%
where the time goes in v6:
time: 39 us; the launch traced here: 38.7 us
  starting transfers between devices  24.4 us (63%)
  local copies, waits for them, and re-layouts  6.53 us (17%)
  Pallas kernels  2.45 us (6%)
  matrix products  2.44 us (6%)
  waiting for transfers between devices  1.89 us (5%)
  between operations  0.88 us (2%)
    ppermute x2, starting transfers between devices, exchange(): from_above = lax.ppermute(lower_half, axis, down)  17.7 us
    ppermute x2, starting transfers between devices, exchange(): from_below = lax.ppermute(upper_half, axis, up)  6.7 us
    unnamed x14, local copies, waits for them, and re-layouts  3.15 us
    pallas_call x1, Pallas kernels, y_pass(): pl.pallas_call(functools.partial(y_pass_kernel, places=tuple(places)), ou...  2.45 us
    ppermute x2, waiting for transfers between devices, exchange(): from_below = lax.ppermute(upper_half, axis, up)  1.89 us
    dot_general x1, matrix products, per_device(): jnp.einsum('xyz,bzk->xbyk', velocity, jnp.asarray(z_maps), precision=EXACT)  1.61 us
    slice x2, local copies, waits for them, and re-layouts, per_device(): one_rows = u[:, 0:2]  0.91 us
    slice x2, local copies, waits for them, and re-layouts, per_device(): above[split:].reshape(wide, ny, lanes)  0.88 us
  transfers between devices with their start and end apart: 4, of which 2 were waited for; matrix products, arithmetic and copies ran while one was open for 4% of the time, Pallas kernels for 0%

profile of v6, /device:TPU:1, one launch (start us, length us, event | category | flops | bytes accessed | tf_op | source)
XLA Modules:
  0.0 38.7 jit_solution(5495267712770796628)
XLA Ops:
  0.6 0.0 copy-start
  0.6 0.9 %copy-done = f32[16,16,256]{2,1,0:T(8,128)S(1)} copy-done((f32[16,16,256]{2,1,0:T(8,128)S(1)}, f32[16,16,256]{2,1,0:T(8,128)}, u32[]{:S(2)}) %copy-start) | copy-done | bytes 262168
  1.6 1.6 %convolution_bitcast_fusion = f32[16,3,16,128]{3,2,0,1:T(8,128)S(1)} fusion(f32[3,256,128,1]{2,1,3,0:T(8,128)} %constant.34, f32[16,16,256]{2,1,0:T(8,128)S(1)} %copy-done), kind=kOutput, calls=%fused_computation | convolution fusion | flops 301989888 | bytes 1048576 | tf_op jit(solution)/shard_map/xyz,bzk->xbyk/dot_general | solution.py:170
  3.2 0.0 copy-start.1
  3.3 1.3 %collective-permute-start.1 = (f32[320,128]{1,0:T(8,128)S(1)}, f32[320,128]{1,0:T(8,128)S(1)}, u32[]{:S(2)}, u32[]{:S(2)}) collective-permute-start(f32[320,128]{1,0:T(8,128)S(1)} %pad_maximum_fusion.5), channel_id=1, source_target_pairs={{1,0},{2,1},{3,2},{4,3},{5,4},{6,5},{7,6},{8,7},{9,8},{10,9},{11,1... | collective-permute-start | bytes 491528 | tf_op jit(solution)/shard_map/ppermute | solution.py:84
  4.6 4.8 %collective-permute-start = (f32[320,128]{1,0:T(8,128)S(1)}, f32[320,128]{1,0:T(8,128)S(1)}, u32[]{:S(2)}, u32[]{:S(2)}) collective-permute-start(f32[320,128]{1,0:T(8,128)S(1)} %pad_maximum_fusion.4), channel_id=1, source_target_pairs={{0,1},{1,2},{2,3},{3,4},{4,5},{5,6},{6,7},{7,8},{8,9},{9,10},{10,1... | collective-permute-start | bytes 491528 | tf_op jit(solution)/shard_map/ppermute | solution.py:83
  9.4 0.0 copy-done.1
  9.4 0.0 copy-start.6
  9.5 0.9 %copy-done.6 = f32[3,48,128]{2,1,0:T(8,128)S(1)} copy-done((f32[3,48,128]{2,1,0:T(8,128)S(1)}, f32[3,48,128]{2,1,0:T(8,128)}, u32[]{:S(2)}) %copy-start.6) | copy-done | bytes 73752
  10.3 0.6 %dynamic-slice_bitcast_fusion = (f32[48,128]{1,0:T(8,128)}, f32[48,128]{1,0:T(8,128)S(1)}) fusion(f32[3,48,128]{2,1,0:T(8,128)S(1)} %copy-done.6, s32[]{:T(128)S(6)} %select_n.20, s32[]{:T(128)S(6)} %select_n.18), kind=kLoop, calls=%fused_computation.13 | loop fusion | bytes 98312 | tf_op jit(solution)/shard_map/jit(dynamic_index_in_dim)/squeeze | solution.py:190
  10.9 0.0 collective-permute-done.1
  10.9 0.0 copy-start.3
  11.0 0.7 %copy-done.3 = f32[320,128]{1,0:T(8,128)} copy-done((f32[320,128]{1,0:T(8,128)}, f32[320,128]{1,0:T(8,128)S(1)}, u32[]{:S(2)}) %copy-start.3) | copy-done | bytes 163864
  11.6 0.1 collective-permute-done
  11.7 0.0 slice-start.1
  11.7 0.9 %slice-done.1 = f32[192,128]{1,0:T(8,128)S(1)} async-done(((f32[320,128]{1,0:T(8,128)}), f32[192,128]{1,0:T(8,128)S(1)}, s32[]{:S(2)}) %slice-start.1) | async-done | bytes 98328 | tf_op jit(solution)/shard_map/slice | solution.py:184
  12.6 0.4 fusion.2
  13.0 0.0 slice-start
  13.0 0.0 copy-start.2
  13.0 0.0 slice-start.2
  13.0 0.9 %slice-done = f32[16,2,16,128]{3,2,0,1:T(8,128)S(1)} async-done(((f32[16,3,16,128]{3,2,0,1:T(8,128)}), f32[16,2,16,128]{3,2,0,1:T(8,128)S(1)}, s32[]{:S(2)}) %slice-start) | async-done | bytes 262168 | tf_op jit(solution)/shard_map/slice | solution.py:173
  14.0 0.0 slice-done.2
  14.0 0.5 %fusion = f32[16,2,16,128]{3,0,2,1:T(8,128)S(1)} fusion(f32[24,2,16,128]{3,2,0,1:T(8,128)S(1)} %pad_maximum_fusion, f32[48,128]{1,0:T(8,128)S(1)} %get-tuple-element.10), kind=kOutput, calls=%fused_computation.2 | convolution fusion | flops 18874368 | bytes 663552 | tf_op jit(solution)/shard_map/kx,xbyz->kbyz/dot_general | solution.py:193
  14.6 0.0 copy-done.2
  14.6 16.4 %collective-permute-start.3 = (f32[384,128]{1,0:T(8,128)S(1)}, f32[384,128]{1,0:T(8,128)S(1)}, u32[]{:S(2)}, u32[]{:S(2)}) collective-permute-start(f32[384,128]{1,0:T(8,128)S(1)} %get-tuple-element.11), channel_id=1, source_target_pairs={{64,0},{128,64},{192,128},{256,192},{320,256},{384,320},{448,384},... | collective-permute-start | bytes 589832 | tf_op jit(solution)/shard_map/ppermute | solution.py:84
  31.0 1.9 %collective-permute-start.2 = (f32[384,128]{1,0:T(8,128)S(1)}, f32[384,128]{1,0:T(8,128)S(1)}, u32[]{:S(2)}, u32[]{:S(2)}) collective-permute-start(f32[384,128]{1,0:T(8,128)S(1)} %get-tuple-element.12), channel_id=1, source_target_pairs={{0,64},{64,128},{128,192},{192,256},{256,320},{320,384},{384,448},... | collective-permute-start | bytes 589832 | tf_op jit(solution)/shard_map/ppermute | solution.py:83
  33.0 0.8 %copy.17 = f32[16,2,16,128]{3,2,1,0:T(8,128)} copy(f32[16,2,16,128]{3,0,2,1:T(8,128)S(1)} %fusion) | data formatting | bytes 524288 | tf_op jit(solution)/shard_map/kx,xbyz->kbyz/dot_general | solution.py:193
  33.7 0.0 collective-permute-done.3.above_ref
  33.7 0.0 copy-start.4
  33.7 1.8 %collective-permute-done.2.below_ref = f32[384,128]{1,0:T(8,128)S(1)} collective-permute-done((f32[384,128]{1,0:T(8,128)S(1)}, f32[384,128]{1,0:T(8,128)S(1)}, u32[]{:S(2)}, u32[]{:S(2)}) %collective-permute-start.2) | collective-permute-done | bytes 196640 | tf_op jit(solution)/shard_map/ppermute | solution.py:83
  35.5 0.0 copy-start.5
  35.5 0.0 copy-done.4
  35.5 0.7 %copy-done.5 = f32[384,128]{1,0:T(8,128)} copy-done((f32[384,128]{1,0:T(8,128)}, f32[384,128]{1,0:T(8,128)S(1)}, u32[]{:S(2)}) %copy-start.5) | copy-done | bytes 196632
  36.2 2.4 %shard_map.58 = (f32[4,4,64]{2,1,0:T(4,128)}, f32[7,4,4,64]{3,2,1,0:T(4,128)}, f32[7,8,8,128]{3,2,1,0:T(8,128)}) custom-call(f32[512,128]{1,0:T(8,128)} %bitcast.35, f32[128,128]{1,0:T(8,128)} %bitcast.37, f32[384,128]{1,0:T(8,128)} %copy-done.5, f32[384,128]{1,0:T(8,128)} %copy-done.4, f32[48,128]{1,0:T(8,128)} %get-tuple-element.9.maps_ref), custom_call_target="tpu_custom_call" | custom-call | tf_op jit(solution)/shard_map/pallas_call | solution.py:152
  (16 shorter events, 0.3 us)
Async XLA Ops:
  0.6 1.0 %copy-start = (f32[16,16,256]{2,1,0:T(8,128)S(1)}, f32[16,16,256]{2,1,0:T(8,128)}, u32[]{:S(2)}) copy-start(f32[16,16,256]{2,1,0:T(8,128)} %param.3) | copy-start | bytes 786436
  3.2 6.2 %copy-start.1 = (f32[16,3,16,128]{3,2,0,1:T(8,128)}, f32[16,3,16,128]{3,2,0,1:T(8,128)S(1)}, u32[]{:S(2)}) copy-start(f32[16,3,16,128]{3,2,0,1:T(8,128)S(1)} %convolution_bitcast_fusion) | copy-start | bytes 1179652
  3.3 7.7 %collective-permute-start.1 = (f32[320,128]{1,0:T(8,128)S(1)}, f32[320,128]{1,0:T(8,128)S(1)}, u32[]{:S(2)}, u32[]{:S(2)}) collective-permute-start(f32[320,128]{1,0:T(8,128)S(1)} %pad_maximum_fusion.5), channel_id=1, source_target_pairs={{1,0},{2,1},{3,2},{4,3},{5,4},{6,5},{7,6},{8,7},{9,8},{10,9},{11,1... | collective-permute-start | bytes 491528 | tf_op jit(solution)/shard_map/ppermute | solution.py:84
  4.6 7.1 %collective-permute-start = (f32[320,128]{1,0:T(8,128)S(1)}, f32[320,128]{1,0:T(8,128)S(1)}, u32[]{:S(2)}, u32[]{:S(2)}) collective-permute-start(f32[320,128]{1,0:T(8,128)S(1)} %pad_maximum_fusion.4), channel_id=1, source_target_pairs={{0,1},{1,2},{2,3},{3,4},{4,5},{5,6},{6,7},{7,8},{8,9},{9,10},{10,1... | collective-permute-start | bytes 491528 | tf_op jit(solution)/shard_map/ppermute | solution.py:83
  9.4 0.9 %copy-start.6 = (f32[3,48,128]{2,1,0:T(8,128)S(1)}, f32[3,48,128]{2,1,0:T(8,128)}, u32[]{:S(2)}) copy-start(f32[3,48,128]{2,1,0:T(8,128)} %constant.32.clone) | copy-start | bytes 221188
  10.9 0.7 %copy-start.3 = (f32[320,128]{1,0:T(8,128)}, f32[320,128]{1,0:T(8,128)S(1)}, u32[]{:S(2)}) copy-start(f32[320,128]{1,0:T(8,128)S(1)} %collective-permute-done.1) | copy-start | bytes 491524
  11.7 0.9 %slice-start.1 = ((f32[320,128]{1,0:T(8,128)}), f32[192,128]{1,0:T(8,128)S(1)}, s32[]{:S(2)}) async-start(f32[320,128]{1,0:T(8,128)} %copy-done.3), calls=%async_computation.1 | async-start | bytes 196608 | tf_op jit(solution)/shard_map/slice | solution.py:184
  13.0 1.0 %slice-start = ((f32[16,3,16,128]{3,2,0,1:T(8,128)}), f32[16,2,16,128]{3,2,0,1:T(8,128)S(1)}, s32[]{:S(2)}) async-start(f32[16,3,16,128]{3,2,0,1:T(8,128)} %copy-done.1), calls=%async_computation | async-start | bytes 524288 | tf_op jit(solution)/shard_map/slice | solution.py:173
  13.0 1.6 %copy-start.2 = (f32[8,16,128]{2,1,0:T(8,128)}, f32[8,16,128]{2,1,0:T(8,128)S(1)}, u32[]{:S(2)}) copy-start(f32[8,16,128]{2,1,0:T(8,128)S(1)} %copy.19) | copy-start | bytes 196612
  13.0 0.9 %slice-start.2 = ((f32[320,128]{1,0:T(8,128)}), f32[128,128]{1,0:T(8,128)S(1)}, s32[]{:S(2)}) async-start(f32[320,128]{1,0:T(8,128)} %copy-done.3), calls=%async_computation.2 | async-start | bytes 131072 | tf_op jit(solution)/shard_map/slice | solution.py:181
  14.6 19.1 %collective-permute-start.3 = (f32[384,128]{1,0:T(8,128)S(1)}, f32[384,128]{1,0:T(8,128)S(1)}, u32[]{:S(2)}, u32[]{:S(2)}) collective-permute-start(f32[384,128]{1,0:T(8,128)S(1)} %get-tuple-element.11), channel_id=1, source_target_pairs={{64,0},{128,64},{192,128},{256,192},{320,256},{384,320},{448,384},... | collective-permute-start | bytes 589832 | tf_op jit(solution)/shard_map/ppermute | solution.py:84
  31.0 4.5 %collective-permute-start.2 = (f32[384,128]{1,0:T(8,128)S(1)}, f32[384,128]{1,0:T(8,128)S(1)}, u32[]{:S(2)}, u32[]{:S(2)}) collective-permute-start(f32[384,128]{1,0:T(8,128)S(1)} %get-tuple-element.12), channel_id=1, source_target_pairs={{0,64},{64,128},{128,192},{192,256},{256,320},{320,384},{384,448},... | collective-permute-start | bytes 589832 | tf_op jit(solution)/shard_map/ppermute | solution.py:83
  33.7 1.8 %copy-start.4 = (f32[384,128]{1,0:T(8,128)}, f32[384,128]{1,0:T(8,128)S(1)}, u32[]{:S(2)}) copy-start(f32[384,128]{1,0:T(8,128)S(1)} %collective-permute-done.3.above_ref) | copy-start | bytes 589828
  35.5 0.7 %copy-start.5 = (f32[384,128]{1,0:T(8,128)}, f32[384,128]{1,0:T(8,128)S(1)}, u32[]{:S(2)}) copy-start(f32[384,128]{1,0:T(8,128)S(1)} %collective-permute-done.2.below_ref) | copy-start | bytes 589828

commit v7 on v6

--- a/solution.py
+++ b/solution.py
@@ -161,6 +161,80 @@
     )(x_one.reshape(-1, lanes), x_two.reshape(-1, lanes), below, above, y_maps)
 
 
+def x_pass_kernel(own_ref, below_ref, above_ref, maps_ref, one_out, two_out, top_out, bottom_out, *,
+                  taps, places, bands):
+    ny = two_out.shape[0] // len(taps[1])
+    slab = 2 * ny
+    stride = bands * ny
+    lo1, lo2 = 4, 12
+    split = lo1 * slab
+
+    def one_slab(i):
+        if i < lo1:
+            return below_ref[i * slab : (i + 1) * slab, :]
+        if i < lo1 + ny:
+            return own_ref[(i - lo1) * stride : (i - lo1) * stride + slab, :]
+        j = i - lo1 - ny
+        return above_ref[j * slab : (j + 1) * slab, :]
+
+    def two_slab(i):
+        if i < lo2:
+            return below_ref[split + i * ny : split + (i + 1) * ny, :]
+        if i < lo2 + ny:
+            at = (i - lo2) * stride + slab
+            return own_ref[at : at + ny, :]
+        j = i - lo2 - ny
+        return above_ref[split + j * ny : split + (j + 1) * ny, :]
+
+    narrow = (top_out.shape[0] - two_out.shape[0]) // (len(taps[0]) * 2)
+    row1 = places[0][0]
+    for k, used in enumerate(taps[0]):
+        acc = None
+        for i in used:
+            term = maps_ref[row1 + k, i] * one_slab(i)
+            acc = term if acc is None else acc + term
+        one_out[k * slab : (k + 1) * slab, :] = acc
+        for b in range(2):
+            at = (k * 2 + b) * narrow
+            top_out[at : at + narrow, :] = acc[b * ny + ny - narrow : (b + 1) * ny, :]
+            bottom_out[at : at + narrow, :] = acc[b * ny : b * ny + narrow, :]
+    base = len(taps[0]) * 2 * narrow
+    row2 = places[1][0]
+    for k, used in enumerate(taps[1]):
+        acc = None
+        for i in used:
+            term = maps_ref[row2 + k, i] * two_slab(i)
+            acc = term if acc is None else acc + term
+        two_out[k * ny : (k + 1) * ny, :] = acc
+        top_out[base + k * ny : base + (k + 1) * ny, :] = acc
+        bottom_out[base + k * ny : base + (k + 1) * ny, :] = acc
+
+
+def used_taps(maps):
+    present = np.any(np.stack([m != 0 for m in maps]), axis=0)
+    return tuple(tuple(int(i) for i in np.nonzero(row)[0]) for row in present)
+
+
+def x_pass(u, below, above, x_maps, places, nx, ny):
+    lanes = u.shape[-1]
+    taps = (used_taps(window_maps(nx, (4, 4), 0)), used_taps(window_maps(nx, (12, 12), 1)))
+    narrow = 8
+    vmem = pl.BlockSpec(memory_space=pltpu.VMEM)
+    smem = pl.BlockSpec(memory_space=pltpu.SMEM)
+    message = len(taps[0]) * 2 * narrow + len(taps[1]) * ny
+    return pl.pallas_call(
+        functools.partial(x_pass_kernel, taps=taps, places=tuple(places), bands=u.shape[1]),
+        out_shape=(
+            jax.ShapeDtypeStruct((len(taps[0]) * 2 * ny, lanes), jnp.float32),
+            jax.ShapeDtypeStruct((len(taps[1]) * ny, lanes), jnp.float32),
+            jax.ShapeDtypeStruct((message, lanes), jnp.float32),
+            jax.ShapeDtypeStruct((message, lanes), jnp.float32),
+        ),
+        in_specs=[vmem, vmem, vmem, smem],
+        out_specs=(vmem, vmem, vmem, vmem),
+    )(u.reshape(-1, lanes), below, above, x_maps)
+
+
 def per_device(velocity):
     nx, ny, nz = velocity.shape
 
@@ -176,27 +250,13 @@
     top = jnp.concatenate([flat(one_rows[nx - 4 :]), flat(two_rows[nx - wide :])])
     bottom = jnp.concatenate([flat(one_rows[:4]), flat(two_rows[:wide])])
     below, above = exchange(bottom, top, "slab")
-    split = 4 * 2 * ny
-    one_ext = jnp.concatenate(
-        [below[:split].reshape(4, 2, ny, lanes), one_rows, above[:split].reshape(4, 2, ny, lanes)]
-    )
-    two_ext = jnp.concatenate(
-        [below[split:].reshape(wide, ny, lanes), two_rows, above[split:].reshape(wide, ny, lanes)]
-    )
     assert nx == ny and wide == 12
     table, places = packed_maps(nx)
     table = jnp.asarray(table)
     x_maps = lax.dynamic_index_in_dim(table, case_of("slab"), keepdims=False)
     y_maps = lax.dynamic_index_in_dim(table, case_of("morton"), keepdims=False)
-    pick = lambda maps, i: maps[places[i][0] : places[i][0] + places[i][1], : places[i][2]]
-    a1x, a2x = pick(x_maps, 0), pick(x_maps, 1)
-    x_one = jnp.einsum("kx,xbyz->kbyz", a1x, one_ext, precision=EXACT)
-    x_two = jnp.einsum("kx,xyz->kyz", a2x, two_ext, precision=EXACT)
-
-    narrow = 8
-    kx1, kx2 = x_one.shape[0], x_two.shape[0]
-    top = jnp.concatenate([flat(x_one[:, :, ny - narrow :]), flat(x_two)])
-    bottom = jnp.concatenate([flat(x_one[:, :, :narrow]), flat(x_two)])
+    x_one, x_two, top, bottom = x_pass(u, below, above, x_maps, places, nx, ny)
+
     below, above = exchange(bottom, top, "morton")
     return y_pass(x_one, x_two, below, above, y_maps, places, nx, ny, nz)
 

time: 39 us -> 38.7 us (level)
  the two profiles are of different devices: /device:TPU:1 before, /device:TPU:503 now
where the time goes in v7:
time: 38.7 us; the launch traced here: 38.4 us
  starting transfers between devices  15.1 us (39%)
  waiting for transfers between devices  12.4 us (32%)
  Pallas kernels  4.72 us (12%)
  local copies, waits for them, and re-layouts  3.81 us (10%)
  matrix products  1.62 us (4%)
  between operations  0.74 us (2%)
    ppermute x2, waiting for transfers between devices, exchange(): from_above = lax.ppermute(lower_half, axis, down)  11.3 us
    ppermute x2, starting transfers between devices, exchange(): from_below = lax.ppermute(upper_half, axis, up)  10.6 us
    ppermute x2, starting transfers between devices, exchange(): from_above = lax.ppermute(lower_half, axis, down)  4.46 us
    pallas_call x1, Pallas kernels, y_pass(): pl.pallas_call(functools.partial(y_pass_kernel, places=tuple(places)), ou...  2.42 us
    unnamed x12, local copies, waits for them, and re-layouts  2.39 us
    pallas_call x1, Pallas kernels, x_pass(): pl.pallas_call(functools.partial(x_pass_kernel, taps=taps, places=tuple(p...  2.31 us
    dot_general x1, matrix products, per_device(): jnp.einsum('xyz,bzk->xbyk', velocity, jnp.asarray(z_maps), precision=EXACT)  1.62 us
    ppermute x2, waiting for transfers between devices, exchange(): from_below = lax.ppermute(upper_half, axis, up)  1.1 us
  transfers between devices with their start and end apart: 4, of which 4 were waited for; matrix products, arithmetic and copies ran while one was open for 4% of the time, Pallas kernels for 0%

profile of v7, /device:TPU:503, one launch (start us, length us, event | category | flops | bytes accessed | tf_op | source)
XLA Modules:
  0.0 38.4 jit_solution(14393177624138713884)
XLA Ops:
  0.6 0.0 copy-start
  0.6 0.9 %copy-done = f32[16,16,256]{2,1,0:T(8,128)S(1)} copy-done((f32[16,16,256]{2,1,0:T(8,128)S(1)}, f32[16,16,256]{2,1,0:T(8,128)}, u32[]{:S(2)}) %copy-start) | copy-done | bytes 262168
  1.6 1.6 %convolution_bitcast_fusion = f32[16,3,16,128]{3,2,0,1:T(8,128)S(1)} fusion(f32[3,256,128,1]{2,1,3,0:T(8,128)} %constant.34, f32[16,16,256]{2,1,0:T(8,128)S(1)} %copy-done), kind=kOutput, calls=%fused_computation | convolution fusion | flops 301989888 | bytes 1048576 | tf_op jit(solution)/shard_map/xyz,bzk->xbyk/dot_general | solution.py:244
  3.3 2.7 %collective-permute-start = (f32[320,128]{1,0:T(8,128)S(1)}, f32[320,128]{1,0:T(8,128)S(1)}, u32[]{:S(2)}, u32[]{:S(2)}) collective-permute-start(f32[320,128]{1,0:T(8,128)S(1)} %pad_maximum_fusion), channel_id=1, source_target_pairs={{0,1},{1,2},{2,3},{3,4},{4,5},{5,6},{6,7},{7,8},{8,9},{9,10},{10,1... | collective-permute-start | bytes 491528 | tf_op jit(solution)/shard_map/ppermute | solution.py:83
  6.1 2.5 %collective-permute-start.1 = (f32[320,128]{1,0:T(8,128)S(1)}, f32[320,128]{1,0:T(8,128)S(1)}, u32[]{:S(2)}, u32[]{:S(2)}) collective-permute-start(f32[320,128]{1,0:T(8,128)S(1)} %pad_maximum_fusion.1), channel_id=1, source_target_pairs={{1,0},{2,1},{3,2},{4,3},{5,4},{6,5},{7,6},{8,7},{9,8},{10,9},{11,1... | collective-permute-start | bytes 491528 | tf_op jit(solution)/shard_map/ppermute | solution.py:84
  8.6 0.0 copy-start.5
  8.6 0.8 %copy.6 = f32[16,3,16,128]{3,2,1,0:T(8,128)} copy(f32[16,3,16,128]{3,2,0,1:T(8,128)S(1)} %convolution_bitcast_fusion) | data formatting | bytes 786432 | tf_op jit(solution)/shard_map/xyz,bzk->xbyk/transpose | solution.py:244
  9.4 0.1 copy-done.5
  9.5 0.6 %dynamic-slice_bitcast_fusion = (f32[48,128]{1,0:T(8,128)}, f32[48,128]{1,0:T(8,128)}) fusion(f32[3,48,128]{2,1,0:T(8,128)S(1)} %copy-done.5, s32[]{:T(128)S(6)} %select_n.20, s32[]{:T(128)S(6)} %select_n.18), kind=kLoop, calls=%fused_computation.4 | loop fusion | bytes 98312 | tf_op jit(solution)/shard_map/jit(dynamic_index_in_dim)/squeeze | solution.py:257
  10.1 0.1 collective-permute-done.below_ref
  10.3 0.0 copy-start.3
  10.3 5.8 %collective-permute-done.1.above_ref = f32[320,128]{1,0:T(8,128)S(1)} collective-permute-done((f32[320,128]{1,0:T(8,128)S(1)}, f32[320,128]{1,0:T(8,128)S(1)}, u32[]{:S(2)}, u32[]{:S(2)}) %collective-permute-start.1) | collective-permute-done | bytes 163872 | tf_op jit(solution)/shard_map/ppermute | solution.py:84
  16.0 0.0 copy-start.4
  16.0 0.0 copy-done.3
  16.0 0.6 %copy-done.4 = f32[320,128]{1,0:T(8,128)} copy-done((f32[320,128]{1,0:T(8,128)}, f32[320,128]{1,0:T(8,128)S(1)}, u32[]{:S(2)}) %copy-start.4) | copy-done | bytes 163864
  16.7 2.3 %shard_map.58 = (f32[512,128]{1,0:T(8,128)}, f32[128,128]{1,0:T(8,128)}, f32[384,128]{1,0:T(8,128)}, f32[384,128]{1,0:T(8,128)}) custom-call(f32[768,128]{1,0:T(8,128)} %bitcast.18, f32[320,128]{1,0:T(8,128)} %copy-done.3, f32[320,128]{1,0:T(8,128)} %copy-done.4, f32[48,128]{1,0:T(8,128)} %get-tuple-element.16.maps_ref), custom_call_target="tpu_custom_call" | custom-call | tf_op jit(solution)/shard_map/pallas_call | solution.py:225
  19.0 7.9 %collective-permute-start.2 = (f32[384,128]{1,0:T(8,128)}, f32[384,128]{1,0:T(8,128)S(1)}, u32[]{:S(2)}, u32[]{:S(2)}) collective-permute-start(f32[384,128]{1,0:T(8,128)} %get-tuple-element.9), channel_id=1, source_target_pairs={{0,64},{64,128},{128,192},{192,256},{256,320},{320,384},{384,448},... | collective-permute-start | bytes 589832 | tf_op jit(solution)/shard_map/ppermute | solution.py:83
  26.9 1.9 %collective-permute-start.3 = (f32[384,128]{1,0:T(8,128)}, f32[384,128]{1,0:T(8,128)S(1)}, u32[]{:S(2)}, u32[]{:S(2)}) collective-permute-start(f32[384,128]{1,0:T(8,128)} %get-tuple-element.10), channel_id=1, source_target_pairs={{64,0},{128,64},{192,128},{256,192},{320,256},{384,320},{448,384},... | collective-permute-start | bytes 589832 | tf_op jit(solution)/shard_map/ppermute | solution.py:84
  28.8 1.0 %collective-permute-done.2.below_ref = f32[384,128]{1,0:T(8,128)S(1)} collective-permute-done((f32[384,128]{1,0:T(8,128)}, f32[384,128]{1,0:T(8,128)S(1)}, u32[]{:S(2)}, u32[]{:S(2)}) %collective-permute-start.2) | collective-permute-done | bytes 196640 | tf_op jit(solution)/shard_map/ppermute | solution.py:83
  29.8 0.0 copy-start.1
  29.8 5.5 %collective-permute-done.3.above_ref = f32[384,128]{1,0:T(8,128)S(1)} collective-permute-done((f32[384,128]{1,0:T(8,128)}, f32[384,128]{1,0:T(8,128)S(1)}, u32[]{:S(2)}, u32[]{:S(2)}) %collective-permute-start.3) | collective-permute-done | bytes 196640 | tf_op jit(solution)/shard_map/ppermute | solution.py:84
  35.3 0.0 copy-start.2
  35.3 0.0 copy-done.1
  35.3 0.7 %copy-done.2 = f32[384,128]{1,0:T(8,128)} copy-done((f32[384,128]{1,0:T(8,128)}, f32[384,128]{1,0:T(8,128)S(1)}, u32[]{:S(2)}) %copy-start.2) | copy-done | bytes 196632
  35.9 2.4 %shard_map.59 = (f32[4,4,64]{2,1,0:T(4,128)}, f32[7,4,4,64]{3,2,1,0:T(4,128)}, f32[7,8,8,128]{3,2,1,0:T(8,128)}) custom-call(f32[512,128]{1,0:T(8,128)} %get-tuple-element.7.one_ref, f32[128,128]{1,0:T(8,128)} %get-tuple-element.8.two_ref, f32[384,128]{1,0:T(8,128)} %copy-done.1, f32[384,128]{1,0:T(8,128)} %copy-done.2, f32[48,128]{1,0:T(8,128)} %get-tuple-element.15.maps_ref), custom_call_target="tpu_custom_call" | custom-call | tf_op jit(solution)/shard_map/pallas_call | solution.py:152
  (6 shorter events, 0.1 us)
Async XLA Ops:
  0.6 1.0 %copy-start = (f32[16,16,256]{2,1,0:T(8,128)S(1)}, f32[16,16,256]{2,1,0:T(8,128)}, u32[]{:S(2)}) copy-start(f32[16,16,256]{2,1,0:T(8,128)} %param.3) | copy-start | bytes 786436
  3.3 7.0 %collective-permute-start = (f32[320,128]{1,0:T(8,128)S(1)}, f32[320,128]{1,0:T(8,128)S(1)}, u32[]{:S(2)}, u32[]{:S(2)}) collective-permute-start(f32[320,128]{1,0:T(8,128)S(1)} %pad_maximum_fusion), channel_id=1, source_target_pairs={{0,1},{1,2},{2,3},{3,4},{4,5},{5,6},{6,7},{7,8},{8,9},{9,10},{10,1... | collective-permute-start | bytes 491528 | tf_op jit(solution)/shard_map/ppermute | solution.py:83
  6.1 10.0 %collective-permute-start.1 = (f32[320,128]{1,0:T(8,128)S(1)}, f32[320,128]{1,0:T(8,128)S(1)}, u32[]{:S(2)}, u32[]{:S(2)}) collective-permute-start(f32[320,128]{1,0:T(8,128)S(1)} %pad_maximum_fusion.1), channel_id=1, source_target_pairs={{1,0},{2,1},{3,2},{4,3},{5,4},{6,5},{7,6},{8,7},{9,8},{10,9},{11,1... | collective-permute-start | bytes 491528 | tf_op jit(solution)/shard_map/ppermute | solution.py:84
  8.6 0.9 %copy-start.5 = (f32[3,48,128]{2,1,0:T(8,128)S(1)}, f32[3,48,128]{2,1,0:T(8,128)}, u32[]{:S(2)}) copy-start(f32[3,48,128]{2,1,0:T(8,128)} %constant.32.clone) | copy-start | bytes 221188
  10.3 5.8 %copy-start.3 = (f32[320,128]{1,0:T(8,128)}, f32[320,128]{1,0:T(8,128)S(1)}, u32[]{:S(2)}) copy-start(f32[320,128]{1,0:T(8,128)S(1)} %collective-permute-done.below_ref) | copy-start | bytes 491524
  16.0 0.7 %copy-start.4 = (f32[320,128]{1,0:T(8,128)}, f32[320,128]{1,0:T(8,128)S(1)}, u32[]{:S(2)}) copy-start(f32[320,128]{1,0:T(8,128)S(1)} %collective-permute-done.1.above_ref) | copy-start | bytes 491524
  19.0 10.8 %collective-permute-start.2 = (f32[384,128]{1,0:T(8,128)}, f32[384,128]{1,0:T(8,128)S(1)}, u32[]{:S(2)}, u32[]{:S(2)}) collective-permute-start(f32[384,128]{1,0:T(8,128)} %get-tuple-element.9), channel_id=1, source_target_pairs={{0,64},{64,128},{128,192},{192,256},{256,320},{320,384},{384,448},... | collective-permute-start | bytes 589832 | tf_op jit(solution)/shard_map/ppermute | solution.py:83
  26.9 8.4 %collective-permute-start.3 = (f32[384,128]{1,0:T(8,128)}, f32[384,128]{1,0:T(8,128)S(1)}, u32[]{:S(2)}, u32[]{:S(2)}) collective-permute-start(f32[384,128]{1,0:T(8,128)} %get-tuple-element.10), channel_id=1, source_target_pairs={{64,0},{128,64},{192,128},{256,192},{320,256},{384,320},{448,384},... | collective-permute-start | bytes 589832 | tf_op jit(solution)/shard_map/ppermute | solution.py:84
  29.8 5.5 %copy-start.1 = (f32[384,128]{1,0:T(8,128)}, f32[384,128]{1,0:T(8,128)S(1)}, u32[]{:S(2)}) copy-start(f32[384,128]{1,0:T(8,128)S(1)} %collective-permute-done.2.below_ref) | copy-start | bytes 589828
  35.3 0.7 %copy-start.2 = (f32[384,128]{1,0:T(8,128)}, f32[384,128]{1,0:T(8,128)S(1)}, u32[]{:S(2)}) copy-start(f32[384,128]{1,0:T(8,128)S(1)} %collective-permute-done.3.above_ref) | copy-start | bytes 589828

commit v8 on v7

--- a/solution.py
+++ b/solution.py
@@ -165,7 +165,7 @@
                   taps, places, bands):
     ny = two_out.shape[0] // len(taps[1])
     slab = 2 * ny
-    stride = bands * ny
+    plane = own_ref.shape[0] // bands
     lo1, lo2 = 4, 12
     split = lo1 * slab
 
@@ -173,7 +173,8 @@
         if i < lo1:
             return below_ref[i * slab : (i + 1) * slab, :]
         if i < lo1 + ny:
-            return own_ref[(i - lo1) * stride : (i - lo1) * stride + slab, :]
+            at = (i - lo1) * ny
+            return jnp.concatenate([own_ref[at : at + ny, :], own_ref[plane + at : plane + at + ny, :]])
         j = i - lo1 - ny
         return above_ref[j * slab : (j + 1) * slab, :]
 
@@ -181,7 +182,7 @@
         if i < lo2:
             return below_ref[split + i * ny : split + (i + 1) * ny, :]
         if i < lo2 + ny:
-            at = (i - lo2) * stride + slab
+            at = 2 * plane + (i - lo2) * ny
             return own_ref[at : at + ny, :]
         j = i - lo2 - ny
         return above_ref[split + j * ny : split + (j + 1) * ny, :]
@@ -232,7 +233,7 @@
         ),
         in_specs=[vmem, vmem, vmem, smem],
         out_specs=(vmem, vmem, vmem, vmem),
-    )(u.reshape(-1, lanes), below, above, x_maps)
+    )(u.transpose(1, 0, 2, 3).reshape(-1, lanes), below, above, x_maps)
 
 
 def per_device(velocity):

time: 38.7 us -> 39.4 us (1.018)
  waiting for transfers between devices: 12.4 us -> 13.2 us
    ppermute x2, waiting for transfers between devices: 1.1 us -> 1.94 us  [exchange(): from_below = lax.ppermute(upper_half, axis, up)]
    transpose x1 -> x0, local copies, waits for them, and re-layouts: 0.77 us -> none  [per_device(): jnp.einsum('xyz,bzk->xbyk', velocity, jnp.asarray(z_maps), precision=EXACT)]
    unnamed x12 -> x14, local copies, waits for them, and re-layouts: 2.39 us -> 2.98 us
  transfers between devices with their start and end apart: 4 -> 4, of which waited for: 4 -> 4; matrix products, arithmetic and copies ran while one was open for 4% -> 2% of each run, Pallas kernels for 0% -> 0%
where the time goes in v8:
time: 39.4 us; the launch traced here: 39.1 us
  starting transfers between devices  15.1 us (38%)
  waiting for transfers between devices  13.2 us (34%)
  Pallas kernels  4.72 us (12%)
  local copies, waits for them, and re-layouts  3.64 us (9%)
  matrix products  1.62 us (4%)
  between operations  0.77 us (2%)
    ppermute x2, waiting for transfers between devices, exchange(): from_above = lax.ppermute(lower_half, axis, down)  11.3 us
    ppermute x2, starting transfers between devices, exchange(): from_below = lax.ppermute(upper_half, axis, up)  10.6 us
    ppermute x2, starting transfers between devices, exchange(): from_above = lax.ppermute(lower_half, axis, down)  4.46 us
    unnamed x14, local copies, waits for them, and re-layouts  2.98 us
    pallas_call x1, Pallas kernels, y_pass(): pl.pallas_call(functools.partial(y_pass_kernel, places=tuple(places)), ou...  2.42 us
    pallas_call x1, Pallas kernels, x_pass(): pl.pallas_call(functools.partial(x_pass_kernel, taps=taps, places=tuple(p...  2.31 us
    ppermute x2, waiting for transfers between devices, exchange(): from_below = lax.ppermute(upper_half, axis, up)  1.94 us
    dot_general x1, matrix products, per_device(): jnp.einsum('xyz,bzk->xbyk', velocity, jnp.asarray(z_maps), precision=EXACT)  1.62 us
  transfers between devices with their start and end apart: 4, of which 4 were waited for; matrix products, arithmetic and copies ran while one was open for 2% of the time, Pallas kernels for 0%

profile of v8, /device:TPU:503, one launch (start us, length us, event | category | flops | bytes accessed | tf_op | source)
XLA Modules:
  0.0 39.1 jit_solution(2296472484744903940)
XLA Ops:
  0.6 0.0 copy-start
  0.6 0.9 %copy-done = f32[16,16,256]{2,1,0:T(8,128)S(1)} copy-done((f32[16,16,256]{2,1,0:T(8,128)S(1)}, f32[16,16,256]{2,1,0:T(8,128)}, u32[]{:S(2)}) %copy-start) | copy-done | bytes 262168
  1.6 1.6 %fusion = f32[3,128,16,16]{1,3,2,0:T(8,128)S(1)} fusion(f32[3,256,128,1]{2,1,3,0:T(8,128)} %constant.34, f32[16,16,256]{2,1,0:T(8,128)S(1)} %copy-done), kind=kOutput, calls=%fused_computation | convolution fusion | flops 301989888 | bytes 1048576 | tf_op jit(solution)/shard_map/xyz,bzk->xbyk/dot_general | solution.py:245
  3.2 0.0 copy-start.1
  3.3 0.7 %copy-done.1 = f32[3,128,16,16]{1,3,2,0:T(8,128)} copy-done((f32[3,128,16,16]{1,3,2,0:T(8,128)}, f32[3,128,16,16]{1,3,2,0:T(8,128)S(1)}, u32[]{:S(2)}) %copy-start.1) | copy-done | bytes 393240
  4.0 2.7 %collective-permute-start = (f32[320,128]{1,0:T(8,128)S(1)}, f32[320,128]{1,0:T(8,128)S(1)}, u32[]{:S(2)}, u32[]{:S(2)}) collective-permute-start(f32[320,128]{1,0:T(8,128)S(1)} %pad_maximum_fusion), channel_id=1, source_target_pairs={{0,1},{1,2},{2,3},{3,4},{4,5},{5,6},{6,7},{7,8},{8,9},{9,10},{10,1... | collective-permute-start | bytes 491528 | tf_op jit(solution)/shard_map/ppermute | solution.py:83
  6.7 0.0 copy-start.6
  6.8 2.5 %collective-permute-start.1 = (f32[320,128]{1,0:T(8,128)S(1)}, f32[320,128]{1,0:T(8,128)S(1)}, u32[]{:S(2)}, u32[]{:S(2)}) collective-permute-start(f32[320,128]{1,0:T(8,128)S(1)} %pad_maximum_fusion.1), channel_id=1, source_target_pairs={{1,0},{2,1},{3,2},{4,3},{5,4},{6,5},{7,6},{8,7},{9,8},{10,9},{11,1... | collective-permute-start | bytes 491528 | tf_op jit(solution)/shard_map/ppermute | solution.py:84
  9.3 0.0 copy-done.6
  9.3 0.6 %dynamic-slice_bitcast_fusion = (f32[48,128]{1,0:T(8,128)}, f32[48,128]{1,0:T(8,128)}) fusion(f32[3,48,128]{2,1,0:T(8,128)S(1)} %copy-done.6, s32[]{:T(128)S(6)} %select_n.20, s32[]{:T(128)S(6)} %select_n.18), kind=kLoop, calls=%fused_computation.4 | loop fusion | bytes 98312 | tf_op jit(solution)/shard_map/jit(dynamic_index_in_dim)/squeeze | solution.py:258
  10.0 1.0 %collective-permute-done.below_ref = f32[320,128]{1,0:T(8,128)S(1)} collective-permute-done((f32[320,128]{1,0:T(8,128)S(1)}, f32[320,128]{1,0:T(8,128)S(1)}, u32[]{:S(2)}, u32[]{:S(2)}) %collective-permute-start) | collective-permute-done | bytes 163872 | tf_op jit(solution)/shard_map/ppermute | solution.py:83
  10.9 0.0 copy-start.4
  10.9 5.8 %collective-permute-done.1.above_ref = f32[320,128]{1,0:T(8,128)S(1)} collective-permute-done((f32[320,128]{1,0:T(8,128)S(1)}, f32[320,128]{1,0:T(8,128)S(1)}, u32[]{:S(2)}, u32[]{:S(2)}) %collective-permute-start.1) | collective-permute-done | bytes 163872 | tf_op jit(solution)/shard_map/ppermute | solution.py:84
  16.7 0.0 copy-start.5
  16.7 0.0 copy-done.4
  16.7 0.7 %copy-done.5 = f32[320,128]{1,0:T(8,128)} copy-done((f32[320,128]{1,0:T(8,128)}, f32[320,128]{1,0:T(8,128)S(1)}, u32[]{:S(2)}) %copy-start.5) | copy-done | bytes 163864
  17.4 2.3 %shard_map.58 = (f32[512,128]{1,0:T(8,128)}, f32[128,128]{1,0:T(8,128)}, f32[384,128]{1,0:T(8,128)}, f32[384,128]{1,0:T(8,128)}) custom-call(f32[768,128]{1,0:T(8,128)} %bitcast.21, f32[320,128]{1,0:T(8,128)} %copy-done.4, f32[320,128]{1,0:T(8,128)} %copy-done.5, f32[48,128]{1,0:T(8,128)} %get-tuple-element.16.maps_ref), custom_call_target="tpu_custom_call" | custom-call | tf_op jit(solution)/shard_map/pallas_call | solution.py:226
  19.7 7.9 %collective-permute-start.2 = (f32[384,128]{1,0:T(8,128)}, f32[384,128]{1,0:T(8,128)S(1)}, u32[]{:S(2)}, u32[]{:S(2)}) collective-permute-start(f32[384,128]{1,0:T(8,128)} %get-tuple-element.9), channel_id=1, source_target_pairs={{0,64},{64,128},{128,192},{192,256},{256,320},{320,384},{384,448},... | collective-permute-start | bytes 589832 | tf_op jit(solution)/shard_map/ppermute | solution.py:83
  27.6 1.9 %collective-permute-start.3 = (f32[384,128]{1,0:T(8,128)}, f32[384,128]{1,0:T(8,128)S(1)}, u32[]{:S(2)}, u32[]{:S(2)}) collective-permute-start(f32[384,128]{1,0:T(8,128)} %get-tuple-element.10), channel_id=1, source_target_pairs={{64,0},{128,64},{192,128},{256,192},{320,256},{384,320},{448,384},... | collective-permute-start | bytes 589832 | tf_op jit(solution)/shard_map/ppermute | solution.py:84
  29.5 1.0 %collective-permute-done.2.below_ref = f32[384,128]{1,0:T(8,128)S(1)} collective-permute-done((f32[384,128]{1,0:T(8,128)}, f32[384,128]{1,0:T(8,128)S(1)}, u32[]{:S(2)}, u32[]{:S(2)}) %collective-permute-start.2) | collective-permute-done | bytes 196640 | tf_op jit(solution)/shard_map/ppermute | solution.py:83
  30.5 0.0 copy-start.2
  30.5 5.5 %collective-permute-done.3.above_ref = f32[384,128]{1,0:T(8,128)S(1)} collective-permute-done((f32[384,128]{1,0:T(8,128)}, f32[384,128]{1,0:T(8,128)S(1)}, u32[]{:S(2)}, u32[]{:S(2)}) %collective-permute-start.3) | collective-permute-done | bytes 196640 | tf_op jit(solution)/shard_map/ppermute | solution.py:84
  36.0 0.0 copy-start.3
  36.0 0.0 copy-done.2
  36.0 0.7 %copy-done.3 = f32[384,128]{1,0:T(8,128)} copy-done((f32[384,128]{1,0:T(8,128)}, f32[384,128]{1,0:T(8,128)S(1)}, u32[]{:S(2)}) %copy-start.3) | copy-done | bytes 196632
  36.7 2.4 %shard_map.59 = (f32[4,4,64]{2,1,0:T(4,128)}, f32[7,4,4,64]{3,2,1,0:T(4,128)}, f32[7,8,8,128]{3,2,1,0:T(8,128)}) custom-call(f32[512,128]{1,0:T(8,128)} %get-tuple-element.7.one_ref, f32[128,128]{1,0:T(8,128)} %get-tuple-element.8.two_ref, f32[384,128]{1,0:T(8,128)} %copy-done.2, f32[384,128]{1,0:T(8,128)} %copy-done.3, f32[48,128]{1,0:T(8,128)} %get-tuple-element.15.maps_ref), custom_call_target="tpu_custom_call" | custom-call | tf_op jit(solution)/shard_map/pallas_call | solution.py:152
  (6 shorter events, 0.1 us)
Async XLA Ops:
  0.6 1.0 %copy-start = (f32[16,16,256]{2,1,0:T(8,128)S(1)}, f32[16,16,256]{2,1,0:T(8,128)}, u32[]{:S(2)}) copy-start(f32[16,16,256]{2,1,0:T(8,128)} %param.3) | copy-start | bytes 786436
  3.2 0.7 %copy-start.1 = (f32[3,128,16,16]{1,3,2,0:T(8,128)}, f32[3,128,16,16]{1,3,2,0:T(8,128)S(1)}, u32[]{:S(2)}) copy-start(f32[3,128,16,16]{1,3,2,0:T(8,128)S(1)} %fusion) | copy-start | bytes 1179652
  4.0 7.0 %collective-permute-start = (f32[320,128]{1,0:T(8,128)S(1)}, f32[320,128]{1,0:T(8,128)S(1)}, u32[]{:S(2)}, u32[]{:S(2)}) collective-permute-start(f32[320,128]{1,0:T(8,128)S(1)} %pad_maximum_fusion), channel_id=1, source_target_pairs={{0,1},{1,2},{2,3},{3,4},{4,5},{5,6},{6,7},{7,8},{8,9},{9,10},{10,1... | collective-permute-start | bytes 491528 | tf_op jit(solution)/shard_map/ppermute | solution.py:83
  6.7 2.6 %copy-start.6 = (f32[3,48,128]{2,1,0:T(8,128)S(1)}, f32[3,48,128]{2,1,0:T(8,128)}, u32[]{:S(2)}) copy-start(f32[3,48,128]{2,1,0:T(8,128)} %constant.32.clone) | copy-start | bytes 221188
  6.8 10.0 %collective-permute-start.1 = (f32[320,128]{1,0:T(8,128)S(1)}, f32[320,128]{1,0:T(8,128)S(1)}, u32[]{:S(2)}, u32[]{:S(2)}) collective-permute-start(f32[320,128]{1,0:T(8,128)S(1)} %pad_maximum_fusion.1), channel_id=1, source_target_pairs={{1,0},{2,1},{3,2},{4,3},{5,4},{6,5},{7,6},{8,7},{9,8},{10,9},{11,1... | collective-permute-start | bytes 491528 | tf_op jit(solution)/shard_map/ppermute | solution.py:84
  10.9 5.8 %copy-start.4 = (f32[320,128]{1,0:T(8,128)}, f32[320,128]{1,0:T(8,128)S(1)}, u32[]{:S(2)}) copy-start(f32[320,128]{1,0:T(8,128)S(1)} %collective-permute-done.below_ref) | copy-start | bytes 491524
  16.7 0.7 %copy-start.5 = (f32[320,128]{1,0:T(8,128)}, f32[320,128]{1,0:T(8,128)S(1)}, u32[]{:S(2)}) copy-start(f32[320,128]{1,0:T(8,128)S(1)} %collective-permute-done.1.above_ref) | copy-start | bytes 491524
  19.7 10.8 %collective-permute-start.2 = (f32[384,128]{1,0:T(8,128)}, f32[384,128]{1,0:T(8,128)S(1)}, u32[]{:S(2)}, u32[]{:S(2)}) collective-permute-start(f32[384,128]{1,0:T(8,128)} %get-tuple-element.9), channel_id=1, source_target_pairs={{0,64},{64,128},{128,192},{192,256},{256,320},{320,384},{384,448},... | collective-permute-start | bytes 589832 | tf_op jit(solution)/shard_map/ppermute | solution.py:83
  27.6 8.4 %collective-permute-start.3 = (f32[384,128]{1,0:T(8,128)}, f32[384,128]{1,0:T(8,128)S(1)}, u32[]{:S(2)}, u32[]{:S(2)}) collective-permute-start(f32[384,128]{1,0:T(8,128)} %get-tuple-element.10), channel_id=1, source_target_pairs={{64,0},{128,64},{192,128},{256,192},{320,256},{384,320},{448,384},... | collective-permute-start | bytes 589832 | tf_op jit(solution)/shard_map/ppermute | solution.py:84
  30.5 5.5 %copy-start.2 = (f32[384,128]{1,0:T(8,128)}, f32[384,128]{1,0:T(8,128)S(1)}, u32[]{:S(2)}) copy-start(f32[384,128]{1,0:T(8,128)S(1)} %collective-permute-done.2.below_ref) | copy-start | bytes 589828
  36.0 0.7 %copy-start.3 = (f32[384,128]{1,0:T(8,128)}, f32[384,128]{1,0:T(8,128)S(1)}, u32[]{:S(2)}) copy-start(f32[384,128]{1,0:T(8,128)S(1)} %collective-permute-done.3.above_ref) | copy-start | bytes 589828

commit v9 on v7

--- a/solution.py
+++ b/solution.py
@@ -244,12 +244,15 @@
     u = jnp.einsum("xyz,bzk->xbyk", velocity, jnp.asarray(z_maps), precision=EXACT)
 
     wide = 12
-    one_rows = u[:, 0:2]
-    two_rows = u[:, 2]
+    below_raw, above_raw = exchange(velocity[:wide], velocity[nx - wide :], "slab")
     flat = lambda a: a.reshape(-1, lanes)
-    top = jnp.concatenate([flat(one_rows[nx - 4 :]), flat(two_rows[nx - wide :])])
-    bottom = jnp.concatenate([flat(one_rows[:4]), flat(two_rows[:wide])])
-    below, above = exchange(bottom, top, "slab")
+    near = jnp.stack([below_raw[wide - 4 :], above_raw[:4]])
+    halo_one = jnp.einsum("hxyz,bzk->hxbyk", near, jnp.asarray(z_maps[0:2]), precision=EXACT)
+    halo_two = jnp.einsum(
+        "hxyz,zk->hxyk", jnp.stack([below_raw, above_raw]), jnp.asarray(z_maps[2]), precision=EXACT
+    )
+    below = jnp.concatenate([flat(halo_one[0]), flat(halo_two[0])])
+    above = jnp.concatenate([flat(halo_one[1]), flat(halo_two[1])])
     assert nx == ny and wide == 12
     table, places = packed_maps(nx)
     table = jnp.asarray(table)

time: 38.7 us -> 39.7 us (1.026)
  other arithmetic: 0.03 us -> 0.76 us
  local copies, waits for them, and re-layouts: 3.81 us -> 4.24 us
    slice x4 -> x3, local copies, waits for them, and re-layouts: 0.04 us -> 1.14 us  [the longest x1 1.11 us: per_device(): velocity[nx - wide:]]
    dot_general x1, matrix products: 1.62 us -> 0.61 us  [per_device(): jnp.einsum('xyz,bzk->xbyk', velocity, jnp.asarray(z_maps), precision=EXACT)]
    dot_general x0 -> x2, matrix products: none -> 0.76 us  [the longest x1 0.48 us: per_device(): jnp.einsum('hxyz,zk->hxyk', jnp.stack([below_raw, above_raw]), jnp.asarra...]
    concatenate x2 -> x1, other arithmetic: 0.03 us -> 0.76 us  [per_device(): below = jnp.concatenate([flat(halo_one[0]), flat(halo_two[0])])]
    unnamed x12 -> x14, local copies, waits for them, and re-layouts: 2.39 us -> 1.69 us
  transfers between devices with their start and end apart: 4 -> 4, of which waited for: 4 -> 4; matrix products, arithmetic and copies ran while one was open for 4% -> 5% of each run, Pallas kernels for 0% -> 0%
where the time goes in v9:
time: 39.7 us; the launch traced here: 39.4 us
  starting transfers between devices  15.1 us (38%)
  waiting for transfers between devices  12.4 us (31%)
  Pallas kernels  4.72 us (12%)
  local copies, waits for them, and re-layouts  4.24 us (11%)
  matrix products  1.37 us (3%)
  between operations  0.8 us (2%)
  other arithmetic  0.76 us (2%)
    ppermute x2, waiting for transfers between devices, exchange(): from_above = lax.ppermute(lower_half, axis, down)  11.2 us
    ppermute x2, starting transfers between devices, exchange(): from_below = lax.ppermute(upper_half, axis, up)  10.6 us
    ppermute x2, starting transfers between devices, exchange(): from_above = lax.ppermute(lower_half, axis, down)  4.46 us
    pallas_call x1, Pallas kernels, y_pass(): pl.pallas_call(functools.partial(y_pass_kernel, places=tuple(places)), ou...  2.42 us
    pallas_call x1, Pallas kernels, x_pass(): pl.pallas_call(functools.partial(x_pass_kernel, taps=taps, places=tuple(p...  2.31 us
    unnamed x14, local copies, waits for them, and re-layouts  1.69 us
    ppermute x2, waiting for transfers between devices, exchange(): from_below = lax.ppermute(upper_half, axis, up)  1.18 us
    slice x1, local copies, waits for them, and re-layouts, per_device(): velocity[nx - wide:]  1.11 us
  transfers between devices with their start and end apart: 4, of which 4 were waited for; matrix products, arithmetic and copies ran while one was open for 5% of the time, Pallas kernels for 0%

profile of v9, /device:TPU:503, one launch (start us, length us, event | category | flops | bytes accessed | tf_op | source)
XLA Modules:
  0.0 39.4 jit_solution(15184719499728339166)
XLA Ops:
  0.6 0.0 copy-start.1
  0.6 0.0 copy-start
  0.7 1.1 %fusion.9 = (f32[12,16,256]{2,1,0:T(8,128)S(1)}, f32[12,16,256]{2,1,0:T(8,128)S(1)}) fusion(f32[16,16,256]{2,1,0:T(8,128)} %param.5), kind=kLoop, calls=%fused_computation.18 | loop fusion | bytes 786432 | tf_op jit(solution)/shard_map/slice | solution.py:247
  1.8 2.7 %collective-permute-start = (f32[12,16,256]{2,1,0:T(8,128)S(1)}, f32[12,16,256]{2,1,0:T(8,128)S(1)}, u32[]{:S(2)}, u32[]{:S(2)}) collective-permute-start(f32[12,16,256]{2,1,0:T(8,128)S(1)} %get-tuple-element.11), channel_id=1, source_target_pairs={{0,1},{1,2},{2,3},{3,4},{4,5},{5,6},{6,7},{7,8},{8,9},{9,10},{10,1... | collective-permute-start | bytes 589832 | tf_op jit(solution)/shard_map/ppermute | solution.py:83
  4.5 2.5 %collective-permute-start.1 = (f32[12,16,256]{2,1,0:T(8,128)S(1)}, f32[12,16,256]{2,1,0:T(8,128)S(1)}, u32[]{:S(2)}, u32[]{:S(2)}) collective-permute-start(f32[12,16,256]{2,1,0:T(8,128)S(1)} %get-tuple-element.12), channel_id=1, source_target_pairs={{1,0},{2,1},{3,2},{4,3},{5,4},{6,5},{7,6},{8,7},{9,8},{10,9},{11,1... | collective-permute-start | bytes 589832 | tf_op jit(solution)/shard_map/ppermute | solution.py:84
  7.1 0.0 copy-done.1
  7.1 0.0 copy-done
  7.1 0.6 %convolution_bitcast_fusion = f32[16,3,16,128]{3,2,0,1:T(8,128)S(1)} fusion(f32[3,256,128,1]{2,1,3,0:T(8,128)S(1)} %copy-done.1, f32[16,16,256]{2,1,0:T(8,128)S(1)} %copy-done), kind=kOutput, calls=%fused_computation | convolution fusion | flops 301989888 | bytes 1048576 | tf_op jit(solution)/shard_map/xyz,bzk->xbyk/dot_general | solution.py:244
  7.7 0.0 copy-start.6
  7.7 0.0 copy-start.5
  7.7 0.8 %copy.8 = f32[16,3,16,128]{3,2,1,0:T(8,128)} copy(f32[16,3,16,128]{3,2,0,1:T(8,128)S(1)} %convolution_bitcast_fusion) | data formatting | bytes 786432 | tf_op jit(solution)/shard_map/xyz,bzk->xbyk/transpose | solution.py:244
  8.5 0.1 copy-done.6
  8.6 0.6 %dynamic-slice_bitcast_fusion = (f32[48,128]{1,0:T(8,128)}, f32[48,128]{1,0:T(8,128)}) fusion(f32[3,48,128]{2,1,0:T(8,128)S(1)} %copy-done.6, s32[]{:T(128)S(6)} %select_n.20, s32[]{:T(128)S(6)} %select_n.18), kind=kLoop, calls=%fused_computation.14 | loop fusion | bytes 98312 | tf_op jit(solution)/shard_map/jit(dynamic_index_in_dim)/squeeze | solution.py:260
  9.2 0.2 collective-permute-done
  9.4 5.7 %collective-permute-done.1 = f32[12,16,256]{2,1,0:T(8,128)S(1)} collective-permute-done((f32[12,16,256]{2,1,0:T(8,128)S(1)}, f32[12,16,256]{2,1,0:T(8,128)S(1)}, u32[]{:S(2)}, u32[]{:S(2)}) %collective-permute-start.1) | collective-permute-done | bytes 196640 | tf_op jit(solution)/shard_map/ppermute | solution.py:84
  15.2 0.0 copy-done.5
  15.2 0.5 %fusion = f32[2,12,16,128]{3,2,1,0:T(8,128)S(1)} fusion(f32[256,128,1,1]{1,0,3,2:T(8,128)S(1)} %copy-done.5, f32[1,12,16,256]{3,2,1,0:T(8,128)S(1)} %bitcast.43, f32[1,12,16,256]{3,2,1,0:T(8,128)S(1)} %bitcast.42), kind=kOutput, calls=%fused_computation.2 | convolution fusion | flops 151093248 | bytes 720896 | tf_op jit(solution)/shard_map/hxyz,zk->hxyk/dot_general | solution.py:251
  15.7 0.0 copy-start.2
  15.7 0.9 %copy-done.2 = f32[2,256,128,1,1]{2,1,0,4,3:T(8,128)S(1)} copy-done((f32[2,256,128,1,1]{2,1,0,4,3:T(8,128)S(1)}, f32[2,256,128,1,1]{2,1,0,4,3:T(8,128)}, u32[]{:S(2)}) %copy-start.2) | copy-done | bytes 262168
  16.6 0.3 convolution_bitcast_fusion.1
  16.9 0.8 %pad_maximum_fusion = (f32[320,128]{1,0:T(8,128)}, f32[320,128]{1,0:T(8,128)}) fusion(f32[192,128]{1,0:T(8,128)S(1)} %bitcast.41, f32[128,128]{1,0:T(8,128)S(1)} %bitcast.45, f32[192,128]{1,0:T(8,128)S(1)} %bitcast.40, f32[128,128]{1,0:T(8,128)S(1)} %bitcast.44), kind=kLoop, calls=%fused_computation.7 | loop fusion | flops 81920 | bytes 655360 | tf_op jit(solution)/shard_map/concatenate | solution.py:254
  17.7 2.3 %shard_map.76 = (f32[512,128]{1,0:T(8,128)}, f32[128,128]{1,0:T(8,128)}, f32[384,128]{1,0:T(8,128)}, f32[384,128]{1,0:T(8,128)}) custom-call(f32[768,128]{1,0:T(8,128)} %bitcast.39, f32[320,128]{1,0:T(8,128)} %get-tuple-element.19.below_ref, f32[320,128]{1,0:T(8,128)} %get-tuple-element.20.above_ref, f32[48,128]{1,0:T(8,128)} %get-tuple-element.18.maps_ref), custom_call_target="tpu_custom_call" | custom-call | tf_op jit(solution)/shard_map/pallas_call | solution.py:225
  20.0 7.9 %collective-permute-start.2 = (f32[384,128]{1,0:T(8,128)}, f32[384,128]{1,0:T(8,128)S(1)}, u32[]{:S(2)}, u32[]{:S(2)}) collective-permute-start(f32[384,128]{1,0:T(8,128)} %get-tuple-element.9), channel_id=1, source_target_pairs={{0,64},{64,128},{128,192},{192,256},{256,320},{320,384},{384,448},... | collective-permute-start | bytes 589832 | tf_op jit(solution)/shard_map/ppermute | solution.py:83
  27.9 1.9 %collective-permute-start.3 = (f32[384,128]{1,0:T(8,128)}, f32[384,128]{1,0:T(8,128)S(1)}, u32[]{:S(2)}, u32[]{:S(2)}) collective-permute-start(f32[384,128]{1,0:T(8,128)} %get-tuple-element.10), channel_id=1, source_target_pairs={{64,0},{128,64},{192,128},{256,192},{320,256},{384,320},{448,384},... | collective-permute-start | bytes 589832 | tf_op jit(solution)/shard_map/ppermute | solution.py:84
  29.8 1.0 %collective-permute-done.2.below_ref = f32[384,128]{1,0:T(8,128)S(1)} collective-permute-done((f32[384,128]{1,0:T(8,128)}, f32[384,128]{1,0:T(8,128)S(1)}, u32[]{:S(2)}, u32[]{:S(2)}) %collective-permute-start.2) | collective-permute-done | bytes 196640 | tf_op jit(solution)/shard_map/ppermute | solution.py:83
  30.8 0.0 copy-start.3
  30.8 5.5 %collective-permute-done.3.above_ref = f32[384,128]{1,0:T(8,128)S(1)} collective-permute-done((f32[384,128]{1,0:T(8,128)}, f32[384,128]{1,0:T(8,128)S(1)}, u32[]{:S(2)}, u32[]{:S(2)}) %collective-permute-start.3) | collective-permute-done | bytes 196640 | tf_op jit(solution)/shard_map/ppermute | solution.py:84
  36.3 0.0 copy-start.4
  36.3 0.0 copy-done.3
  36.3 0.7 %copy-done.4 = f32[384,128]{1,0:T(8,128)} copy-done((f32[384,128]{1,0:T(8,128)}, f32[384,128]{1,0:T(8,128)S(1)}, u32[]{:S(2)}) %copy-start.4) | copy-done | bytes 196632
  37.0 2.4 %shard_map.77 = (f32[4,4,64]{2,1,0:T(4,128)}, f32[7,4,4,64]{3,2,1,0:T(4,128)}, f32[7,8,8,128]{3,2,1,0:T(8,128)}) custom-call(f32[512,128]{1,0:T(8,128)} %get-tuple-element.7.one_ref, f32[128,128]{1,0:T(8,128)} %get-tuple-element.8.two_ref, f32[384,128]{1,0:T(8,128)} %copy-done.3, f32[384,128]{1,0:T(8,128)} %copy-done.4, f32[48,128]{1,0:T(8,128)} %get-tuple-element.17.maps_ref), custom_call_target="tpu_custom_call" | custom-call | tf_op jit(solution)/shard_map/pallas_call | solution.py:152
  (4 shorter events, 0.0 us)
Async XLA Ops:
  0.6 6.4 %copy-start.1 = (f32[3,256,128,1]{2,1,3,0:T(8,128)S(1)}, f32[3,256,128,1]{2,1,3,0:T(8,128)}, u32[]{:S(2)}) copy-start(f32[3,256,128,1]{2,1,3,0:T(8,128)} %constant.40) | copy-start | bytes 1179652
  0.6 6.4 %copy-start = (f32[16,16,256]{2,1,0:T(8,128)S(1)}, f32[16,16,256]{2,1,0:T(8,128)}, u32[]{:S(2)}) copy-start(f32[16,16,256]{2,1,0:T(8,128)} %param.5) | copy-start | bytes 786436
  1.8 7.7 %collective-permute-start = (f32[12,16,256]{2,1,0:T(8,128)S(1)}, f32[12,16,256]{2,1,0:T(8,128)S(1)}, u32[]{:S(2)}, u32[]{:S(2)}) collective-permute-start(f32[12,16,256]{2,1,0:T(8,128)S(1)} %get-tuple-element.11), channel_id=1, source_target_pairs={{0,1},{1,2},{2,3},{3,4},{4,5},{5,6},{6,7},{7,8},{8,9},{9,10},{10,1... | collective-permute-start | bytes 589832 | tf_op jit(solution)/shard_map/ppermute | solution.py:83
  4.5 10.7 %collective-permute-start.1 = (f32[12,16,256]{2,1,0:T(8,128)S(1)}, f32[12,16,256]{2,1,0:T(8,128)S(1)}, u32[]{:S(2)}, u32[]{:S(2)}) collective-permute-start(f32[12,16,256]{2,1,0:T(8,128)S(1)} %get-tuple-element.12), channel_id=1, source_target_pairs={{1,0},{2,1},{3,2},{4,3},{5,4},{6,5},{7,6},{8,7},{9,8},{10,9},{11,1... | collective-permute-start | bytes 589832 | tf_op jit(solution)/shard_map/ppermute | solution.py:84
  7.7 0.9 %copy-start.6 = (f32[3,48,128]{2,1,0:T(8,128)S(1)}, f32[3,48,128]{2,1,0:T(8,128)}, u32[]{:S(2)}) copy-start(f32[3,48,128]{2,1,0:T(8,128)} %constant.38.clone) | copy-start | bytes 221188
  7.7 7.4 %copy-start.5 = (f32[256,128,1,1]{1,0,3,2:T(8,128)S(1)}, f32[256,128,1,1]{1,0,3,2:T(8,128)}, u32[]{:S(2)}) copy-start(f32[256,128,1,1]{1,0,3,2:T(8,128)} %constant.42) | copy-start | bytes 393220
  15.7 1.0 %copy-start.2 = (f32[2,256,128,1,1]{2,1,0,4,3:T(8,128)S(1)}, f32[2,256,128,1,1]{2,1,0,4,3:T(8,128)}, u32[]{:S(2)}) copy-start(f32[2,256,128,1,1]{2,1,0,4,3:T(8,128)} %constant.41) | copy-start | bytes 786436
  20.0 10.8 %collective-permute-start.2 = (f32[384,128]{1,0:T(8,128)}, f32[384,128]{1,0:T(8,128)S(1)}, u32[]{:S(2)}, u32[]{:S(2)}) collective-permute-start(f32[384,128]{1,0:T(8,128)} %get-tuple-element.9), channel_id=1, source_target_pairs={{0,64},{64,128},{128,192},{192,256},{256,320},{320,384},{384,448},... | collective-permute-start | bytes 589832 | tf_op jit(solution)/shard_map/ppermute | solution.py:83
  27.9 8.4 %collective-permute-start.3 = (f32[384,128]{1,0:T(8,128)}, f32[384,128]{1,0:T(8,128)S(1)}, u32[]{:S(2)}, u32[]{:S(2)}) collective-permute-start(f32[384,128]{1,0:T(8,128)} %get-tuple-element.10), channel_id=1, source_target_pairs={{64,0},{128,64},{192,128},{256,192},{320,256},{384,320},{448,384},... | collective-permute-start | bytes 589832 | tf_op jit(solution)/shard_map/ppermute | solution.py:84
  30.8 5.5 %copy-start.3 = (f32[384,128]{1,0:T(8,128)}, f32[384,128]{1,0:T(8,128)S(1)}, u32[]{:S(2)}) copy-start(f32[384,128]{1,0:T(8,128)S(1)} %collective-permute-done.2.below_ref) | copy-start | bytes 589828
  36.3 0.7 %copy-start.4 = (f32[384,128]{1,0:T(8,128)}, f32[384,128]{1,0:T(8,128)S(1)}, u32[]{:S(2)}) copy-start(f32[384,128]{1,0:T(8,128)S(1)} %collective-permute-done.3.above_ref) | copy-start | bytes 589828

commit v10 on v9

--- a/solution.py
+++ b/solution.py
@@ -161,30 +161,30 @@
     )(x_one.reshape(-1, lanes), x_two.reshape(-1, lanes), below, above, y_maps)
 
 
-def x_pass_kernel(own_ref, below_ref, above_ref, maps_ref, one_out, two_out, top_out, bottom_out, *,
+def x_pass_kernel(own_ref, near_ref, far_ref, maps_ref, one_out, two_out, top_out, bottom_out, *,
                   taps, places, bands):
     ny = two_out.shape[0] // len(taps[1])
     slab = 2 * ny
     stride = bands * ny
     lo1, lo2 = 4, 12
-    split = lo1 * slab
+    side_one, side_two = lo1 * slab, lo2 * ny
 
     def one_slab(i):
         if i < lo1:
-            return below_ref[i * slab : (i + 1) * slab, :]
+            return near_ref[i * slab : (i + 1) * slab, :]
         if i < lo1 + ny:
             return own_ref[(i - lo1) * stride : (i - lo1) * stride + slab, :]
         j = i - lo1 - ny
-        return above_ref[j * slab : (j + 1) * slab, :]
+        return near_ref[side_one + j * slab : side_one + (j + 1) * slab, :]
 
     def two_slab(i):
         if i < lo2:
-            return below_ref[split + i * ny : split + (i + 1) * ny, :]
+            return far_ref[i * ny : (i + 1) * ny, :]
         if i < lo2 + ny:
             at = (i - lo2) * stride + slab
             return own_ref[at : at + ny, :]
         j = i - lo2 - ny
-        return above_ref[split + j * ny : split + (j + 1) * ny, :]
+        return far_ref[side_two + j * ny : side_two + (j + 1) * ny, :]
 
     narrow = (top_out.shape[0] - two_out.shape[0]) // (len(taps[0]) * 2)
     row1 = places[0][0]
@@ -215,7 +215,7 @@
     return tuple(tuple(int(i) for i in np.nonzero(row)[0]) for row in present)
 
 
-def x_pass(u, below, above, x_maps, places, nx, ny):
+def x_pass(u, near, far, x_maps, places, nx, ny):
     lanes = u.shape[-1]
     taps = (used_taps(window_maps(nx, (4, 4), 0)), used_taps(window_maps(nx, (12, 12), 1)))
     narrow = 8
@@ -232,7 +232,7 @@
         ),
         in_specs=[vmem, vmem, vmem, smem],
         out_specs=(vmem, vmem, vmem, vmem),
-    )(u.reshape(-1, lanes), below, above, x_maps)
+    )(u.reshape(-1, lanes), near.reshape(-1, lanes), far.reshape(-1, lanes), x_maps)
 
 
 def per_device(velocity):
@@ -251,14 +251,12 @@
     halo_two = jnp.einsum(
         "hxyz,zk->hxyk", jnp.stack([below_raw, above_raw]), jnp.asarray(z_maps[2]), precision=EXACT
     )
-    below = jnp.concatenate([flat(halo_one[0]), flat(halo_two[0])])
-    above = jnp.concatenate([flat(halo_one[1]), flat(halo_two[1])])
     assert nx == ny and wide == 12
     table, places = packed_maps(nx)
     table = jnp.asarray(table)
     x_maps = lax.dynamic_index_in_dim(table, case_of("slab"), keepdims=False)
     y_maps = lax.dynamic_index_in_dim(table, case_of("morton"), keepdims=False)
-    x_one, x_two, top, bottom = x_pass(u, below, above, x_maps, places, nx, ny)
+    x_one, x_two, top, bottom = x_pass(u, halo_one, halo_two, x_maps, places, nx, ny)
 
     below, above = exchange(bottom, top, "morton")
     return y_pass(x_one, x_two, below, above, y_maps, places, nx, ny, nz)

time: 39.7 us -> 39.3 us (0.990)
  matrix products: 1.37 us -> 2.7 us
  local copies, waits for them, and re-layouts: 4.24 us -> 3.31 us
  other arithmetic: 0.76 us -> 0 us
    unnamed x14, local copies, waits for them, and re-layouts: 1.69 us -> 0.8 us
    concatenate x1 -> x0, other arithmetic: 0.76 us -> none  [per_device(): below = jnp.concatenate([flat(halo_one[0]), flat(halo_two[0])])]
    dot_general x1, matrix products: 0.48 us -> 1.15 us  [per_device(): jnp.einsum('hxyz,zk->hxyk', jnp.stack([below_raw, above_raw]), jnp.asarra...]
    dot_general x1, matrix products: 0.28 us -> 0.93 us  [per_device(): jnp.einsum('hxyz,bzk->hxbyk', near, jnp.asarray(z_maps[0:2]), precision=E...]
where the time goes in v10:
time: 39.3 us; the launch traced here: 39 us
  starting transfers between devices  15.1 us (38%)
  waiting for transfers between devices  12.4 us (32%)
  Pallas kernels  4.74 us (12%)
  local copies, waits for them, and re-layouts  3.31 us (8%)
  matrix products  2.7 us (7%)
  between operations  0.76 us (2%)
    ppermute x2, waiting for transfers between devices, exchange(): from_above = lax.ppermute(lower_half, axis, down)  11.2 us
    ppermute x2, starting transfers between devices, exchange(): from_below = lax.ppermute(upper_half, axis, up)  10.6 us
    ppermute x2, starting transfers between devices, exchange(): from_above = lax.ppermute(lower_half, axis, down)  4.46 us
    pallas_call x1, Pallas kernels, y_pass(): pl.pallas_call(functools.partial(y_pass_kernel, places=tuple(places)), ou...  2.41 us
    pallas_call x1, Pallas kernels, x_pass(): pl.pallas_call(functools.partial(x_pass_kernel, taps=taps, places=tuple(p...  2.33 us
    ppermute x2, waiting for transfers between devices, exchange(): from_below = lax.ppermute(upper_half, axis, up)  1.18 us
    dot_general x1, matrix products, per_device(): jnp.einsum('hxyz,zk->hxyk', jnp.stack([below_raw, above_raw]), jnp.asarra...  1.15 us
    slice x1, local copies, waits for them, and re-layouts, per_device(): velocity[nx - wide:]  1.11 us
  transfers between devices with their start and end apart: 4, of which 4 were waited for; matrix products, arithmetic and copies ran while one was open for 5% of the time, Pallas kernels for 0%

profile of v10, /device:TPU:503, one launch (start us, length us, event | category | flops | bytes accessed | tf_op | source)
XLA Modules:
  0.0 39.0 jit_solution(9522888407917338301)
XLA Ops:
  0.6 0.0 copy-start.1
  0.6 0.0 copy-start
  0.7 1.1 %fusion.10 = (f32[12,16,256]{2,1,0:T(8,128)S(1)}, f32[12,16,256]{2,1,0:T(8,128)S(1)}) fusion(f32[16,16,256]{2,1,0:T(8,128)} %param.5), kind=kLoop, calls=%fused_computation.16 | loop fusion | bytes 786432 | tf_op jit(solution)/shard_map/slice | solution.py:247
  1.8 2.7 %collective-permute-start = (f32[12,16,256]{2,1,0:T(8,128)S(1)}, f32[12,16,256]{2,1,0:T(8,128)S(1)}, u32[]{:S(2)}, u32[]{:S(2)}) collective-permute-start(f32[12,16,256]{2,1,0:T(8,128)S(1)} %get-tuple-element.11), channel_id=1, source_target_pairs={{0,1},{1,2},{2,3},{3,4},{4,5},{5,6},{6,7},{7,8},{8,9},{9,10},{10,1... | collective-permute-start | bytes 589832 | tf_op jit(solution)/shard_map/ppermute | solution.py:83
  4.5 2.5 %collective-permute-start.1 = (f32[12,16,256]{2,1,0:T(8,128)S(1)}, f32[12,16,256]{2,1,0:T(8,128)S(1)}, u32[]{:S(2)}, u32[]{:S(2)}) collective-permute-start(f32[12,16,256]{2,1,0:T(8,128)S(1)} %get-tuple-element.12), channel_id=1, source_target_pairs={{1,0},{2,1},{3,2},{4,3},{5,4},{6,5},{7,6},{8,7},{9,8},{10,9},{11,1... | collective-permute-start | bytes 589832 | tf_op jit(solution)/shard_map/ppermute | solution.py:84
  7.1 0.0 copy-done.1
  7.1 0.0 copy-done
  7.1 0.6 %convolution_bitcast_fusion = f32[16,3,16,128]{3,2,0,1:T(8,128)S(1)} fusion(f32[3,256,128,1]{2,1,3,0:T(8,128)S(1)} %copy-done.1, f32[16,16,256]{2,1,0:T(8,128)S(1)} %copy-done), kind=kOutput, calls=%fused_computation | convolution fusion | flops 301989888 | bytes 1048576 | tf_op jit(solution)/shard_map/xyz,bzk->xbyk/dot_general | solution.py:244
  7.7 0.0 copy-start.6
  7.7 0.0 copy-start.5
  7.7 0.8 %copy.8 = f32[16,3,16,128]{3,2,1,0:T(8,128)} copy(f32[16,3,16,128]{3,2,0,1:T(8,128)S(1)} %convolution_bitcast_fusion) | data formatting | bytes 786432 | tf_op jit(solution)/shard_map/xyz,bzk->xbyk/transpose | solution.py:244
  8.5 0.1 copy-done.6
  8.6 0.6 %dynamic-slice_bitcast_fusion = (f32[48,128]{1,0:T(8,128)}, f32[48,128]{1,0:T(8,128)}) fusion(f32[3,48,128]{2,1,0:T(8,128)S(1)} %copy-done.6, s32[]{:T(128)S(6)} %select_n.20, s32[]{:T(128)S(6)} %select_n.18), kind=kLoop, calls=%fused_computation.12 | loop fusion | bytes 98312 | tf_op jit(solution)/shard_map/jit(dynamic_index_in_dim)/squeeze | solution.py:258
  9.2 0.2 collective-permute-done
  9.4 5.7 %collective-permute-done.1 = f32[12,16,256]{2,1,0:T(8,128)S(1)} collective-permute-done((f32[12,16,256]{2,1,0:T(8,128)S(1)}, f32[12,16,256]{2,1,0:T(8,128)S(1)}, u32[]{:S(2)}, u32[]{:S(2)}) %collective-permute-start.1) | collective-permute-done | bytes 196640 | tf_op jit(solution)/shard_map/ppermute | solution.py:84
  15.2 0.0 copy-done.5
  15.2 0.0 copy-start.2
  15.2 1.2 %fusion = f32[2,12,16,128]{3,2,1,0:T(8,128)} fusion(f32[256,128,1,1]{1,0,3,2:T(8,128)S(1)} %copy-done.5, f32[1,12,16,256]{3,2,1,0:T(8,128)S(1)} %bitcast.41, f32[1,12,16,256]{3,2,1,0:T(8,128)S(1)} %bitcast.40), kind=kOutput, calls=%fused_computation.1 | convolution fusion | flops 151093248 | bytes 720896 | tf_op jit(solution)/shard_map/hxyz,zk->hxyk/dot_general | solution.py:251
  16.4 0.0 copy-done.2
  16.4 0.9 %fusion.5 = f32[2,4,16,2,128]{4,2,3,1,0:T(8,128)} fusion(f32[2,256,128,1,1]{2,1,0,4,3:T(8,128)S(1)} %copy-done.2, f32[1,4,16,256]{3,2,1,0:T(8,128)S(1)} %slice_bitcast_fusion, f32[1,4,16,256]{3,2,1,0:T(8,128)S(1)} %slice_bitcast_fusion.1), kind=kOutput, calls=%fused_computation.7 | convolution fusion | flops 100696064 | bytes 524288 | tf_op jit(solution)/shard_map/hxyz,bzk->hxbyk/dot_general | solution.py:250
  17.3 2.3 %shard_map.76 = (f32[512,128]{1,0:T(8,128)}, f32[128,128]{1,0:T(8,128)}, f32[384,128]{1,0:T(8,128)}, f32[384,128]{1,0:T(8,128)}) custom-call(f32[768,128]{1,0:T(8,128)} %bitcast.37, f32[256,128]{1,0:T(8,128)} %bitcast.39, f32[384,128]{1,0:T(8,128)} %bitcast.38, f32[48,128]{1,0:T(8,128)} %get-tuple-element.14.maps_ref), custom_call_target="tpu_custom_call" | custom-call | tf_op jit(solution)/shard_map/pallas_call | solution.py:225
  19.6 7.9 %collective-permute-start.2 = (f32[384,128]{1,0:T(8,128)}, f32[384,128]{1,0:T(8,128)S(1)}, u32[]{:S(2)}, u32[]{:S(2)}) collective-permute-start(f32[384,128]{1,0:T(8,128)} %get-tuple-element.9), channel_id=1, source_target_pairs={{0,64},{64,128},{128,192},{192,256},{256,320},{320,384},{384,448},... | collective-permute-start | bytes 589832 | tf_op jit(solution)/shard_map/ppermute | solution.py:83
  27.5 1.9 %collective-permute-start.3 = (f32[384,128]{1,0:T(8,128)}, f32[384,128]{1,0:T(8,128)S(1)}, u32[]{:S(2)}, u32[]{:S(2)}) collective-permute-start(f32[384,128]{1,0:T(8,128)} %get-tuple-element.10), channel_id=1, source_target_pairs={{64,0},{128,64},{192,128},{256,192},{320,256},{384,320},{448,384},... | collective-permute-start | bytes 589832 | tf_op jit(solution)/shard_map/ppermute | solution.py:84
  29.4 1.0 %collective-permute-done.2.below_ref = f32[384,128]{1,0:T(8,128)S(1)} collective-permute-done((f32[384,128]{1,0:T(8,128)}, f32[384,128]{1,0:T(8,128)S(1)}, u32[]{:S(2)}, u32[]{:S(2)}) %collective-permute-start.2) | collective-permute-done | bytes 196640 | tf_op jit(solution)/shard_map/ppermute | solution.py:83
  30.4 0.0 copy-start.3
  30.4 5.5 %collective-permute-done.3.above_ref = f32[384,128]{1,0:T(8,128)S(1)} collective-permute-done((f32[384,128]{1,0:T(8,128)}, f32[384,128]{1,0:T(8,128)S(1)}, u32[]{:S(2)}, u32[]{:S(2)}) %collective-permute-start.3) | collective-permute-done | bytes 196640 | tf_op jit(solution)/shard_map/ppermute | solution.py:84
  35.9 0.0 copy-start.4
  35.9 0.0 copy-done.3
  35.9 0.7 %copy-done.4 = f32[384,128]{1,0:T(8,128)} copy-done((f32[384,128]{1,0:T(8,128)}, f32[384,128]{1,0:T(8,128)S(1)}, u32[]{:S(2)}) %copy-start.4) | copy-done | bytes 196632
  36.6 2.4 %shard_map.77 = (f32[4,4,64]{2,1,0:T(4,128)}, f32[7,4,4,64]{3,2,1,0:T(4,128)}, f32[7,8,8,128]{3,2,1,0:T(8,128)}) custom-call(f32[512,128]{1,0:T(8,128)} %get-tuple-element.7.one_ref, f32[128,128]{1,0:T(8,128)} %get-tuple-element.8.two_ref, f32[384,128]{1,0:T(8,128)} %copy-done.3, f32[384,128]{1,0:T(8,128)} %copy-done.4, f32[48,128]{1,0:T(8,128)} %get-tuple-element.13.maps_ref), custom_call_target="tpu_custom_call" | custom-call | tf_op jit(solution)/shard_map/pallas_call | solution.py:152
  (2 shorter events, 0.0 us)
Async XLA Ops:
  0.6 6.4 %copy-start.1 = (f32[3,256,128,1]{2,1,3,0:T(8,128)S(1)}, f32[3,256,128,1]{2,1,3,0:T(8,128)}, u32[]{:S(2)}) copy-start(f32[3,256,128,1]{2,1,3,0:T(8,128)} %constant.40) | copy-start | bytes 1179652
  0.6 6.4 %copy-start = (f32[16,16,256]{2,1,0:T(8,128)S(1)}, f32[16,16,256]{2,1,0:T(8,128)}, u32[]{:S(2)}) copy-start(f32[16,16,256]{2,1,0:T(8,128)} %param.5) | copy-start | bytes 786436
  1.8 7.7 %collective-permute-start = (f32[12,16,256]{2,1,0:T(8,128)S(1)}, f32[12,16,256]{2,1,0:T(8,128)S(1)}, u32[]{:S(2)}, u32[]{:S(2)}) collective-permute-start(f32[12,16,256]{2,1,0:T(8,128)S(1)} %get-tuple-element.11), channel_id=1, source_target_pairs={{0,1},{1,2},{2,3},{3,4},{4,5},{5,6},{6,7},{7,8},{8,9},{9,10},{10,1... | collective-permute-start | bytes 589832 | tf_op jit(solution)/shard_map/ppermute | solution.py:83
  4.5 10.7 %collective-permute-start.1 = (f32[12,16,256]{2,1,0:T(8,128)S(1)}, f32[12,16,256]{2,1,0:T(8,128)S(1)}, u32[]{:S(2)}, u32[]{:S(2)}) collective-permute-start(f32[12,16,256]{2,1,0:T(8,128)S(1)} %get-tuple-element.12), channel_id=1, source_target_pairs={{1,0},{2,1},{3,2},{4,3},{5,4},{6,5},{7,6},{8,7},{9,8},{10,9},{11,1... | collective-permute-start | bytes 589832 | tf_op jit(solution)/shard_map/ppermute | solution.py:84
  7.7 0.9 %copy-start.6 = (f32[3,48,128]{2,1,0:T(8,128)S(1)}, f32[3,48,128]{2,1,0:T(8,128)}, u32[]{:S(2)}) copy-start(f32[3,48,128]{2,1,0:T(8,128)} %constant.38.clone) | copy-start | bytes 221188
  7.7 7.4 %copy-start.5 = (f32[256,128,1,1]{1,0,3,2:T(8,128)S(1)}, f32[256,128,1,1]{1,0,3,2:T(8,128)}, u32[]{:S(2)}) copy-start(f32[256,128,1,1]{1,0,3,2:T(8,128)} %constant.42) | copy-start | bytes 393220
  15.2 1.2 %copy-start.2 = (f32[2,256,128,1,1]{2,1,0,4,3:T(8,128)S(1)}, f32[2,256,128,1,1]{2,1,0,4,3:T(8,128)}, u32[]{:S(2)}) copy-start(f32[2,256,128,1,1]{2,1,0,4,3:T(8,128)} %constant.41) | copy-start | bytes 786436
  19.6 10.8 %collective-permute-start.2 = (f32[384,128]{1,0:T(8,128)}, f32[384,128]{1,0:T(8,128)S(1)}, u32[]{:S(2)}, u32[]{:S(2)}) collective-permute-start(f32[384,128]{1,0:T(8,128)} %get-tuple-element.9), channel_id=1, source_target_pairs={{0,64},{64,128},{128,192},{192,256},{256,320},{320,384},{384,448},... | collective-permute-start | bytes 589832 | tf_op jit(solution)/shard_map/ppermute | solution.py:83
  27.5 8.4 %collective-permute-start.3 = (f32[384,128]{1,0:T(8,128)}, f32[384,128]{1,0:T(8,128)S(1)}, u32[]{:S(2)}, u32[]{:S(2)}) collective-permute-start(f32[384,128]{1,0:T(8,128)} %get-tuple-element.10), channel_id=1, source_target_pairs={{64,0},{128,64},{192,128},{256,192},{320,256},{384,320},{448,384},... | collective-permute-start | bytes 589832 | tf_op jit(solution)/shard_map/ppermute | solution.py:84
  30.4 5.5 %copy-start.3 = (f32[384,128]{1,0:T(8,128)}, f32[384,128]{1,0:T(8,128)S(1)}, u32[]{:S(2)}) copy-start(f32[384,128]{1,0:T(8,128)S(1)} %collective-permute-done.2.below_ref) | copy-start | bytes 589828
  35.9 0.7 %copy-start.4 = (f32[384,128]{1,0:T(8,128)}, f32[384,128]{1,0:T(8,128)S(1)}, u32[]{:S(2)}) copy-start(f32[384,128]{1,0:T(8,128)S(1)} %collective-permute-done.3.above_ref) | copy-start | bytes 589828

commit v11 on v7

--- a/solution.py
+++ b/solution.py
@@ -161,6 +161,52 @@
     )(x_one.reshape(-1, lanes), x_two.reshape(-1, lanes), below, above, y_maps)
 
 
+def z_pass_kernel(v_ref, z_ref, u_out, top_out, bottom_out, *, rows_one, rows_two):
+    lanes = u_out.shape[1]
+    bands = z_ref.shape[1] // lanes
+    ny = top_out.shape[0] // (rows_one * 2 + rows_two)
+    nx = v_ref.shape[0] // ny
+    result = jnp.dot(v_ref[...], z_ref[...], precision=EXACT, preferred_element_type=jnp.float32)
+    split = rows_one * 2 * ny
+    for x in range(nx):
+        for b in range(bands):
+            block = result[x * ny : (x + 1) * ny, b * lanes : (b + 1) * lanes]
+            u_out[(x * bands + b) * ny : (x * bands + b + 1) * ny, :] = block
+            if b < 2:
+                if x >= nx - rows_one:
+                    at = ((x - nx + rows_one) * 2 + b) * ny
+                    top_out[at : at + ny, :] = block
+                if x < rows_one:
+                    at = (x * 2 + b) * ny
+                    bottom_out[at : at + ny, :] = block
+            else:
+                if x >= nx - rows_two:
+                    at = split + (x - nx + rows_two) * ny
+                    top_out[at : at + ny, :] = block
+                if x < rows_two:
+                    at = split + x * ny
+                    bottom_out[at : at + ny, :] = block
+
+
+def z_pass(velocity, z_maps, rows_one, rows_two):
+    nx, ny, nz = velocity.shape
+    lanes = z_maps.shape[2]
+    bands = z_maps.shape[0]
+    matrix = np.concatenate(list(z_maps), axis=1)
+    vmem = pl.BlockSpec(memory_space=pltpu.VMEM)
+    message = (rows_one * 2 + rows_two) * ny
+    return pl.pallas_call(
+        functools.partial(z_pass_kernel, rows_one=rows_one, rows_two=rows_two),
+        out_shape=(
+            jax.ShapeDtypeStruct((nx * bands * ny, lanes), jnp.float32),
+            jax.ShapeDtypeStruct((message, lanes), jnp.float32),
+            jax.ShapeDtypeStruct((message, lanes), jnp.float32),
+        ),
+        in_specs=[vmem, vmem],
+        out_specs=(vmem, vmem, vmem),
+    )(velocity.reshape(nx * ny, nz), jnp.asarray(matrix))
+
+
 def x_pass_kernel(own_ref, below_ref, above_ref, maps_ref, one_out, two_out, top_out, bottom_out, *,
                   taps, places, bands):
     ny = two_out.shape[0] // len(taps[1])
@@ -223,7 +269,7 @@
     smem = pl.BlockSpec(memory_space=pltpu.SMEM)
     message = len(taps[0]) * 2 * narrow + len(taps[1]) * ny
     return pl.pallas_call(
-        functools.partial(x_pass_kernel, taps=taps, places=tuple(places), bands=u.shape[1]),
+        functools.partial(x_pass_kernel, taps=taps, places=tuple(places), bands=3),
         out_shape=(
             jax.ShapeDtypeStruct((len(taps[0]) * 2 * ny, lanes), jnp.float32),
             jax.ShapeDtypeStruct((len(taps[1]) * ny, lanes), jnp.float32),
@@ -232,7 +278,7 @@
         ),
         in_specs=[vmem, vmem, vmem, smem],
         out_specs=(vmem, vmem, vmem, vmem),
-    )(u.reshape(-1, lanes), below, above, x_maps)
+    )(u, below, above, x_maps)
 
 
 def per_device(velocity):
@@ -241,14 +287,9 @@
     (z_low, z_high), (z2_low, z2_high) = level_maps(nz)
     z_maps = np.stack([z_low.T, z_high.T, np.concatenate([z2_low, z2_high]).T]).astype(np.float32)
     lanes = z_maps.shape[2]
-    u = jnp.einsum("xyz,bzk->xbyk", velocity, jnp.asarray(z_maps), precision=EXACT)
-
     wide = 12
-    one_rows = u[:, 0:2]
-    two_rows = u[:, 2]
-    flat = lambda a: a.reshape(-1, lanes)
-    top = jnp.concatenate([flat(one_rows[nx - 4 :]), flat(two_rows[nx - wide :])])
-    bottom = jnp.concatenate([flat(one_rows[:4]), flat(two_rows[:wide])])
+    u, top, bottom = z_pass(velocity, z_maps, 4, wide)
+
     below, above = exchange(bottom, top, "slab")
     assert nx == ny and wide == 12
     table, places = packed_maps(nx)

time: 38.7 us -> 38.7 us (level)
  Pallas kernels: 4.72 us -> 7.27 us
  local copies, waits for them, and re-layouts: 3.81 us -> 1.96 us
  matrix products: 1.62 us -> 0 us
  waiting for transfers between devices: 12.4 us -> 13.4 us
    pallas_call x0 -> x1, Pallas kernels: none -> 2.55 us  [z_pass(): pl.pallas_call(functools.partial(z_pass_kernel, rows_one=rows_one, rows_t...]
    dot_general x1 -> x0, matrix products: 1.62 us -> none  [per_device(): jnp.einsum('xyz,bzk->xbyk', velocity, jnp.asarray(z_maps), precision=EXACT)]
    ppermute x2, waiting for transfers between devices: 1.1 us -> 2.2 us  [exchange(): from_below = lax.ppermute(upper_half, axis, up)]
    unnamed x12 -> x10, local copies, waits for them, and re-layouts: 2.39 us -> 1.33 us
    transpose x1 -> x0, local copies, waits for them, and re-layouts: 0.77 us -> none  [per_device(): jnp.einsum('xyz,bzk->xbyk', velocity, jnp.asarray(z_maps), precision=EXACT)]
  transfers between devices with their start and end apart: 4 -> 4, of which waited for: 4 -> 4; matrix products, arithmetic and copies ran while one was open for 4% -> 2% of each run, Pallas kernels for 0% -> 0%
where the time goes in v11:
time: 38.7 us; the launch traced here: 38.4 us
  starting transfers between devices  15 us (39%)
  waiting for transfers between devices  13.4 us (35%)
  Pallas kernels  7.27 us (19%)
  local copies, waits for them, and re-layouts  1.96 us (5%)
  between operations  0.7 us (2%)
    ppermute x2, waiting for transfers between devices, exchange(): from_above = lax.ppermute(lower_half, axis, down)  11.2 us
    ppermute x2, starting transfers between devices, exchange(): from_below = lax.ppermute(upper_half, axis, up)  10.6 us
    ppermute x2, starting transfers between devices, exchange(): from_above = lax.ppermute(lower_half, axis, down)  4.46 us
    pallas_call x1, Pallas kernels, z_pass(): pl.pallas_call(functools.partial(z_pass_kernel, rows_one=rows_one, rows_t...  2.55 us
    pallas_call x1, Pallas kernels, y_pass(): pl.pallas_call(functools.partial(y_pass_kernel, places=tuple(places)), ou...  2.42 us
    pallas_call x1, Pallas kernels, x_pass(): pl.pallas_call(functools.partial(x_pass_kernel, taps=taps, places=tuple(p...  2.31 us
    ppermute x2, waiting for transfers between devices, exchange(): from_below = lax.ppermute(upper_half, axis, up)  2.2 us
    unnamed x10, local copies, waits for them, and re-layouts  1.33 us
  transfers between devices with their start and end apart: 4, of which 4 were waited for; matrix products, arithmetic and copies ran while one was open for 2% of the time, Pallas kernels for 0%

profile of v11, /device:TPU:503, one launch (start us, length us, event | category | flops | bytes accessed | tf_op | source)
XLA Modules:
  0.0 38.4 jit_solution(8389149386952887315)
XLA Ops:
  0.6 0.0 copy-start.4
  0.6 2.5 %shard_map.58 = (f32[768,128]{1,0:T(8,128)}, f32[320,128]{1,0:T(8,128)}, f32[320,128]{1,0:T(8,128)}) custom-call(f32[256,256]{1,0:T(8,128)} %bitcast.5, f32[256,384]{1,0:T(8,128)} %constant.31.clone.z_ref), custom_call_target="tpu_custom_call" | custom-call | tf_op jit(solution)/shard_map/pallas_call | solution.py:198
  3.2 2.7 %collective-permute-start = (f32[320,128]{1,0:T(8,128)}, f32[320,128]{1,0:T(8,128)S(1)}, u32[]{:S(2)}, u32[]{:S(2)}) collective-permute-start(f32[320,128]{1,0:T(8,128)} %get-tuple-element.11), channel_id=1, source_target_pairs={{0,1},{1,2},{2,3},{3,4},{4,5},{5,6},{6,7},{7,8},{8,9},{9,10},{10,1... | collective-permute-start | bytes 491528 | tf_op jit(solution)/shard_map/ppermute | solution.py:83
  5.9 2.5 %collective-permute-start.1 = (f32[320,128]{1,0:T(8,128)}, f32[320,128]{1,0:T(8,128)S(1)}, u32[]{:S(2)}, u32[]{:S(2)}) collective-permute-start(f32[320,128]{1,0:T(8,128)} %get-tuple-element.12), channel_id=1, source_target_pairs={{1,0},{2,1},{3,2},{4,3},{5,4},{6,5},{7,6},{8,7},{9,8},{10,9},{11,1... | collective-permute-start | bytes 491528 | tf_op jit(solution)/shard_map/ppermute | solution.py:84
  8.5 0.0 copy-done.4
  8.5 0.6 %dynamic-slice_bitcast_fusion = (f32[48,128]{1,0:T(8,128)}, f32[48,128]{1,0:T(8,128)}) fusion(f32[3,48,128]{2,1,0:T(8,128)S(1)} %copy-done.4, s32[]{:T(128)S(6)} %select_n.20, s32[]{:T(128)S(6)} %select_n.18), kind=kLoop, calls=%fused_computation | loop fusion | bytes 98312 | tf_op jit(solution)/shard_map/jit(dynamic_index_in_dim)/squeeze | solution.py:298
  9.1 1.2 %collective-permute-done.below_ref = f32[320,128]{1,0:T(8,128)S(1)} collective-permute-done((f32[320,128]{1,0:T(8,128)}, f32[320,128]{1,0:T(8,128)S(1)}, u32[]{:S(2)}, u32[]{:S(2)}) %collective-permute-start) | collective-permute-done | bytes 163872 | tf_op jit(solution)/shard_map/ppermute | solution.py:83
  10.3 0.0 copy-start.2
  10.3 5.7 %collective-permute-done.1.above_ref = f32[320,128]{1,0:T(8,128)S(1)} collective-permute-done((f32[320,128]{1,0:T(8,128)}, f32[320,128]{1,0:T(8,128)S(1)}, u32[]{:S(2)}, u32[]{:S(2)}) %collective-permute-start.1) | collective-permute-done | bytes 163872 | tf_op jit(solution)/shard_map/ppermute | solution.py:84
  16.1 0.0 copy-start.3
  16.1 0.0 copy-done.2
  16.1 0.7 %copy-done.3 = f32[320,128]{1,0:T(8,128)} copy-done((f32[320,128]{1,0:T(8,128)}, f32[320,128]{1,0:T(8,128)S(1)}, u32[]{:S(2)}) %copy-start.3) | copy-done | bytes 163864
  16.8 2.3 %shard_map.59 = (f32[512,128]{1,0:T(8,128)}, f32[128,128]{1,0:T(8,128)}, f32[384,128]{1,0:T(8,128)}, f32[384,128]{1,0:T(8,128)}) custom-call(f32[768,128]{1,0:T(8,128)} %get-tuple-element.10.own_ref, f32[320,128]{1,0:T(8,128)} %copy-done.2, f32[320,128]{1,0:T(8,128)} %copy-done.3, f32[48,128]{1,0:T(8,128)} %get-tuple-element.18.maps_ref), custom_call_target="tpu_custom_call" | custom-call | tf_op jit(solution)/shard_map/pallas_call | solution.py:271
  19.1 7.9 %collective-permute-start.2 = (f32[384,128]{1,0:T(8,128)}, f32[384,128]{1,0:T(8,128)S(1)}, u32[]{:S(2)}, u32[]{:S(2)}) collective-permute-start(f32[384,128]{1,0:T(8,128)} %get-tuple-element.15), channel_id=1, source_target_pairs={{0,64},{64,128},{128,192},{192,256},{256,320},{320,384},{384,448},... | collective-permute-start | bytes 589832 | tf_op jit(solution)/shard_map/ppermute | solution.py:83
  26.9 1.9 %collective-permute-start.3 = (f32[384,128]{1,0:T(8,128)}, f32[384,128]{1,0:T(8,128)S(1)}, u32[]{:S(2)}, u32[]{:S(2)}) collective-permute-start(f32[384,128]{1,0:T(8,128)} %get-tuple-element.16), channel_id=1, source_target_pairs={{64,0},{128,64},{192,128},{256,192},{320,256},{384,320},{448,384},... | collective-permute-start | bytes 589832 | tf_op jit(solution)/shard_map/ppermute | solution.py:84
  28.9 1.0 %collective-permute-done.2.below_ref = f32[384,128]{1,0:T(8,128)S(1)} collective-permute-done((f32[384,128]{1,0:T(8,128)}, f32[384,128]{1,0:T(8,128)S(1)}, u32[]{:S(2)}, u32[]{:S(2)}) %collective-permute-start.2) | collective-permute-done | bytes 196640 | tf_op jit(solution)/shard_map/ppermute | solution.py:83
  29.8 0.0 copy-start
  29.8 5.5 %collective-permute-done.3.above_ref = f32[384,128]{1,0:T(8,128)S(1)} collective-permute-done((f32[384,128]{1,0:T(8,128)}, f32[384,128]{1,0:T(8,128)S(1)}, u32[]{:S(2)}, u32[]{:S(2)}) %collective-permute-start.3) | collective-permute-done | bytes 196640 | tf_op jit(solution)/shard_map/ppermute | solution.py:84
  35.3 0.0 copy-start.1
  35.3 0.0 copy-done
  35.3 0.7 %copy-done.1 = f32[384,128]{1,0:T(8,128)} copy-done((f32[384,128]{1,0:T(8,128)}, f32[384,128]{1,0:T(8,128)S(1)}, u32[]{:S(2)}) %copy-start.1) | copy-done | bytes 196632
  36.0 2.4 %shard_map.60 = (f32[4,4,64]{2,1,0:T(4,128)}, f32[7,4,4,64]{3,2,1,0:T(4,128)}, f32[7,8,8,128]{3,2,1,0:T(8,128)}) custom-call(f32[512,128]{1,0:T(8,128)} %get-tuple-element.13.one_ref, f32[128,128]{1,0:T(8,128)} %get-tuple-element.14.two_ref, f32[384,128]{1,0:T(8,128)} %copy-done, f32[384,128]{1,0:T(8,128)} %copy-done.1, f32[48,128]{1,0:T(8,128)} %get-tuple-element.17.maps_ref), custom_call_target="tpu_custom_call" | custom-call | tf_op jit(solution)/shard_map/pallas_call | solution.py:152
Async XLA Ops:
  0.6 7.9 %copy-start.4 = (f32[3,48,128]{2,1,0:T(8,128)S(1)}, f32[3,48,128]{2,1,0:T(8,128)}, u32[]{:S(2)}) copy-start(f32[3,48,128]{2,1,0:T(8,128)} %constant.32.clone) | copy-start | bytes 221188
  3.2 7.2 %collective-permute-start = (f32[320,128]{1,0:T(8,128)}, f32[320,128]{1,0:T(8,128)S(1)}, u32[]{:S(2)}, u32[]{:S(2)}) collective-permute-start(f32[320,128]{1,0:T(8,128)} %get-tuple-element.11), channel_id=1, source_target_pairs={{0,1},{1,2},{2,3},{3,4},{4,5},{5,6},{6,7},{7,8},{8,9},{9,10},{10,1... | collective-permute-start | bytes 491528 | tf_op jit(solution)/shard_map/ppermute | solution.py:83
  5.9 10.2 %collective-permute-start.1 = (f32[320,128]{1,0:T(8,128)}, f32[320,128]{1,0:T(8,128)S(1)}, u32[]{:S(2)}, u32[]{:S(2)}) collective-permute-start(f32[320,128]{1,0:T(8,128)} %get-tuple-element.12), channel_id=1, source_target_pairs={{1,0},{2,1},{3,2},{4,3},{5,4},{6,5},{7,6},{8,7},{9,8},{10,9},{11,1... | collective-permute-start | bytes 491528 | tf_op jit(solution)/shard_map/ppermute | solution.py:84
  10.3 5.8 %copy-start.2 = (f32[320,128]{1,0:T(8,128)}, f32[320,128]{1,0:T(8,128)S(1)}, u32[]{:S(2)}) copy-start(f32[320,128]{1,0:T(8,128)S(1)} %collective-permute-done.below_ref) | copy-start | bytes 491524
  16.1 0.7 %copy-start.3 = (f32[320,128]{1,0:T(8,128)}, f32[320,128]{1,0:T(8,128)S(1)}, u32[]{:S(2)}) copy-start(f32[320,128]{1,0:T(8,128)S(1)} %collective-permute-done.1.above_ref) | copy-start | bytes 491524
  19.1 10.8 %collective-permute-start.2 = (f32[384,128]{1,0:T(8,128)}, f32[384,128]{1,0:T(8,128)S(1)}, u32[]{:S(2)}, u32[]{:S(2)}) collective-permute-start(f32[384,128]{1,0:T(8,128)} %get-tuple-element.15), channel_id=1, source_target_pairs={{0,64},{64,128},{128,192},{192,256},{256,320},{320,384},{384,448},... | collective-permute-start | bytes 589832 | tf_op jit(solution)/shard_map/ppermute | solution.py:83
  26.9 8.4 %collective-permute-start.3 = (f32[384,128]{1,0:T(8,128)}, f32[384,128]{1,0:T(8,128)S(1)}, u32[]{:S(2)}, u32[]{:S(2)}) collective-permute-start(f32[384,128]{1,0:T(8,128)} %get-tuple-element.16), channel_id=1, source_target_pairs={{64,0},{128,64},{192,128},{256,192},{320,256},{384,320},{448,384},... | collective-permute-start | bytes 589832 | tf_op jit(solution)/shard_map/ppermute | solution.py:84
  29.8 5.5 %copy-start = (f32[384,128]{1,0:T(8,128)}, f32[384,128]{1,0:T(8,128)S(1)}, u32[]{:S(2)}) copy-start(f32[384,128]{1,0:T(8,128)S(1)} %collective-permute-done.2.below_ref) | copy-start | bytes 589828
  35.3 0.7 %copy-start.1 = (f32[384,128]{1,0:T(8,128)}, f32[384,128]{1,0:T(8,128)S(1)}, u32[]{:S(2)}) copy-start(f32[384,128]{1,0:T(8,128)S(1)} %collective-permute-done.3.above_ref) | copy-start | bytes 589828

commit v12 on v7

--- a/solution.py
+++ b/solution.py
@@ -91,7 +91,7 @@
     ny = 2 * one_out.shape[2]
     slabs_one = n_one // ny
     slabs_two = n_two // ny
-    narrow = (below_ref.shape[0] - n_two) // slabs_one
+    narrow, wide = 4, 12
     blocks = []
     for s in range(slabs_one):
         blocks.append(
@@ -103,7 +103,7 @@
                 ]
             )
         )
-    row, rows, cols = places[2]
+    row, rows, cols = places[0]
     a1 = maps_ref[row : row + rows, :][:, :cols]
     result = jnp.dot(a1, jnp.concatenate(blocks, axis=1), precision=EXACT,
                      preferred_element_type=jnp.float32)
@@ -122,13 +122,13 @@
         blocks.append(
             jnp.concatenate(
                 [
-                    below_ref[base + s * ny : base + (s + 1) * ny, :],
+                    below_ref[base + s * wide : base + (s + 1) * wide, :],
                     two_ref[s * ny : (s + 1) * ny, :],
-                    above_ref[base + s * ny : base + (s + 1) * ny, :],
+                    above_ref[base + s * wide : base + (s + 1) * wide, :],
                 ]
             )
         )
-    row, rows, cols = places[3]
+    row, rows, cols = places[1]
     a2 = maps_ref[row : row + rows, :][:, :cols]
     result = jnp.dot(a2, jnp.concatenate(blocks, axis=1), precision=EXACT,
                      preferred_element_type=jnp.float32)
@@ -186,7 +186,7 @@
         j = i - lo2 - ny
         return above_ref[split + j * ny : split + (j + 1) * ny, :]
 
-    narrow = (top_out.shape[0] - two_out.shape[0]) // (len(taps[0]) * 2)
+    narrow, wide = lo1, lo2
     row1 = places[0][0]
     for k, used in enumerate(taps[0]):
         acc = None
@@ -206,8 +206,8 @@
             term = maps_ref[row2 + k, i] * two_slab(i)
             acc = term if acc is None else acc + term
         two_out[k * ny : (k + 1) * ny, :] = acc
-        top_out[base + k * ny : base + (k + 1) * ny, :] = acc
-        bottom_out[base + k * ny : base + (k + 1) * ny, :] = acc
+        top_out[base + k * wide : base + (k + 1) * wide, :] = acc[ny - wide :, :]
+        bottom_out[base + k * wide : base + (k + 1) * wide, :] = acc[:wide, :]
 
 
 def used_taps(maps):
@@ -218,10 +218,10 @@
 def x_pass(u, below, above, x_maps, places, nx, ny):
     lanes = u.shape[-1]
     taps = (used_taps(window_maps(nx, (4, 4), 0)), used_taps(window_maps(nx, (12, 12), 1)))
-    narrow = 8
+    narrow, wide = 4, 12
     vmem = pl.BlockSpec(memory_space=pltpu.VMEM)
     smem = pl.BlockSpec(memory_space=pltpu.SMEM)
-    message = len(taps[0]) * 2 * narrow + len(taps[1]) * ny
+    message = len(taps[0]) * 2 * narrow + len(taps[1]) * wide
     return pl.pallas_call(
         functools.partial(x_pass_kernel, taps=taps, places=tuple(places), bands=u.shape[1]),
         out_shape=(

time: 38.7 us -> 37.7 us (0.974)
  waiting for transfers between devices: 12.4 us -> 11.5 us
    ppermute x2, waiting for transfers between devices: 1.1 us -> 0.28 us  [exchange(): from_below = lax.ppermute(upper_half, axis, up)]
where the time goes in v12:
time: 37.7 us; the launch traced here: 37.4 us
  starting transfers between devices  15.1 us (40%)
  waiting for transfers between devices  11.5 us (31%)
  Pallas kernels  4.62 us (12%)
  local copies, waits for them, and re-layouts  3.8 us (10%)
  matrix products  1.62 us (4%)
  between operations  0.74 us (2%)
    ppermute x2, waiting for transfers between devices, exchange(): from_above = lax.ppermute(lower_half, axis, down)  11.2 us
    ppermute x2, starting transfers between devices, exchange(): from_below = lax.ppermute(upper_half, axis, up)  10.6 us
    ppermute x2, starting transfers between devices, exchange(): from_above = lax.ppermute(lower_half, axis, down)  4.46 us
    unnamed x12, local copies, waits for them, and re-layouts  2.37 us
    pallas_call x1, Pallas kernels, y_pass(): pl.pallas_call(functools.partial(y_pass_kernel, places=tuple(places)), ou...  2.35 us
    pallas_call x1, Pallas kernels, x_pass(): pl.pallas_call(functools.partial(x_pass_kernel, taps=taps, places=tuple(p...  2.28 us
    dot_general x1, matrix products, per_device(): jnp.einsum('xyz,bzk->xbyk', velocity, jnp.asarray(z_maps), precision=EXACT)  1.62 us
    transpose x1, local copies, waits for them, and re-layouts, per_device(): jnp.einsum('xyz,bzk->xbyk', velocity, jnp.asarray(z_maps), precision=EXACT)  0.77 us
  transfers between devices with their start and end apart: 4, of which 4 were waited for; matrix products, arithmetic and copies ran while one was open for 4% of the time, Pallas kernels for 0%

profile of v12, /device:TPU:503, one launch (start us, length us, event | category | flops | bytes accessed | tf_op | source)
XLA Modules:
  0.0 37.4 jit_solution(16716504920428361780)
XLA Ops:
  0.6 0.0 copy-start
  0.6 0.9 %copy-done = f32[16,16,256]{2,1,0:T(8,128)S(1)} copy-done((f32[16,16,256]{2,1,0:T(8,128)S(1)}, f32[16,16,256]{2,1,0:T(8,128)}, u32[]{:S(2)}) %copy-start) | copy-done | bytes 262168
  1.6 1.6 %convolution_bitcast_fusion = f32[16,3,16,128]{3,2,0,1:T(8,128)S(1)} fusion(f32[3,256,128,1]{2,1,3,0:T(8,128)} %constant.34, f32[16,16,256]{2,1,0:T(8,128)S(1)} %copy-done), kind=kOutput, calls=%fused_computation | convolution fusion | flops 301989888 | bytes 1048576 | tf_op jit(solution)/shard_map/xyz,bzk->xbyk/dot_general | solution.py:244
  3.3 2.7 %collective-permute-start = (f32[320,128]{1,0:T(8,128)S(1)}, f32[320,128]{1,0:T(8,128)S(1)}, u32[]{:S(2)}, u32[]{:S(2)}) collective-permute-start(f32[320,128]{1,0:T(8,128)S(1)} %pad_maximum_fusion), channel_id=1, source_target_pairs={{0,1},{1,2},{2,3},{3,4},{4,5},{5,6},{6,7},{7,8},{8,9},{9,10},{10,1... | collective-permute-start | bytes 491528 | tf_op jit(solution)/shard_map/ppermute | solution.py:83
  6.1 2.5 %collective-permute-start.1 = (f32[320,128]{1,0:T(8,128)S(1)}, f32[320,128]{1,0:T(8,128)S(1)}, u32[]{:S(2)}, u32[]{:S(2)}) collective-permute-start(f32[320,128]{1,0:T(8,128)S(1)} %pad_maximum_fusion.1), channel_id=1, source_target_pairs={{1,0},{2,1},{3,2},{4,3},{5,4},{6,5},{7,6},{8,7},{9,8},{10,9},{11,1... | collective-permute-start | bytes 491528 | tf_op jit(solution)/shard_map/ppermute | solution.py:84
  8.6 0.0 copy-start.5
  8.6 0.8 %copy.6 = f32[16,3,16,128]{3,2,1,0:T(8,128)} copy(f32[16,3,16,128]{3,2,0,1:T(8,128)S(1)} %convolution_bitcast_fusion) | data formatting | bytes 786432 | tf_op jit(solution)/shard_map/xyz,bzk->xbyk/transpose | solution.py:244
  9.4 0.1 copy-done.5
  9.5 0.6 %dynamic-slice_bitcast_fusion = (f32[48,128]{1,0:T(8,128)}, f32[48,128]{1,0:T(8,128)}) fusion(f32[3,48,128]{2,1,0:T(8,128)S(1)} %copy-done.5, s32[]{:T(128)S(6)} %select_n.20, s32[]{:T(128)S(6)} %select_n.18), kind=kLoop, calls=%fused_computation.4 | loop fusion | bytes 98312 | tf_op jit(solution)/shard_map/jit(dynamic_index_in_dim)/squeeze | solution.py:257
  10.1 0.1 collective-permute-done.below_ref
  10.3 0.0 copy-start.1
  10.3 5.8 %collective-permute-done.1.above_ref = f32[320,128]{1,0:T(8,128)S(1)} collective-permute-done((f32[320,128]{1,0:T(8,128)S(1)}, f32[320,128]{1,0:T(8,128)S(1)}, u32[]{:S(2)}, u32[]{:S(2)}) %collective-permute-start.1) | collective-permute-done | bytes 163872 | tf_op jit(solution)/shard_map/ppermute | solution.py:84
  16.0 0.0 copy-start.2
  16.0 0.0 copy-done.1
  16.0 0.7 %copy-done.2 = f32[320,128]{1,0:T(8,128)} copy-done((f32[320,128]{1,0:T(8,128)}, f32[320,128]{1,0:T(8,128)S(1)}, u32[]{:S(2)}) %copy-start.2) | copy-done | bytes 163864
  16.7 2.3 %shard_map.58 = (f32[512,128]{1,0:T(8,128)}, f32[128,128]{1,0:T(8,128)}, f32[224,128]{1,0:T(8,128)}, f32[224,128]{1,0:T(8,128)}) custom-call(f32[768,128]{1,0:T(8,128)} %bitcast.18, f32[320,128]{1,0:T(8,128)} %copy-done.1, f32[320,128]{1,0:T(8,128)} %copy-done.2, f32[48,128]{1,0:T(8,128)} %get-tuple-element.16.maps_ref), custom_call_target="tpu_custom_call" | custom-call | tf_op jit(solution)/shard_map/pallas_call | solution.py:225
  19.0 7.9 %collective-permute-start.2 = (f32[224,128]{1,0:T(8,128)}, f32[224,128]{1,0:T(8,128)S(1)}, u32[]{:S(2)}, u32[]{:S(2)}) collective-permute-start(f32[224,128]{1,0:T(8,128)} %get-tuple-element.9), channel_id=1, source_target_pairs={{0,64},{64,128},{128,192},{192,256},{256,320},{320,384},{384,448},... | collective-permute-start | bytes 344072 | tf_op jit(solution)/shard_map/ppermute | solution.py:83
  26.9 1.9 %collective-permute-start.3 = (f32[224,128]{1,0:T(8,128)}, f32[224,128]{1,0:T(8,128)S(1)}, u32[]{:S(2)}, u32[]{:S(2)}) collective-permute-start(f32[224,128]{1,0:T(8,128)} %get-tuple-element.10), channel_id=1, source_target_pairs={{64,0},{128,64},{192,128},{256,192},{320,256},{384,320},{448,384},... | collective-permute-start | bytes 344072 | tf_op jit(solution)/shard_map/ppermute | solution.py:84
  28.8 0.2 collective-permute-done.2.below_ref
  28.9 0.0 copy-start.3
  28.9 5.4 %collective-permute-done.3.above_ref = f32[224,128]{1,0:T(8,128)S(1)} collective-permute-done((f32[224,128]{1,0:T(8,128)}, f32[224,128]{1,0:T(8,128)S(1)}, u32[]{:S(2)}, u32[]{:S(2)}) %collective-permute-start.3) | collective-permute-done | bytes 114720 | tf_op jit(solution)/shard_map/ppermute | solution.py:84
  34.4 0.0 copy-start.4
  34.4 0.0 copy-done.3
  34.4 0.6 %copy-done.4 = f32[224,128]{1,0:T(8,128)} copy-done((f32[224,128]{1,0:T(8,128)}, f32[224,128]{1,0:T(8,128)S(1)}, u32[]{:S(2)}) %copy-start.4) | copy-done | bytes 114712
  35.0 2.3 %shard_map.59 = (f32[4,4,64]{2,1,0:T(4,128)}, f32[7,4,4,64]{3,2,1,0:T(4,128)}, f32[7,8,8,128]{3,2,1,0:T(8,128)}) custom-call(f32[512,128]{1,0:T(8,128)} %get-tuple-element.7.one_ref, f32[128,128]{1,0:T(8,128)} %get-tuple-element.8.two_ref, f32[224,128]{1,0:T(8,128)} %copy-done.3, f32[224,128]{1,0:T(8,128)} %copy-done.4, f32[48,128]{1,0:T(8,128)} %get-tuple-element.15.maps_ref), custom_call_target="tpu_custom_call" | custom-call | tf_op jit(solution)/shard_map/pallas_call | solution.py:152
  (6 shorter events, 0.1 us)
Async XLA Ops:
  0.6 1.0 %copy-start = (f32[16,16,256]{2,1,0:T(8,128)S(1)}, f32[16,16,256]{2,1,0:T(8,128)}, u32[]{:S(2)}) copy-start(f32[16,16,256]{2,1,0:T(8,128)} %param.3) | copy-start | bytes 786436
  3.3 7.0 %collective-permute-start = (f32[320,128]{1,0:T(8,128)S(1)}, f32[320,128]{1,0:T(8,128)S(1)}, u32[]{:S(2)}, u32[]{:S(2)}) collective-permute-start(f32[320,128]{1,0:T(8,128)S(1)} %pad_maximum_fusion), channel_id=1, source_target_pairs={{0,1},{1,2},{2,3},{3,4},{4,5},{5,6},{6,7},{7,8},{8,9},{9,10},{10,1... | collective-permute-start | bytes 491528 | tf_op jit(solution)/shard_map/ppermute | solution.py:83
  6.1 10.0 %collective-permute-start.1 = (f32[320,128]{1,0:T(8,128)S(1)}, f32[320,128]{1,0:T(8,128)S(1)}, u32[]{:S(2)}, u32[]{:S(2)}) collective-permute-start(f32[320,128]{1,0:T(8,128)S(1)} %pad_maximum_fusion.1), channel_id=1, source_target_pairs={{1,0},{2,1},{3,2},{4,3},{5,4},{6,5},{7,6},{8,7},{9,8},{10,9},{11,1... | collective-permute-start | bytes 491528 | tf_op jit(solution)/shard_map/ppermute | solution.py:84
  8.6 0.9 %copy-start.5 = (f32[3,48,128]{2,1,0:T(8,128)S(1)}, f32[3,48,128]{2,1,0:T(8,128)}, u32[]{:S(2)}) copy-start(f32[3,48,128]{2,1,0:T(8,128)} %constant.32.clone) | copy-start | bytes 221188
  10.3 5.8 %copy-start.1 = (f32[320,128]{1,0:T(8,128)}, f32[320,128]{1,0:T(8,128)S(1)}, u32[]{:S(2)}) copy-start(f32[320,128]{1,0:T(8,128)S(1)} %collective-permute-done.below_ref) | copy-start | bytes 491524
  16.0 0.7 %copy-start.2 = (f32[320,128]{1,0:T(8,128)}, f32[320,128]{1,0:T(8,128)S(1)}, u32[]{:S(2)}) copy-start(f32[320,128]{1,0:T(8,128)S(1)} %collective-permute-done.1.above_ref) | copy-start | bytes 491524
  19.0 10.0 %collective-permute-start.2 = (f32[224,128]{1,0:T(8,128)}, f32[224,128]{1,0:T(8,128)S(1)}, u32[]{:S(2)}, u32[]{:S(2)}) collective-permute-start(f32[224,128]{1,0:T(8,128)} %get-tuple-element.9), channel_id=1, source_target_pairs={{0,64},{64,128},{128,192},{192,256},{256,320},{320,384},{384,448},... | collective-permute-start | bytes 344072 | tf_op jit(solution)/shard_map/ppermute | solution.py:83
  26.9 7.5 %collective-permute-start.3 = (f32[224,128]{1,0:T(8,128)}, f32[224,128]{1,0:T(8,128)S(1)}, u32[]{:S(2)}, u32[]{:S(2)}) collective-permute-start(f32[224,128]{1,0:T(8,128)} %get-tuple-element.10), channel_id=1, source_target_pairs={{64,0},{128,64},{192,128},{256,192},{320,256},{384,320},{448,384},... | collective-permute-start | bytes 344072 | tf_op jit(solution)/shard_map/ppermute | solution.py:84
  28.9 5.4 %copy-start.3 = (f32[224,128]{1,0:T(8,128)}, f32[224,128]{1,0:T(8,128)S(1)}, u32[]{:S(2)}) copy-start(f32[224,128]{1,0:T(8,128)S(1)} %collective-permute-done.2.below_ref) | copy-start | bytes 344068
  34.4 0.6 %copy-start.4 = (f32[224,128]{1,0:T(8,128)}, f32[224,128]{1,0:T(8,128)S(1)}, u32[]{:S(2)}) copy-start(f32[224,128]{1,0:T(8,128)S(1)} %collective-permute-done.3.above_ref) | copy-start | bytes 344068

commit v13 on v12

--- a/solution.py
+++ b/solution.py
@@ -161,11 +161,11 @@
     )(x_one.reshape(-1, lanes), x_two.reshape(-1, lanes), below, above, y_maps)
 
 
-def x_pass_kernel(own_ref, below_ref, above_ref, maps_ref, one_out, two_out, top_out, bottom_out, *,
-                  taps, places, bands):
+def x_pass_kernel(edge_ref, middle_ref, coarse_ref, below_ref, above_ref, maps_ref, one_out, two_out,
+                  top_out, bottom_out, *, taps, places):
     ny = two_out.shape[0] // len(taps[1])
     slab = 2 * ny
-    stride = bands * ny
+    nx = coarse_ref.shape[0] // ny
     lo1, lo2 = 4, 12
     split = lo1 * slab
 
@@ -173,7 +173,14 @@
         if i < lo1:
             return below_ref[i * slab : (i + 1) * slab, :]
         if i < lo1 + ny:
-            return own_ref[(i - lo1) * stride : (i - lo1) * stride + slab, :]
+            x = i - lo1
+            if x < lo1:
+                return edge_ref[x * slab : (x + 1) * slab, :]
+            if x >= nx - lo1:
+                x = x - nx + 2 * lo1
+                return edge_ref[x * slab : (x + 1) * slab, :]
+            x = x - lo1
+            return middle_ref[x * slab : (x + 1) * slab, :]
         j = i - lo1 - ny
         return above_ref[j * slab : (j + 1) * slab, :]
 
@@ -181,8 +188,8 @@
         if i < lo2:
             return below_ref[split + i * ny : split + (i + 1) * ny, :]
         if i < lo2 + ny:
-            at = (i - lo2) * stride + slab
-            return own_ref[at : at + ny, :]
+            at = (i - lo2) * ny
+            return coarse_ref[at : at + ny, :]
         j = i - lo2 - ny
         return above_ref[split + j * ny : split + (j + 1) * ny, :]
 
@@ -215,24 +222,26 @@
     return tuple(tuple(int(i) for i in np.nonzero(row)[0]) for row in present)
 
 
-def x_pass(u, below, above, x_maps, places, nx, ny):
-    lanes = u.shape[-1]
+def x_pass(edge, middle, coarse, below, above, x_maps, places, nx, ny):
+    lanes = coarse.shape[-1]
     taps = (used_taps(window_maps(nx, (4, 4), 0)), used_taps(window_maps(nx, (12, 12), 1)))
     narrow, wide = 4, 12
     vmem = pl.BlockSpec(memory_space=pltpu.VMEM)
     smem = pl.BlockSpec(memory_space=pltpu.SMEM)
     message = len(taps[0]) * 2 * narrow + len(taps[1]) * wide
     return pl.pallas_call(
-        functools.partial(x_pass_kernel, taps=taps, places=tuple(places), bands=u.shape[1]),
+        functools.partial(x_pass_kernel, taps=taps, places=tuple(places)),
         out_shape=(
             jax.ShapeDtypeStruct((len(taps[0]) * 2 * ny, lanes), jnp.float32),
             jax.ShapeDtypeStruct((len(taps[1]) * ny, lanes), jnp.float32),
             jax.ShapeDtypeStruct((message, lanes), jnp.float32),
             jax.ShapeDtypeStruct((message, lanes), jnp.float32),
         ),
-        in_specs=[vmem, vmem, vmem, smem],
+        in_specs=[vmem, vmem, vmem, vmem, vmem, smem],
         out_specs=(vmem, vmem, vmem, vmem),
-    )(u.reshape(-1, lanes), below, above, x_maps)
+    )(
+        edge.reshape(-1, lanes), middle.reshape(-1, lanes), coarse.reshape(-1, lanes), below, above, x_maps
+    )
 
 
 def per_device(velocity):
@@ -241,21 +250,21 @@
     (z_low, z_high), (z2_low, z2_high) = level_maps(nz)
     z_maps = np.stack([z_low.T, z_high.T, np.concatenate([z2_low, z2_high]).T]).astype(np.float32)
     lanes = z_maps.shape[2]
-    u = jnp.einsum("xyz,bzk->xbyk", velocity, jnp.asarray(z_maps), precision=EXACT)
-
     wide = 12
-    one_rows = u[:, 0:2]
-    two_rows = u[:, 2]
     flat = lambda a: a.reshape(-1, lanes)
-    top = jnp.concatenate([flat(one_rows[nx - 4 :]), flat(two_rows[nx - wide :])])
-    bottom = jnp.concatenate([flat(one_rows[:4]), flat(two_rows[:wide])])
+    coarse = jnp.einsum("xyz,zk->xyk", velocity, jnp.asarray(z_maps[2]), precision=EXACT)
+    rims = jnp.concatenate([velocity[:4], velocity[nx - 4 :]])
+    edge = jnp.einsum("xyz,bzk->xbyk", rims, jnp.asarray(z_maps[0:2]), precision=EXACT)
+    top = jnp.concatenate([flat(edge[4:]), flat(coarse[nx - wide :])])
+    bottom = jnp.concatenate([flat(edge[:4]), flat(coarse[:wide])])
     below, above = exchange(bottom, top, "slab")
     assert nx == ny and wide == 12
     table, places = packed_maps(nx)
     table = jnp.asarray(table)
     x_maps = lax.dynamic_index_in_dim(table, case_of("slab"), keepdims=False)
     y_maps = lax.dynamic_index_in_dim(table, case_of("morton"), keepdims=False)
-    x_one, x_two, top, bottom = x_pass(u, below, above, x_maps, places, nx, ny)
+    middle = jnp.einsum("xyz,bzk->xbyk", velocity[4 : nx - 4], jnp.asarray(z_maps[0:2]), precision=EXACT)
+    x_one, x_two, top, bottom = x_pass(edge, middle, coarse, below, above, x_maps, places, nx, ny)
 
     below, above = exchange(bottom, top, "morton")
     return y_pass(x_one, x_two, below, above, y_maps, places, nx, ny, nz)

time: 37.7 us -> 38.5 us (1.021)
  local copies, waits for them, and re-layouts: 3.8 us -> 4.47 us
    slice x4 -> x3, local copies, waits for them, and re-layouts: 0.04 us -> 0.95 us  [the longest x1 0.92 us: per_device(): rims = jnp.concatenate([velocity[:4], velocity[nx - 4:]])]
    dot_general x1 -> x3, matrix products: 1.62 us -> 1.9 us  [the longest x1 1.32 us: per_device(): jnp.einsum('xyz,zk->xyk', velocity, jnp.asarray(z_maps[2]), precision=EXACT)]
    unnamed x12 -> x20, local copies, waits for them, and re-layouts: 2.37 us -> 2.24 us
  transfers between devices with their start and end apart: 4 -> 4, of which waited for: 4 -> 3; matrix products, arithmetic and copies ran while one was open for 4% -> 4% of each run, Pallas kernels for 0% -> 0%
where the time goes in v13:
time: 38.5 us; the launch traced here: 38.2 us
  starting transfers between devices  15.2 us (39%)
  waiting for transfers between devices  11.2 us (29%)
  Pallas kernels  4.62 us (12%)
  local copies, waits for them, and re-layouts  4.47 us (12%)
  matrix products  1.9 us (5%)
  between operations  0.8 us (2%)
    ppermute x2, waiting for transfers between devices, exchange(): from_above = lax.ppermute(lower_half, axis, down)  11 us
    ppermute x2, starting transfers between devices, exchange(): from_below = lax.ppermute(upper_half, axis, up)  10.7 us
    ppermute x2, starting transfers between devices, exchange(): from_above = lax.ppermute(lower_half, axis, down)  4.47 us
    pallas_call x1, Pallas kernels, y_pass(): pl.pallas_call(functools.partial(y_pass_kernel, places=tuple(places)), ou...  2.35 us
    pallas_call x1, Pallas kernels, x_pass(): pl.pallas_call(functools.partial(x_pass_kernel, taps=taps, places=tuple(p...  2.27 us
    unnamed x20, local copies, waits for them, and re-layouts  2.24 us
    dot_general x1, matrix products, per_device(): jnp.einsum('xyz,zk->xyk', velocity, jnp.asarray(z_maps[2]), precision=EXACT)  1.32 us
    slice x1, local copies, waits for them, and re-layouts, per_device(): rims = jnp.concatenate([velocity[:4], velocity[nx - 4:]])  0.92 us
  transfers between devices with their start and end apart: 4, of which 3 were waited for; matrix products, arithmetic and copies ran while one was open for 4% of the time, Pallas kernels for 0%

profile of v13, /device:TPU:503, one launch (start us, length us, event | category | flops | bytes accessed | tf_op | source)
XLA Modules:
  0.0 38.2 jit_solution(13188382788335138109)
XLA Ops:
  0.6 0.0 copy-start.2
  0.6 0.9 %fusion.6 = (f32[4,16,256]{2,1,0:T(8,128)S(1)}, f32[4,16,256]{2,1,0:T(8,128)S(1)}) fusion(f32[16,16,256]{2,1,0:T(8,128)} %param.5), kind=kLoop, calls=%fused_computation.12 | loop fusion | bytes 262144 | tf_op jit(solution)/shard_map/slice | solution.py:256
  1.6 0.1 copy-done.2
  1.6 0.0 copy-start.4
  1.6 1.3 %fusion.9 = f32[128,16,16]{0,2,1:T(8,128)S(1)} fusion(f32[256,128,1]{1,0,2:T(8,128)} %constant.39, f32[16,16,256]{2,1,0:T(8,128)S(1)} %copy-done.2), kind=kOutput, calls=%fused_computation.15 | convolution fusion | flops 100663296 | bytes 524288 | tf_op jit(solution)/shard_map/xyz,zk->xyk/dot_general | solution.py:255
  3.0 0.0 copy-start
  3.0 0.0 copy-done.4
  3.0 0.3 fusion
  3.3 0.0 copy-start.1
  3.3 0.6 %copy-done.1 = f32[8,16,2,128]{3,1,2,0:T(8,128)} copy-done((f32[8,16,2,128]{3,1,2,0:T(8,128)}, f32[8,16,2,128]{3,1,2,0:T(8,128)S(1)}, u32[]{:S(2)}) %copy-start.1) | copy-done | bytes 131096
  3.9 0.0 copy-done
  4.0 0.0 copy-start.3
  4.0 2.9 %collective-permute-start = (f32[320,128]{1,0:T(8,128)S(1)}, f32[320,128]{1,0:T(8,128)S(1)}, u32[]{:S(2)}, u32[]{:S(2)}) collective-permute-start(f32[320,128]{1,0:T(8,128)S(1)} %pad_maximum_fusion), channel_id=1, source_target_pairs={{0,1},{1,2},{2,3},{3,4},{4,5},{5,6},{6,7},{7,8},{8,9},{9,10},{10,1... | collective-permute-start | bytes 491528 | tf_op jit(solution)/shard_map/ppermute | solution.py:83
  6.9 2.5 %collective-permute-start.1 = (f32[320,128]{1,0:T(8,128)S(1)}, f32[320,128]{1,0:T(8,128)S(1)}, u32[]{:S(2)}, u32[]{:S(2)}) collective-permute-start(f32[320,128]{1,0:T(8,128)S(1)} %pad_maximum_fusion.1), channel_id=1, source_target_pairs={{1,0},{2,1},{3,2},{4,3},{5,4},{6,5},{7,6},{8,7},{9,8},{10,9},{11,1... | collective-permute-start | bytes 491528 | tf_op jit(solution)/shard_map/ppermute | solution.py:84
  9.4 0.0 copy-done.3
  9.4 0.3 convolution_bitcast_fusion
  9.8 0.0 copy-start.9
  9.8 0.7 %copy.8 = f32[8,2,16,128]{3,2,1,0:T(8,128)} copy(f32[8,2,16,128]{3,2,0,1:T(8,128)S(1)} %convolution_bitcast_fusion) | data formatting | bytes 262144 | tf_op jit(solution)/shard_map/xyz,bzk->xbyk/transpose | solution.py:266
  10.4 0.2 copy-done.9
  10.7 0.6 %dynamic-slice_bitcast_fusion = (f32[48,128]{1,0:T(8,128)}, f32[48,128]{1,0:T(8,128)}) fusion(f32[3,48,128]{2,1,0:T(8,128)S(1)} %copy-done.9, s32[]{:T(128)S(6)} %select_n.20, s32[]{:T(128)S(6)} %select_n.18), kind=kLoop, calls=%fused_computation.9 | loop fusion | bytes 98312 | tf_op jit(solution)/shard_map/jit(dynamic_index_in_dim)/squeeze | solution.py:265
  11.3 0.0 collective-permute-done.below_ref
  11.3 0.0 copy-start.5
  11.3 5.6 %collective-permute-done.1.above_ref = f32[320,128]{1,0:T(8,128)S(1)} collective-permute-done((f32[320,128]{1,0:T(8,128)S(1)}, f32[320,128]{1,0:T(8,128)S(1)}, u32[]{:S(2)}, u32[]{:S(2)}) %collective-permute-start.1) | collective-permute-done | bytes 163872 | tf_op jit(solution)/shard_map/ppermute | solution.py:84
  16.8 0.0 copy-start.6
  16.8 0.0 copy-done.5
  16.8 0.7 %copy-done.6 = f32[320,128]{1,0:T(8,128)} copy-done((f32[320,128]{1,0:T(8,128)}, f32[320,128]{1,0:T(8,128)S(1)}, u32[]{:S(2)}) %copy-start.6) | copy-done | bytes 163864
  17.5 2.3 %shard_map.76 = (f32[512,128]{1,0:T(8,128)}, f32[128,128]{1,0:T(8,128)}, f32[224,128]{1,0:T(8,128)}, f32[224,128]{1,0:T(8,128)}) custom-call(f32[256,128]{1,0:T(8,128)} %bitcast.36, f32[256,128]{1,0:T(8,128)} %bitcast.37, f32[256,128]{1,0:T(8,128)} %bitcast.34, f32[320,128]{1,0:T(8,128)} %copy-done.5, f32[320,128]{1,0:T(8,128)} %copy-done.6, ...), custom_call_target="tpu_custom_call" | custom-call | tf_op jit(solution)/shard_map/pallas_call | solution.py:232
  19.8 7.9 %collective-permute-start.2 = (f32[224,128]{1,0:T(8,128)}, f32[224,128]{1,0:T(8,128)S(1)}, u32[]{:S(2)}, u32[]{:S(2)}) collective-permute-start(f32[224,128]{1,0:T(8,128)} %get-tuple-element.9), channel_id=1, source_target_pairs={{0,64},{64,128},{128,192},{192,256},{256,320},{320,384},{384,448},... | collective-permute-start | bytes 344072 | tf_op jit(solution)/shard_map/ppermute | solution.py:83
  27.6 1.9 %collective-permute-start.3 = (f32[224,128]{1,0:T(8,128)}, f32[224,128]{1,0:T(8,128)S(1)}, u32[]{:S(2)}, u32[]{:S(2)}) collective-permute-start(f32[224,128]{1,0:T(8,128)} %get-tuple-element.10), channel_id=1, source_target_pairs={{64,0},{128,64},{192,128},{256,192},{320,256},{384,320},{448,384},... | collective-permute-start | bytes 344072 | tf_op jit(solution)/shard_map/ppermute | solution.py:84
  29.6 0.2 collective-permute-done.2.below_ref
  29.7 0.0 copy-start.7
  29.7 5.4 %collective-permute-done.3.above_ref = f32[224,128]{1,0:T(8,128)S(1)} collective-permute-done((f32[224,128]{1,0:T(8,128)}, f32[224,128]{1,0:T(8,128)S(1)}, u32[]{:S(2)}, u32[]{:S(2)}) %collective-permute-start.3) | collective-permute-done | bytes 114720 | tf_op jit(solution)/shard_map/ppermute | solution.py:84
  35.2 0.0 copy-start.8
  35.2 0.0 copy-done.7
  35.2 0.6 %copy-done.8 = f32[224,128]{1,0:T(8,128)} copy-done((f32[224,128]{1,0:T(8,128)}, f32[224,128]{1,0:T(8,128)S(1)}, u32[]{:S(2)}) %copy-start.8) | copy-done | bytes 114712
  35.8 2.3 %shard_map.77 = (f32[4,4,64]{2,1,0:T(4,128)}, f32[7,4,4,64]{3,2,1,0:T(4,128)}, f32[7,8,8,128]{3,2,1,0:T(8,128)}) custom-call(f32[512,128]{1,0:T(8,128)} %get-tuple-element.7.one_ref, f32[128,128]{1,0:T(8,128)} %get-tuple-element.8.two_ref, f32[224,128]{1,0:T(8,128)} %copy-done.7, f32[224,128]{1,0:T(8,128)} %copy-done.8, f32[48,128]{1,0:T(8,128)} %get-tuple-element.17.maps_ref), custom_call_target="tpu_custom_call" | custom-call | tf_op jit(solution)/shard_map/pallas_call | solution.py:152
  (4 shorter events, 0.1 us)
Async XLA Ops:
  0.6 1.0 %copy-start.2 = (f32[16,16,256]{2,1,0:T(8,128)S(1)}, f32[16,16,256]{2,1,0:T(8,128)}, u32[]{:S(2)}) copy-start(f32[16,16,256]{2,1,0:T(8,128)} %param.5) | copy-start | bytes 786436
  1.6 1.3 %copy-start.4 = (f32[2,256,128,1]{2,1,0,3:T(8,128)S(1)}, f32[2,256,128,1]{2,1,0,3:T(8,128)}, u32[]{:S(2)}) copy-start(f32[2,256,128,1]{2,1,0,3:T(8,128)} %constant.37) | copy-start | bytes 786436
  3.0 1.0 %copy-start = (f32[128,16,16]{0,2,1:T(8,128)}, f32[128,16,16]{0,2,1:T(8,128)S(1)}, u32[]{:S(2)}) copy-start(f32[128,16,16]{0,2,1:T(8,128)S(1)} %fusion.9) | copy-start | bytes 393220
  3.3 0.7 %copy-start.1 = (f32[8,16,2,128]{3,1,2,0:T(8,128)}, f32[8,16,2,128]{3,1,2,0:T(8,128)S(1)}, u32[]{:S(2)}) copy-start(f32[8,16,2,128]{3,1,2,0:T(8,128)S(1)} %fusion) | copy-start | bytes 393220
  4.0 5.5 %copy-start.3 = (f32[2,256,128,1]{2,1,3,0:T(8,128)S(1)}, f32[2,256,128,1]{2,1,3,0:T(8,128)}, u32[]{:S(2)}) copy-start(f32[2,256,128,1]{2,1,3,0:T(8,128)} %constant.38) | copy-start | bytes 786436
  4.0 7.3 %collective-permute-start = (f32[320,128]{1,0:T(8,128)S(1)}, f32[320,128]{1,0:T(8,128)S(1)}, u32[]{:S(2)}, u32[]{:S(2)}) collective-permute-start(f32[320,128]{1,0:T(8,128)S(1)} %pad_maximum_fusion), channel_id=1, source_target_pairs={{0,1},{1,2},{2,3},{3,4},{4,5},{5,6},{6,7},{7,8},{8,9},{9,10},{10,1... | collective-permute-start | bytes 491528 | tf_op jit(solution)/shard_map/ppermute | solution.py:83
  6.9 10.0 %collective-permute-start.1 = (f32[320,128]{1,0:T(8,128)S(1)}, f32[320,128]{1,0:T(8,128)S(1)}, u32[]{:S(2)}, u32[]{:S(2)}) collective-permute-start(f32[320,128]{1,0:T(8,128)S(1)} %pad_maximum_fusion.1), channel_id=1, source_target_pairs={{1,0},{2,1},{3,2},{4,3},{5,4},{6,5},{7,6},{8,7},{9,8},{10,9},{11,1... | collective-permute-start | bytes 491528 | tf_op jit(solution)/shard_map/ppermute | solution.py:84
  9.8 0.9 %copy-start.9 = (f32[3,48,128]{2,1,0:T(8,128)S(1)}, f32[3,48,128]{2,1,0:T(8,128)}, u32[]{:S(2)}) copy-start(f32[3,48,128]{2,1,0:T(8,128)} %constant.35.clone) | copy-start | bytes 221188
  11.3 5.6 %copy-start.5 = (f32[320,128]{1,0:T(8,128)}, f32[320,128]{1,0:T(8,128)S(1)}, u32[]{:S(2)}) copy-start(f32[320,128]{1,0:T(8,128)S(1)} %collective-permute-done.below_ref) | copy-start | bytes 491524
  16.8 0.7 %copy-start.6 = (f32[320,128]{1,0:T(8,128)}, f32[320,128]{1,0:T(8,128)S(1)}, u32[]{:S(2)}) copy-start(f32[320,128]{1,0:T(8,128)S(1)} %collective-permute-done.1.above_ref) | copy-start | bytes 491524
  19.8 10.0 %collective-permute-start.2 = (f32[224,128]{1,0:T(8,128)}, f32[224,128]{1,0:T(8,128)S(1)}, u32[]{:S(2)}, u32[]{:S(2)}) collective-permute-start(f32[224,128]{1,0:T(8,128)} %get-tuple-element.9), channel_id=1, source_target_pairs={{0,64},{64,128},{128,192},{192,256},{256,320},{320,384},{384,448},... | collective-permute-start | bytes 344072 | tf_op jit(solution)/shard_map/ppermute | solution.py:83
  27.6 7.5 %collective-permute-start.3 = (f32[224,128]{1,0:T(8,128)}, f32[224,128]{1,0:T(8,128)S(1)}, u32[]{:S(2)}, u32[]{:S(2)}) collective-permute-start(f32[224,128]{1,0:T(8,128)} %get-tuple-element.10), channel_id=1, source_target_pairs={{64,0},{128,64},{192,128},{256,192},{320,256},{384,320},{448,384},... | collective-permute-start | bytes 344072 | tf_op jit(solution)/shard_map/ppermute | solution.py:84
  29.7 5.4 %copy-start.7 = (f32[224,128]{1,0:T(8,128)}, f32[224,128]{1,0:T(8,128)S(1)}, u32[]{:S(2)}) copy-start(f32[224,128]{1,0:T(8,128)S(1)} %collective-permute-done.2.below_ref) | copy-start | bytes 344068
  35.2 0.6 %copy-start.8 = (f32[224,128]{1,0:T(8,128)}, f32[224,128]{1,0:T(8,128)S(1)}, u32[]{:S(2)}) copy-start(f32[224,128]{1,0:T(8,128)S(1)} %collective-permute-done.3.above_ref) | copy-start | bytes 344068

commit v14 on v12

--- a/solution.py
+++ b/solution.py
@@ -161,8 +161,12 @@
     )(x_one.reshape(-1, lanes), x_two.reshape(-1, lanes), below, above, y_maps)
 
 
-def x_pass_kernel(own_ref, below_ref, above_ref, maps_ref, one_out, two_out, top_out, bottom_out, *,
-                  taps, places, bands):
+def x_pass_kernel(own_ref, below_hbm, above_hbm, maps_ref, one_out, two_out, top_out, bottom_out,
+                  below_ref, above_ref, sems, *, taps, places, bands):
+    fetch_below = pltpu.make_async_copy(below_hbm, below_ref, sems.at[0])
+    fetch_above = pltpu.make_async_copy(above_hbm, above_ref, sems.at[1])
+    fetch_below.start()
+    fetch_above.start()
     ny = two_out.shape[0] // len(taps[1])
     slab = 2 * ny
     stride = bands * ny
@@ -186,25 +190,37 @@
         j = i - lo2 - ny
         return above_ref[split + j * ny : split + (j + 1) * ny, :]
 
+    def weighted(row, used, piece, inside, acc):
+        for i in used:
+            if inside(i):
+                term = maps_ref[row, i] * piece(i)
+                acc = term if acc is None else acc + term
+        return acc
+
+    row1, row2 = places[0][0], places[1][0]
+    own_one = lambda i: lo1 <= i < lo1 + ny
+    own_two = lambda i: lo2 <= i < lo2 + ny
+    lanes = own_ref.shape[1]
+    for k, used in enumerate(taps[0]):
+        acc = weighted(row1 + k, used, one_slab, own_one, None)
+        one_out[k * slab : (k + 1) * slab, :] = acc if acc is not None else jnp.zeros((slab, lanes), jnp.float32)
+    for k, used in enumerate(taps[1]):
+        acc = weighted(row2 + k, used, two_slab, own_two, None)
+        two_out[k * ny : (k + 1) * ny, :] = acc if acc is not None else jnp.zeros((ny, lanes), jnp.float32)
+    fetch_below.wait()
+    fetch_above.wait()
+
     narrow, wide = lo1, lo2
-    row1 = places[0][0]
     for k, used in enumerate(taps[0]):
-        acc = None
-        for i in used:
-            term = maps_ref[row1 + k, i] * one_slab(i)
-            acc = term if acc is None else acc + term
+        acc = weighted(row1 + k, used, one_slab, lambda i: not own_one(i), one_out[k * slab : (k + 1) * slab, :])
         one_out[k * slab : (k + 1) * slab, :] = acc
         for b in range(2):
             at = (k * 2 + b) * narrow
             top_out[at : at + narrow, :] = acc[b * ny + ny - narrow : (b + 1) * ny, :]
             bottom_out[at : at + narrow, :] = acc[b * ny : b * ny + narrow, :]
     base = len(taps[0]) * 2 * narrow
-    row2 = places[1][0]
     for k, used in enumerate(taps[1]):
-        acc = None
-        for i in used:
-            term = maps_ref[row2 + k, i] * two_slab(i)
-            acc = term if acc is None else acc + term
+        acc = weighted(row2 + k, used, two_slab, lambda i: not own_two(i), two_out[k * ny : (k + 1) * ny, :])
         two_out[k * ny : (k + 1) * ny, :] = acc
         top_out[base + k * wide : base + (k + 1) * wide, :] = acc[ny - wide :, :]
         bottom_out[base + k * wide : base + (k + 1) * wide, :] = acc[:wide, :]
@@ -230,8 +246,13 @@
             jax.ShapeDtypeStruct((message, lanes), jnp.float32),
             jax.ShapeDtypeStruct((message, lanes), jnp.float32),
         ),
-        in_specs=[vmem, vmem, vmem, smem],
+        in_specs=[vmem, pl.BlockSpec(memory_space=pl.ANY), pl.BlockSpec(memory_space=pl.ANY), smem],
         out_specs=(vmem, vmem, vmem, vmem),
+        scratch_shapes=[
+            pltpu.VMEM(below.shape, jnp.float32),
+            pltpu.VMEM(above.shape, jnp.float32),
+            pltpu.SemaphoreType.DMA((2,)),
+        ],
     )(u.reshape(-1, lanes), below, above, x_maps)
 
 

time: 37.7 us -> 38.6 us (1.024)
  Pallas kernels: 4.62 us -> 5.44 us
    pallas_call x1, Pallas kernels: 2.28 us -> 3.09 us  [x_pass(): pl.pallas_call(functools.partial(x_pass_kernel, taps=taps, places=tuple(p...]
where the time goes in v14:
time: 38.6 us; the launch traced here: 38.2 us
  starting transfers between devices  15.1 us (39%)
  waiting for transfers between devices  11.5 us (30%)
  Pallas kernels  5.44 us (14%)
  local copies, waits for them, and re-layouts  3.8 us (10%)
  matrix products  1.62 us (4%)
  between operations  0.75 us (2%)
    ppermute x2, waiting for transfers between devices, exchange(): from_above = lax.ppermute(lower_half, axis, down)  11.2 us
    ppermute x2, starting transfers between devices, exchange(): from_below = lax.ppermute(upper_half, axis, up)  10.6 us
    ppermute x2, starting transfers between devices, exchange(): from_above = lax.ppermute(lower_half, axis, down)  4.46 us
    pallas_call x1, Pallas kernels, x_pass(): pl.pallas_call(functools.partial(x_pass_kernel, taps=taps, places=tuple(p...  3.09 us
    unnamed x12, local copies, waits for them, and re-layouts  2.37 us
    pallas_call x1, Pallas kernels, y_pass(): pl.pallas_call(functools.partial(y_pass_kernel, places=tuple(places)), ou...  2.35 us
    dot_general x1, matrix products, per_device(): jnp.einsum('xyz,bzk->xbyk', velocity, jnp.asarray(z_maps), precision=EXACT)  1.62 us
  transfers between devices with their start and end apart: 4, of which 4 were waited for; matrix products, arithmetic and copies ran while one was open for 4% of the time, Pallas kernels for 0%

profile of v14, /device:TPU:503, one launch (start us, length us, event | category | flops | bytes accessed | tf_op | source)
XLA Modules:
  0.0 38.2 jit_solution(5583047160408043271)
XLA Ops:
  0.6 0.0 copy-start
  0.6 0.9 %copy-done = f32[16,16,256]{2,1,0:T(8,128)S(1)} copy-done((f32[16,16,256]{2,1,0:T(8,128)S(1)}, f32[16,16,256]{2,1,0:T(8,128)}, u32[]{:S(2)}) %copy-start) | copy-done | bytes 262168
  1.6 1.6 %convolution_bitcast_fusion = f32[16,3,16,128]{3,2,0,1:T(8,128)S(1)} fusion(f32[3,256,128,1]{2,1,3,0:T(8,128)} %constant.34, f32[16,16,256]{2,1,0:T(8,128)S(1)} %copy-done), kind=kOutput, calls=%fused_computation | convolution fusion | flops 301989888 | bytes 1048576 | tf_op jit(solution)/shard_map/xyz,bzk->xbyk/dot_general | solution.py:265
  3.3 2.7 %collective-permute-start = (f32[320,128]{1,0:T(8,128)S(1)}, f32[320,128]{1,0:T(8,128)S(1)}, u32[]{:S(2)}, u32[]{:S(2)}) collective-permute-start(f32[320,128]{1,0:T(8,128)S(1)} %pad_maximum_fusion), channel_id=1, source_target_pairs={{0,1},{1,2},{2,3},{3,4},{4,5},{5,6},{6,7},{7,8},{8,9},{9,10},{10,1... | collective-permute-start | bytes 491528 | tf_op jit(solution)/shard_map/ppermute | solution.py:83
  6.1 2.5 %collective-permute-start.1 = (f32[320,128]{1,0:T(8,128)S(1)}, f32[320,128]{1,0:T(8,128)S(1)}, u32[]{:S(2)}, u32[]{:S(2)}) collective-permute-start(f32[320,128]{1,0:T(8,128)S(1)} %pad_maximum_fusion.1), channel_id=1, source_target_pairs={{1,0},{2,1},{3,2},{4,3},{5,4},{6,5},{7,6},{8,7},{9,8},{10,9},{11,1... | collective-permute-start | bytes 491528 | tf_op jit(solution)/shard_map/ppermute | solution.py:84
  8.6 0.0 copy-start.5
  8.6 0.8 %copy.6 = f32[16,3,16,128]{3,2,1,0:T(8,128)} copy(f32[16,3,16,128]{3,2,0,1:T(8,128)S(1)} %convolution_bitcast_fusion) | data formatting | bytes 786432 | tf_op jit(solution)/shard_map/xyz,bzk->xbyk/transpose | solution.py:265
  9.4 0.1 copy-done.5
  9.5 0.6 %dynamic-slice_bitcast_fusion = (f32[48,128]{1,0:T(8,128)}, f32[48,128]{1,0:T(8,128)}) fusion(f32[3,48,128]{2,1,0:T(8,128)S(1)} %copy-done.5, s32[]{:T(128)S(6)} %select_n.20, s32[]{:T(128)S(6)} %select_n.18), kind=kLoop, calls=%fused_computation.4 | loop fusion | bytes 98312 | tf_op jit(solution)/shard_map/jit(dynamic_index_in_dim)/squeeze | solution.py:278
  10.1 0.1 collective-permute-done.below_hbm
  10.3 0.0 copy-start.1
  10.3 5.8 %collective-permute-done.1.above_hbm = f32[320,128]{1,0:T(8,128)S(1)} collective-permute-done((f32[320,128]{1,0:T(8,128)S(1)}, f32[320,128]{1,0:T(8,128)S(1)}, u32[]{:S(2)}, u32[]{:S(2)}) %collective-permute-start.1) | collective-permute-done | bytes 163872 | tf_op jit(solution)/shard_map/ppermute | solution.py:84
  16.0 0.0 copy-start.2
  16.0 0.0 copy-done.1
  16.0 0.7 %copy-done.2 = f32[320,128]{1,0:T(8,128)} copy-done((f32[320,128]{1,0:T(8,128)}, f32[320,128]{1,0:T(8,128)S(1)}, u32[]{:S(2)}) %copy-start.2) | copy-done | bytes 163864
  16.7 3.1 %shard_map.58 = (f32[512,128]{1,0:T(8,128)}, f32[128,128]{1,0:T(8,128)}, f32[224,128]{1,0:T(8,128)}, f32[224,128]{1,0:T(8,128)}) custom-call(f32[768,128]{1,0:T(8,128)} %bitcast.18, f32[320,128]{1,0:T(8,128)} %copy-done.1, f32[320,128]{1,0:T(8,128)} %copy-done.2, f32[48,128]{1,0:T(8,128)} %get-tuple-element.16.maps_ref), custom_call_target="tpu_custom_call" | custom-call | tf_op jit(solution)/shard_map/pallas_call | solution.py:241
  19.8 7.9 %collective-permute-start.2 = (f32[224,128]{1,0:T(8,128)}, f32[224,128]{1,0:T(8,128)S(1)}, u32[]{:S(2)}, u32[]{:S(2)}) collective-permute-start(f32[224,128]{1,0:T(8,128)} %get-tuple-element.9), channel_id=1, source_target_pairs={{0,64},{64,128},{128,192},{192,256},{256,320},{320,384},{384,448},... | collective-permute-start | bytes 344072 | tf_op jit(solution)/shard_map/ppermute | solution.py:83
  27.7 1.9 %collective-permute-start.3 = (f32[224,128]{1,0:T(8,128)}, f32[224,128]{1,0:T(8,128)S(1)}, u32[]{:S(2)}, u32[]{:S(2)}) collective-permute-start(f32[224,128]{1,0:T(8,128)} %get-tuple-element.10), channel_id=1, source_target_pairs={{64,0},{128,64},{192,128},{256,192},{320,256},{384,320},{448,384},... | collective-permute-start | bytes 344072 | tf_op jit(solution)/shard_map/ppermute | solution.py:84
  29.6 0.2 collective-permute-done.2.below_ref
  29.8 0.0 copy-start.3
  29.8 5.4 %collective-permute-done.3.above_ref = f32[224,128]{1,0:T(8,128)S(1)} collective-permute-done((f32[224,128]{1,0:T(8,128)}, f32[224,128]{1,0:T(8,128)S(1)}, u32[]{:S(2)}, u32[]{:S(2)}) %collective-permute-start.3) | collective-permute-done | bytes 114720 | tf_op jit(solution)/shard_map/ppermute | solution.py:84
  35.2 0.0 copy-start.4
  35.2 0.0 copy-done.3
  35.2 0.6 %copy-done.4 = f32[224,128]{1,0:T(8,128)} copy-done((f32[224,128]{1,0:T(8,128)}, f32[224,128]{1,0:T(8,128)S(1)}, u32[]{:S(2)}) %copy-start.4) | copy-done | bytes 114712
  35.9 2.3 %shard_map.59 = (f32[4,4,64]{2,1,0:T(4,128)}, f32[7,4,4,64]{3,2,1,0:T(4,128)}, f32[7,8,8,128]{3,2,1,0:T(8,128)}) custom-call(f32[512,128]{1,0:T(8,128)} %get-tuple-element.7.one_ref, f32[128,128]{1,0:T(8,128)} %get-tuple-element.8.two_ref, f32[224,128]{1,0:T(8,128)} %copy-done.3, f32[224,128]{1,0:T(8,128)} %copy-done.4, f32[48,128]{1,0:T(8,128)} %get-tuple-element.15.maps_ref), custom_call_target="tpu_custom_call" | custom-call | tf_op jit(solution)/shard_map/pallas_call | solution.py:152
  (6 shorter events, 0.1 us)
Async XLA Ops:
  0.6 1.0 %copy-start = (f32[16,16,256]{2,1,0:T(8,128)S(1)}, f32[16,16,256]{2,1,0:T(8,128)}, u32[]{:S(2)}) copy-start(f32[16,16,256]{2,1,0:T(8,128)} %param.3) | copy-start | bytes 786436
  3.3 7.0 %collective-permute-start = (f32[320,128]{1,0:T(8,128)S(1)}, f32[320,128]{1,0:T(8,128)S(1)}, u32[]{:S(2)}, u32[]{:S(2)}) collective-permute-start(f32[320,128]{1,0:T(8,128)S(1)} %pad_maximum_fusion), channel_id=1, source_target_pairs={{0,1},{1,2},{2,3},{3,4},{4,5},{5,6},{6,7},{7,8},{8,9},{9,10},{10,1... | collective-permute-start | bytes 491528 | tf_op jit(solution)/shard_map/ppermute | solution.py:83
  6.1 10.0 %collective-permute-start.1 = (f32[320,128]{1,0:T(8,128)S(1)}, f32[320,128]{1,0:T(8,128)S(1)}, u32[]{:S(2)}, u32[]{:S(2)}) collective-permute-start(f32[320,128]{1,0:T(8,128)S(1)} %pad_maximum_fusion.1), channel_id=1, source_target_pairs={{1,0},{2,1},{3,2},{4,3},{5,4},{6,5},{7,6},{8,7},{9,8},{10,9},{11,1... | collective-permute-start | bytes 491528 | tf_op jit(solution)/shard_map/ppermute | solution.py:84
  8.6 0.9 %copy-start.5 = (f32[3,48,128]{2,1,0:T(8,128)S(1)}, f32[3,48,128]{2,1,0:T(8,128)}, u32[]{:S(2)}) copy-start(f32[3,48,128]{2,1,0:T(8,128)} %constant.32.clone) | copy-start | bytes 221188
  10.3 5.8 %copy-start.1 = (f32[320,128]{1,0:T(8,128)}, f32[320,128]{1,0:T(8,128)S(1)}, u32[]{:S(2)}) copy-start(f32[320,128]{1,0:T(8,128)S(1)} %collective-permute-done.below_hbm) | copy-start | bytes 491524
  16.0 0.7 %copy-start.2 = (f32[320,128]{1,0:T(8,128)}, f32[320,128]{1,0:T(8,128)S(1)}, u32[]{:S(2)}) copy-start(f32[320,128]{1,0:T(8,128)S(1)} %collective-permute-done.1.above_hbm) | copy-start | bytes 491524
  19.8 10.0 %collective-permute-start.2 = (f32[224,128]{1,0:T(8,128)}, f32[224,128]{1,0:T(8,128)S(1)}, u32[]{:S(2)}, u32[]{:S(2)}) collective-permute-start(f32[224,128]{1,0:T(8,128)} %get-tuple-element.9), channel_id=1, source_target_pairs={{0,64},{64,128},{128,192},{192,256},{256,320},{320,384},{384,448},... | collective-permute-start | bytes 344072 | tf_op jit(solution)/shard_map/ppermute | solution.py:83
  27.7 7.5 %collective-permute-start.3 = (f32[224,128]{1,0:T(8,128)}, f32[224,128]{1,0:T(8,128)S(1)}, u32[]{:S(2)}, u32[]{:S(2)}) collective-permute-start(f32[224,128]{1,0:T(8,128)} %get-tuple-element.10), channel_id=1, source_target_pairs={{64,0},{128,64},{192,128},{256,192},{320,256},{384,320},{448,384},... | collective-permute-start | bytes 344072 | tf_op jit(solution)/shard_map/ppermute | solution.py:84
  29.8 5.4 %copy-start.3 = (f32[224,128]{1,0:T(8,128)}, f32[224,128]{1,0:T(8,128)S(1)}, u32[]{:S(2)}) copy-start(f32[224,128]{1,0:T(8,128)S(1)} %collective-permute-done.2.below_ref) | copy-start | bytes 344068
  35.2 0.6 %copy-start.4 = (f32[224,128]{1,0:T(8,128)}, f32[224,128]{1,0:T(8,128)S(1)}, u32[]{:S(2)}) copy-start(f32[224,128]{1,0:T(8,128)S(1)} %collective-permute-done.3.above_ref) | copy-start | bytes 344068

commit v15 on v12

--- a/solution.py
+++ b/solution.py
@@ -54,8 +54,6 @@
     parts = [
         window_maps(block, (4, 4), 0),
         window_maps(block, (12, 12), 1),
-        window_maps(block, (8, 8), 0),
-        window_maps(block, (block, block), 1),
     ]
     height = sum(p[0].shape[0] for p in parts)
     width = -(-max(p[0].shape[1] for p in parts) // 128) * 128

time: 37.7 us -> 37.7 us (level)
  no operation moved by 1% of the time
where the time goes in v15:
time: 37.7 us; the launch traced here: 37.3 us
  starting transfers between devices  15.1 us (40%)
  waiting for transfers between devices  11.6 us (31%)
  Pallas kernels  4.56 us (12%)
  local copies, waits for them, and re-layouts  3.68 us (10%)
  matrix products  1.62 us (4%)
  between operations  0.74 us (2%)
    ppermute x2, waiting for transfers between devices, exchange(): from_above = lax.ppermute(lower_half, axis, down)  11.2 us
    ppermute x2, starting transfers between devices, exchange(): from_below = lax.ppermute(upper_half, axis, up)  10.6 us
    ppermute x2, starting transfers between devices, exchange(): from_above = lax.ppermute(lower_half, axis, down)  4.46 us
    pallas_call x1, Pallas kernels, y_pass(): pl.pallas_call(functools.partial(y_pass_kernel, places=tuple(places)), ou...  2.35 us
    unnamed x12, local copies, waits for them, and re-layouts  2.27 us
    pallas_call x1, Pallas kernels, x_pass(): pl.pallas_call(functools.partial(x_pass_kernel, taps=taps, places=tuple(p...  2.21 us
    dot_general x1, matrix products, per_device(): jnp.einsum('xyz,bzk->xbyk', velocity, jnp.asarray(z_maps), precision=EXACT)  1.62 us
    transpose x1, local copies, waits for them, and re-layouts, per_device(): jnp.einsum('xyz,bzk->xbyk', velocity, jnp.asarray(z_maps), precision=EXACT)  0.77 us
  transfers between devices with their start and end apart: 4, of which 4 were waited for; matrix products, arithmetic and copies ran while one was open for 4% of the time, Pallas kernels for 0%

profile of v15, /device:TPU:503, one launch (start us, length us, event | category | flops | bytes accessed | tf_op | source)
XLA Modules:
  0.0 37.3 jit_solution(2198723278250421917)
XLA Ops:
  0.6 0.0 copy-start
  0.6 0.9 %copy-done = f32[16,16,256]{2,1,0:T(8,128)S(1)} copy-done((f32[16,16,256]{2,1,0:T(8,128)S(1)}, f32[16,16,256]{2,1,0:T(8,128)}, u32[]{:S(2)}) %copy-start) | copy-done | bytes 262168
  1.6 1.6 %convolution_bitcast_fusion = f32[16,3,16,128]{3,2,0,1:T(8,128)S(1)} fusion(f32[3,256,128,1]{2,1,3,0:T(8,128)} %constant.34, f32[16,16,256]{2,1,0:T(8,128)S(1)} %copy-done), kind=kOutput, calls=%fused_computation | convolution fusion | flops 301989888 | bytes 1048576 | tf_op jit(solution)/shard_map/xyz,bzk->xbyk/dot_general | solution.py:242
  3.3 2.7 %collective-permute-start = (f32[320,128]{1,0:T(8,128)S(1)}, f32[320,128]{1,0:T(8,128)S(1)}, u32[]{:S(2)}, u32[]{:S(2)}) collective-permute-start(f32[320,128]{1,0:T(8,128)S(1)} %pad_maximum_fusion), channel_id=1, source_target_pairs={{0,1},{1,2},{2,3},{3,4},{4,5},{5,6},{6,7},{7,8},{8,9},{9,10},{10,1... | collective-permute-start | bytes 491528 | tf_op jit(solution)/shard_map/ppermute | solution.py:81
  6.1 2.5 %collective-permute-start.1 = (f32[320,128]{1,0:T(8,128)S(1)}, f32[320,128]{1,0:T(8,128)S(1)}, u32[]{:S(2)}, u32[]{:S(2)}) collective-permute-start(f32[320,128]{1,0:T(8,128)S(1)} %pad_maximum_fusion.1), channel_id=1, source_target_pairs={{1,0},{2,1},{3,2},{4,3},{5,4},{6,5},{7,6},{8,7},{9,8},{10,9},{11,1... | collective-permute-start | bytes 491528 | tf_op jit(solution)/shard_map/ppermute | solution.py:82
  8.6 0.0 copy-start.5
  8.6 0.8 %copy.6 = f32[16,3,16,128]{3,2,1,0:T(8,128)} copy(f32[16,3,16,128]{3,2,0,1:T(8,128)S(1)} %convolution_bitcast_fusion) | data formatting | bytes 786432 | tf_op jit(solution)/shard_map/xyz,bzk->xbyk/transpose | solution.py:242
  9.4 0.0 copy-done.5
  9.4 0.6 %dynamic-slice_bitcast_fusion = (f32[24,128]{1,0:T(8,128)}, f32[24,128]{1,0:T(8,128)}) fusion(f32[3,24,128]{2,1,0:T(8,128)S(1)} %copy-done.5, s32[]{:T(128)S(6)} %select_n.20, s32[]{:T(128)S(6)} %select_n.18), kind=kLoop, calls=%fused_computation.4 | loop fusion | bytes 49160 | tf_op jit(solution)/shard_map/jit(dynamic_index_in_dim)/squeeze | solution.py:255
  10.0 0.2 collective-permute-done.below_ref
  10.3 0.0 copy-start.1
  10.3 5.8 %collective-permute-done.1.above_ref = f32[320,128]{1,0:T(8,128)S(1)} collective-permute-done((f32[320,128]{1,0:T(8,128)S(1)}, f32[320,128]{1,0:T(8,128)S(1)}, u32[]{:S(2)}, u32[]{:S(2)}) %collective-permute-start.1) | collective-permute-done | bytes 163872 | tf_op jit(solution)/shard_map/ppermute | solution.py:82
  16.0 0.0 copy-start.2
  16.0 0.0 copy-done.1
  16.0 0.7 %copy-done.2 = f32[320,128]{1,0:T(8,128)} copy-done((f32[320,128]{1,0:T(8,128)}, f32[320,128]{1,0:T(8,128)S(1)}, u32[]{:S(2)}) %copy-start.2) | copy-done | bytes 163864
  16.7 2.2 %shard_map.58 = (f32[512,128]{1,0:T(8,128)}, f32[128,128]{1,0:T(8,128)}, f32[224,128]{1,0:T(8,128)}, f32[224,128]{1,0:T(8,128)}) custom-call(f32[768,128]{1,0:T(8,128)} %bitcast.18, f32[320,128]{1,0:T(8,128)} %copy-done.1, f32[320,128]{1,0:T(8,128)} %copy-done.2, f32[24,128]{1,0:T(8,128)} %get-tuple-element.16.maps_ref), custom_call_target="tpu_custom_call" | custom-call | tf_op jit(solution)/shard_map/pallas_call | solution.py:223
  18.9 7.9 %collective-permute-start.2 = (f32[224,128]{1,0:T(8,128)}, f32[224,128]{1,0:T(8,128)S(1)}, u32[]{:S(2)}, u32[]{:S(2)}) collective-permute-start(f32[224,128]{1,0:T(8,128)} %get-tuple-element.9), channel_id=1, source_target_pairs={{0,64},{64,128},{128,192},{192,256},{256,320},{320,384},{384,448},... | collective-permute-start | bytes 344072 | tf_op jit(solution)/shard_map/ppermute | solution.py:81
  26.8 1.9 %collective-permute-start.3 = (f32[224,128]{1,0:T(8,128)}, f32[224,128]{1,0:T(8,128)S(1)}, u32[]{:S(2)}, u32[]{:S(2)}) collective-permute-start(f32[224,128]{1,0:T(8,128)} %get-tuple-element.10), channel_id=1, source_target_pairs={{64,0},{128,64},{192,128},{256,192},{320,256},{384,320},{448,384},... | collective-permute-start | bytes 344072 | tf_op jit(solution)/shard_map/ppermute | solution.py:82
  28.7 0.2 collective-permute-done.2.below_ref
  28.9 0.0 copy-start.3
  28.9 5.4 %collective-permute-done.3.above_ref = f32[224,128]{1,0:T(8,128)S(1)} collective-permute-done((f32[224,128]{1,0:T(8,128)}, f32[224,128]{1,0:T(8,128)S(1)}, u32[]{:S(2)}, u32[]{:S(2)}) %collective-permute-start.3) | collective-permute-done | bytes 114720 | tf_op jit(solution)/shard_map/ppermute | solution.py:82
  34.3 0.0 copy-start.4
  34.3 0.0 copy-done.3
  34.3 0.6 %copy-done.4 = f32[224,128]{1,0:T(8,128)} copy-done((f32[224,128]{1,0:T(8,128)}, f32[224,128]{1,0:T(8,128)S(1)}, u32[]{:S(2)}) %copy-start.4) | copy-done | bytes 114712
  35.0 2.3 %shard_map.59 = (f32[4,4,64]{2,1,0:T(4,128)}, f32[7,4,4,64]{3,2,1,0:T(4,128)}, f32[7,8,8,128]{3,2,1,0:T(8,128)}) custom-call(f32[512,128]{1,0:T(8,128)} %get-tuple-element.7.one_ref, f32[128,128]{1,0:T(8,128)} %get-tuple-element.8.two_ref, f32[224,128]{1,0:T(8,128)} %copy-done.3, f32[224,128]{1,0:T(8,128)} %copy-done.4, f32[24,128]{1,0:T(8,128)} %get-tuple-element.15.maps_ref), custom_call_target="tpu_custom_call" | custom-call | tf_op jit(solution)/shard_map/pallas_call | solution.py:150
  (6 shorter events, 0.1 us)
Async XLA Ops:
  0.6 1.0 %copy-start = (f32[16,16,256]{2,1,0:T(8,128)S(1)}, f32[16,16,256]{2,1,0:T(8,128)}, u32[]{:S(2)}) copy-start(f32[16,16,256]{2,1,0:T(8,128)} %param.3) | copy-start | bytes 786436
  3.3 7.0 %collective-permute-start = (f32[320,128]{1,0:T(8,128)S(1)}, f32[320,128]{1,0:T(8,128)S(1)}, u32[]{:S(2)}, u32[]{:S(2)}) collective-permute-start(f32[320,128]{1,0:T(8,128)S(1)} %pad_maximum_fusion), channel_id=1, source_target_pairs={{0,1},{1,2},{2,3},{3,4},{4,5},{5,6},{6,7},{7,8},{8,9},{9,10},{10,1... | collective-permute-start | bytes 491528 | tf_op jit(solution)/shard_map/ppermute | solution.py:81
  6.1 10.0 %collective-permute-start.1 = (f32[320,128]{1,0:T(8,128)S(1)}, f32[320,128]{1,0:T(8,128)S(1)}, u32[]{:S(2)}, u32[]{:S(2)}) collective-permute-start(f32[320,128]{1,0:T(8,128)S(1)} %pad_maximum_fusion.1), channel_id=1, source_target_pairs={{1,0},{2,1},{3,2},{4,3},{5,4},{6,5},{7,6},{8,7},{9,8},{10,9},{11,1... | collective-permute-start | bytes 491528 | tf_op jit(solution)/shard_map/ppermute | solution.py:82
  8.6 0.8 %copy-start.5 = (f32[3,24,128]{2,1,0:T(8,128)S(1)}, f32[3,24,128]{2,1,0:T(8,128)}, u32[]{:S(2)}) copy-start(f32[3,24,128]{2,1,0:T(8,128)} %constant.32.clone) | copy-start | bytes 110596
  10.3 5.8 %copy-start.1 = (f32[320,128]{1,0:T(8,128)}, f32[320,128]{1,0:T(8,128)S(1)}, u32[]{:S(2)}) copy-start(f32[320,128]{1,0:T(8,128)S(1)} %collective-permute-done.below_ref) | copy-start | bytes 491524
  16.0 0.7 %copy-start.2 = (f32[320,128]{1,0:T(8,128)}, f32[320,128]{1,0:T(8,128)S(1)}, u32[]{:S(2)}) copy-start(f32[320,128]{1,0:T(8,128)S(1)} %collective-permute-done.1.above_ref) | copy-start | bytes 491524
  18.9 10.0 %collective-permute-start.2 = (f32[224,128]{1,0:T(8,128)}, f32[224,128]{1,0:T(8,128)S(1)}, u32[]{:S(2)}, u32[]{:S(2)}) collective-permute-start(f32[224,128]{1,0:T(8,128)} %get-tuple-element.9), channel_id=1, source_target_pairs={{0,64},{64,128},{128,192},{192,256},{256,320},{320,384},{384,448},... | collective-permute-start | bytes 344072 | tf_op jit(solution)/shard_map/ppermute | solution.py:81
  26.8 7.5 %collective-permute-start.3 = (f32[224,128]{1,0:T(8,128)}, f32[224,128]{1,0:T(8,128)S(1)}, u32[]{:S(2)}, u32[]{:S(2)}) collective-permute-start(f32[224,128]{1,0:T(8,128)} %get-tuple-element.10), channel_id=1, source_target_pairs={{64,0},{128,64},{192,128},{256,192},{320,256},{384,320},{448,384},... | collective-permute-start | bytes 344072 | tf_op jit(solution)/shard_map/ppermute | solution.py:82
  28.9 5.4 %copy-start.3 = (f32[224,128]{1,0:T(8,128)}, f32[224,128]{1,0:T(8,128)S(1)}, u32[]{:S(2)}) copy-start(f32[224,128]{1,0:T(8,128)S(1)} %collective-permute-done.2.below_ref) | copy-start | bytes 344068
  34.3 0.6 %copy-start.4 = (f32[224,128]{1,0:T(8,128)}, f32[224,128]{1,0:T(8,128)S(1)}, u32[]{:S(2)}) copy-start(f32[224,128]{1,0:T(8,128)S(1)} %collective-permute-done.3.above_ref) | copy-start | bytes 344068
